TPU v7x, 32 devices: a whole 2x2x4 slice. The times are simulated.
32 devices in a mesh: gx: 4 (over y, x), gz: 8 (over z, core).
Axes of the slice: x: 2, y: 2, z: 4, core: 2. Of those that a mesh axis runs over, the one named last changes fastest.
Arguments:
- theta: float32 [152, 256, 512], P(None, 'gz', 'gx'), may hold values from -5 to 5
- section_store: float32 [152, 256, 512], P(None, 'gz', 'gx'), may hold values from -3 to 3
- stream_speed: bfloat16 [152, 256, 512], P(None, 'gz', 'gx'), may hold values from 0.19921875 to 1.1953125
- span_speed: bfloat16 [152, 256, 512], P(None, 'gz', 'gx'), may hold values from -2.5 to 2.5
- conductivity: float32 [2, 152], replicated, may hold values from 0.05 to 0.5
- wall_layers: int32 [256], P('gz'), may hold values from 32 to 47
- contact: int32 [512], P('gx'), may hold values 0 or 1
- spanwise_number: float32 [32], replicated, may hold values from 3072 to 6144
- block_inverse: float32 [32, 31, 31], replicated, may hold values from 0 to 1, as said below
Outputs:
- theta_new: float32 [152, 256, 512], P(None, 'gz', 'gx')
- section_new: float32 [152, 256, 512], P(None, 'gz', 'gx')
Inputs may be any that keep to these rules, and one draw needn't show every extreme that they name: block_inverse[l] is the symmetric inverse of the 31-square tridiagonal matrix with 1 + 2 spanwise_number[l] on its diagonal and -spanwise_number[l] beside it.
All inputs are finite; a program needn't handle non-finite values. No bound on the sum of `contact` on one device may be relied on, other than what follows from the above.
Results may differ from a plain program's by a relative error of at most 0.0003.
Values sent between devices are 32-bit elements; how exact they have to be, the bound alone decides.
No kernel may reach another device: no remote copies, remote signals or barrier semaphores. Data moves between devices by JAX's collectives and lax.ppermute only.
A program may use at most 64 MiB of HBM per device.

v0:
```python
import jax
import jax.numpy as jnp
from jax import lax
from jax.sharding import PartitionSpec as P

keep_factor = -5.0 / 9.0
section_weight = 15.0 / 16.0
stream_courant = 0.4
span_courant = 0.4
damping = 1.0 / 256.0
slope_weights = (-1.0, 9.0, -45.0, 0.0, 45.0, -9.0, 1.0)
smooth_weights = (1.0, -8.0, 28.0, -56.0, 70.0, -56.0, 28.0, -8.0, 1.0)


def padded_2(shard, sides, width, wrap):
    for axis, dim in sides:
        count, length = (lax.axis_size(axis), shard.shape[dim])
        up = [(i, (i + 1) % count) for i in range(count if wrap else count - 1)]
        down = [(j, i) for i, j in up]
        last = lax.slice_in_dim(shard, length - width, length, axis=dim)
        first = lax.slice_in_dim(shard, 0, width, axis=dim)
        before = lax.ppermute(last, axis, up)
        after = lax.ppermute(first, axis, down)
        shard = jnp.concatenate([before, shard, after], axis=dim)
    return shard


def from_behind(shard, axis, by):
    count = lax.axis_size(axis)
    return lax.ppermute(shard, axis, [(i, (i + by) % count) for i in range(count)])


def stencil(padded, along, length, weights, first_offset):
    running = jnp.zeros_like(lax.slice_in_dim(padded, 0, length, axis=along))
    for offset, weight in enumerate(weights):
        if weight != 0.0:
            begin = first_offset + offset
            running = running + weight * lax.slice_in_dim(padded, begin, begin + length, axis=along)
    return running


def horizontal_term(span_pad, stream_pad, stream_speed, span_speed):
    span_length = stream_pad.shape[1]
    stream_length = span_pad.shape[2]
    span_slope = stencil(span_pad, 1, span_length, slope_weights, 1) / 60.0
    stream_slope = stencil(stream_pad, 2, stream_length, slope_weights, 1) / 60.0
    smoothing = stencil(span_pad, 1, span_length, smooth_weights, 0) + stencil(
        stream_pad, 2, stream_length, smooth_weights, 0
    )
    return (
        -stream_courant * stream_speed.astype(jnp.float32) * stream_slope
        - span_courant * span_speed.astype(jnp.float32) * span_slope
        - damping * smoothing
    )


def normal_term(theta, conductivity, wall_layers, contact):
    layer_index = jnp.arange(theta.shape[0], dtype=jnp.int32)[:, None]
    solid_cell = layer_index < wall_layers[None, :]
    cell_cond = jnp.where(solid_cell, conductivity[0][:, None], conductivity[1][:, None])
    face_cond = 2.0 * cell_cond[:-1] * cell_cond[1:] / (cell_cond[:-1] + cell_cond[1:])
    at_wall = layer_index[:-1] == wall_layers[None, :] - 1
    contact_float = contact.astype(jnp.float32)
    face_full = jnp.where(
        at_wall[:, :, None],
        face_cond[:, :, None] * contact_float[None, None, :],
        face_cond[:, :, None],
    )
    face_flux = face_full * (theta[1:] - theta[:-1])
    border = jnp.zeros((1,) + theta.shape[1:], jnp.float32)
    return jnp.concatenate([face_flux, border], 0) - jnp.concatenate([border, face_flux], 0)


def interior_solve(inverse, interior_cells):
    return jnp.einsum("lij,lkjx->lkix", inverse, interior_cells, precision=lax.Precision.HIGHEST)


def cycle_coefficients(number, inverse):
    square = number * number
    diagonal = 1.0 + 2.0 * number - square * (inverse[:, 0, 0] + inverse[:, -1, -1])
    return (diagonal, square * inverse[:, 0, -1])


def cyclic_solve(right_side, diagonal, beside):
    layers = right_side.shape[0]
    group_count = right_side.shape[1]
    unit_row = jnp.ones((layers, group_count), jnp.float32)
    main_diag = diagonal[:, None] * unit_row
    main_diag = main_diag.at[:, 0].add(diagonal)
    main_diag = main_diag.at[:, -1].add(beside * beside / diagonal)
    lower = (-beside[:, None] * unit_row).at[:, 0].set(0.0)
    upper = (-beside[:, None] * unit_row).at[:, -1].set(0.0)
    first_solve = lax.linalg.tridiagonal_solve(lower, main_diag, upper, right_side)
    corner = jnp.zeros((layers, group_count, 1), jnp.float32)
    corner = corner.at[:, 0, 0].set(-diagonal).at[:, -1, 0].set(-beside)
    second = lax.linalg.tridiagonal_solve(lower, main_diag, upper, corner)
    corner_ratio = (beside / diagonal)[:, None]
    top_term = first_solve[:, 0, :] + corner_ratio * first_solve[:, -1, :]
    bottom = 1.0 + second[:, 0, :] + corner_ratio * second[:, -1, :]
    return first_solve - (top_term / bottom)[:, None, :] * second


def complete_blocks(interior, head_values, following, number, inverse):
    number_scale = number[:, None, None, None]
    interior = interior + number_scale * (
        inverse[:, None, :, 0, None] * head_values[:, :, None, :]
        + inverse[:, None, :, -1, None] * following[:, :, None, :]
    )
    return jnp.concatenate([head_values[:, :, None, :], interior], 2)


def local(
    theta,
    section_store,
    stream_speed,
    span_speed,
    conductivity,
    wall_layers,
    contact,
    spanwise_number,
    block_inverse,
):
    solid_count = block_inverse.shape[0]
    block_width = block_inverse.shape[1] + 1
    stream_cells = theta.shape[2]
    fluid_theta = theta[solid_count:]
    fluid_stream = stream_speed[solid_count:]
    fluid_span = span_speed[solid_count:]
    span_pad = padded_2(fluid_theta, (("gz", 1),), 4, True)
    stream_pad = padded_2(fluid_theta, (("gx", 2),), 4, False)
    across = horizontal_term(span_pad, stream_pad, fluid_stream, fluid_span)
    layer_index = jnp.arange(solid_count, theta.shape[0], dtype=jnp.int32)[:, None, None]
    fluid_mask = layer_index >= wall_layers[None, :, None]
    across = jnp.where(fluid_mask, across, 0.0)
    section_rate = normal_term(theta, conductivity, wall_layers, contact) + jnp.concatenate(
        [jnp.zeros_like(theta[:solid_count]), across], 0
    )
    section_new = keep_factor * section_store + section_rate
    advanced = theta + section_weight * section_new
    substrate_now = advanced[:solid_count]
    group_count = lax.axis_size("gz")
    blocks = substrate_now[:, None]
    interior = interior_solve(block_inverse, blocks[:, :, 1:, :])
    number_scale = spanwise_number[:, None, None]
    from_left = from_behind(interior[:, :, -1, :], "gz", 1)
    target = blocks[:, :, 0, :] + number_scale * from_left + number_scale * interior[:, :, 0, :]
    cycle_targets = lax.all_gather(target, "gz", axis=1, tiled=True)
    diagonal, beside = cycle_coefficients(spanwise_number, block_inverse)
    all_heads = cyclic_solve(cycle_targets, diagonal, beside)
    position = lax.axis_index("gz")
    head_values = lax.dynamic_slice_in_dim(all_heads, position, 1, 1)
    following = lax.dynamic_slice_in_dim(all_heads, (position + 1) % group_count, 1, 1)
    solved = complete_blocks(interior, head_values, following, spanwise_number, block_inverse)
    substrate = solved.reshape(solid_count, block_width, stream_cells)
    theta_new = jnp.concatenate([substrate, advanced[solid_count:]], 0)
    return (theta_new, section_new)


def solution(mesh):
    return jax.shard_map(
        local,
        mesh=mesh,
        in_specs=(
            P(None, "gz", "gx"),
            P(None, "gz", "gx"),
            P(None, "gz", "gx"),
            P(None, "gz", "gx"),
            P(),
            P("gz"),
            P("gx"),
            P(),
            P(),
        ),
        out_specs=(P(None, "gz", "gx"), P(None, "gz", "gx")),
        check_vma=False,
    )
```

profile of v0, /device:TPU:0, one launch (start us, length us, event | category | flops | bytes accessed | tf_op | source)
XLA Modules:
  0.0 88.1 jit_solution(16138623948509846424)
XLA Ops:
  0.6 4.7 %fusion.94 = (f32[120,32,4]{2,1,0:T(8,128)}, f32[120,32,4]{2,1,0:T(8,128)}) fusion(f32[152,32,128]{2,1,0:T(8,128)} %param.21), kind=kLoop, calls=%fused_computation.228 | loop fusion | bytes 245760 | tf_op jit(solution)/shard_map/slice | solution.py:20
  5.3 2.7 %copy.33 = f32[120,32,4]{0,1,2:T(8,128)S(1)} copy(f32[120,32,4]{2,1,0:T(8,128)} %get-tuple-element.120) | data formatting | bytes 122880
  8.0 1.4 %collective-permute-start.1 = (f32[120,32,4]{0,1,2:T(8,128)S(1)}, f32[120,32,4]{0,1,2:T(8,128)S(1)}, u32[]{:S(2)}, u32[]{:S(2)}) collective-permute-start(f32[120,32,4]{0,1,2:T(8,128)S(1)} %copy.33), channel_id=1, source_target_pairs={{8,0},{16,8},{24,16},{9,1},{17,9},{25,17},{10,2},{18,10},{26,18},{... | collective-permute-start | bytes 184328 | tf_op jit(solution)/shard_map/ppermute | solution.py:23
  9.5 2.6 %copy.32 = f32[120,32,4]{0,1,2:T(8,128)S(1)} copy(f32[120,32,4]{2,1,0:T(8,128)} %get-tuple-element.119) | data formatting | bytes 122880
  12.0 6.2 %collective-permute-start = (f32[120,32,4]{0,1,2:T(8,128)S(1)}, f32[120,32,4]{0,1,2:T(8,128)}, u32[]{:S(2)}, u32[]{:S(2)}) collective-permute-start(f32[120,32,4]{0,1,2:T(8,128)S(1)} %copy.32), channel_id=1, source_target_pairs={{0,8},{8,16},{16,24},{1,9},{9,17},{17,25},{2,10},{10,18},{18,26},{... | collective-permute-start | bytes 184328 | tf_op jit(solution)/shard_map/ppermute | solution.py:22
  18.3 0.9 fusion.93
  19.2 3.0 %collective-permute-start.3 = (f32[120,4,128]{2,1,0:T(4,128)}, f32[120,4,128]{2,1,0:T(4,128)S(1)}, u32[]{:S(2)}, u32[]{:S(2)}) collective-permute-start(f32[120,4,128]{2,1,0:T(4,128)} %get-tuple-element.118), channel_id=1, source_target_pairs={{1,0},{2,1},{3,2},{4,3},{5,4},{6,5},{7,6},{0,7},{9,8},{10,9},{11,1... | collective-permute-start | bytes 737288 | tf_op jit(solution)/shard_map/ppermute | solution.py:23
  23.5 1.1 %fusion.95 = (f32[32,31,1]{2,0,1:T(8,128)}, f32[32,31,1]{2,0,1:T(8,128)}) fusion(f32[32,31,31]{2,0,1:T(8,128)S(1)} %copy-done.3), kind=kLoop, calls=%fused_computation.229 | loop fusion | bytes 15872 | tf_op jit(solution)/shard_map/slice | solution.py:106
  26.7 1.1 %fusion.58 = f32[32,1]{0,1:T(1,128)} fusion(f32[32]{0:T(128)S(1)} %get-tuple-element.108, pred[]{:T(512)} %compare_reduce_fusion), kind=kLoop, calls=%fused_computation.151 | loop fusion | flops 64 | bytes 257 | tf_op jit(solution)/shard_map/reshape.1534
  30.8 1.4 %fusion.67 = (f32[32,1]{0,1:T(1,128)S(1)}, f32[32,1]{0,1:T(1,128)S(1)}, f32[32,1]{0,1:T(1,128)S(1)}, f32[32,1]{0,1:T(1,128)S(1)}, f32[32,1]{0,1:T(1,128)S(1)}, /...) fusion(f32[7,32,1]{1,2,0:T(1,128)} %slice_bitcast_fusion.8, ...), kind=kLoop, calls=%fused_computation.164 | loop fusion | flops 992 | bytes 4480 | tf_op jit(solution)/shard_map/vmap()/eval_jaxpr/div | solution.py:96
  32.2 1.3 %fusion.80 = (f32[32,1,1]{0,2,1:T(1,128)}, f32[32,1]{0,1:T(1,128)S(1)}, f32[32,1]{0,1:T(1,128)S(1)}, f32[32,1]{0,1:T(1,128)S(1)}, f32[32,1]{0,1:T(1,128)S(1)}, /...) fusion(f32[32,1]{0,1:T(1,128)S(1)} %get-tuple-element.94, ...), kind=kLoop, calls=%fused_computation.224 | loop fusion | flops 832 | bytes 3584 | tf_op jit(solution)/shard_map/vmap()/broadcast_in_dim | solution.py:96
  34.4 3.5 %subtract_multiply_fusion = f32[151,32,128]{2,1,0:T(8,128)} fusion(f32[152,32,128]{2,1,0:T(8,128)S(1)} %copy-done, f32[128]{0:T(128)} %convert_element_type.9, f32[151,32]{1,0:T(8,128)S(1)} %add_divide_fusion, pred[151,32]{1,0:T(8,128)(4,1)S(1)} %broadcast_compare_fusion), kind=kLoop, calls=%fused_computation.27 | loop fusion | flops 2473984 | bytes 7446624 | tf_op jit(solution)/shard_map/mul | solution.py:69
  39.1 2.7 %copy.24 = f32[120,32,4]{2,1,0:T(8,128)} copy(f32[120,32,4]{0,1,2:T(8,128)S(1)} %collective-permute-done.1) | data formatting | bytes 122880 | tf_op jit(solution)/shard_map/ppermute | solution.py:23
  41.8 3.6 %copy.22 = f32[120,32,4]{2,1,0:T(8,128)} copy(f32[120,32,4]{0,1,2:T(8,128)} %collective-permute-done) | data formatting | bytes 122880 | tf_op jit(solution)/shard_map/ppermute | solution.py:22
  45.5 14.6 %fusion.16 = f32[120,32,128]{2,1,0:T(8,128)S(1)} fusion(f32[120,32,4]{2,1,0:T(8,128)} %copy.24, f32[120,32,128]{2,1,0:T(8,128)S(1)} %slice-done, f32[120,32,4]{2,1,0:T(8,128)} %copy.22, f32[120,4,128]{2,1,0:T(4,128)S(1)} %collective-permute-done.3, f32[120,4,128]{2,1,0:T(4,128)} %collective-permute-done.2, bf16[152,32,128]{2,1,0:T(8,128)(2,1)} %param.24, ...), kind=kLoop, calls=%fused_computation.45 | loop fusion | flops 38338560 | bytes 6516480 | tf_op jit(solution)/shard_map/jit(_where)/select_n | solution.py:134
  60.1 2.6 %multiply_add_fusion = (f32[152,32,128]{2,1,0:T(8,128)S(1)}, f32[152,32,128]{2,1,0:T(8,128)}) fusion(f32[152,32,128]{2,1,0:T(8,128)S(1)} %copy-done.1, f32[120,32,128]{2,1,0:T(8,128)S(1)} %fusion.16, f32[151,32,128]{2,1,0:T(8,128)S(1)} %copy-done.2, f32[152,32,128]{2,1,0:T(8,128)S(1)} %copy-done.4), kind=kLoop, calls=%fused_computation.25 | loop fusion | flops 3735552 | bytes 14401536 | tf_op jit(solution)/shard_map/add | solution.py:139
  62.8 0.9 %fusion.32 = f32[32,128,31]{1,2,0:T(8,128)S(1)} fusion(f32[32,1,32,128]{3,2,0,1:T(8,128)S(1)} %slice_bitcast_fusion.2, f32[32,31,31]{2,0,1:T(8,128)S(1)} %copy-done.3), kind=kOutput, calls=%fused_computation.65 | convolution fusion | flops 47235072 | bytes 1155200 | tf_op jit(solution)/shard_map/lij,lkjx->lkix/dot_general | solution.py:75
  65.3 1.3 %copy.37 = f32[32,31,1]{0,1,2:T(8,128)S(1)} copy(f32[32,31,1]{2,0,1:T(8,128)} %get-tuple-element.122) | data formatting | bytes 7936 | tf_op jit(solution)/shard_map/mul | solution.py:107
  66.5 1.3 %copy.36 = f32[32,31,1]{0,1,2:T(8,128)S(1)} copy(f32[32,31,1]{2,0,1:T(8,128)} %get-tuple-element.121) | data formatting | bytes 7936 | tf_op jit(solution)/shard_map/mul | solution.py:106
  68.2 0.9 %slice.515 = f32[32,1,1,128]{3,2,0,1:T(1,128)S(1)} slice(f32[32,1,32,128]{3,2,0,1:T(8,128)} %copy-done.5), slice={[0:32], [0:1], [0:1], [0:128]} | slice | bytes 32768 | tf_op jit(solution)/shard_map/slice | solution.py:146
  69.1 0.8 collective-permute-done.4
  69.9 0.8 fusion.39
  70.7 13.9 %all_gather.3 = f32[32,8,128]{2,0,1:T(8,128)S(1)} all-gather(f32[32,1,128]{2,0,1:T(8,128)S(1)} %fusion.39), channel_id=1, replica_groups=mesh['gx'=4,'gz'=8] {'gz'}, dimensions={1}, use_global_device_ids=true | all-gather | bytes 147456 | tf_op jit(solution)/shard_map/all_gather | solution.py:147
  86.4 1.7 %pad_maximum_fusion = f32[152,32,128]{2,1,0:T(8,128)} fusion(f32[120,32,128]{2,1,0:T(8,128)S(1)} %slice.539, f32[32,32,128]{2,1,0:T(8,128)S(1)} %copy.31), kind=kLoop, calls=%fused_computation.24 | loop fusion | flops 622592 | bytes 4980736 | tf_op jit(solution)/shard_map/concatenate | solution.py:155
  (151 shorter events, 11.6 us)
Async XLA Ops:
  8.0 31.0 %collective-permute-start.1 = (f32[120,32,4]{0,1,2:T(8,128)S(1)}, f32[120,32,4]{0,1,2:T(8,128)S(1)}, u32[]{:S(2)}, u32[]{:S(2)}) collective-permute-start(f32[120,32,4]{0,1,2:T(8,128)S(1)} %copy.33), channel_id=1, source_target_pairs={{8,0},{16,8},{24,16},{9,1},{17,9},{25,17},{10,2},{18,10},{26,18},{... | collective-permute-start | bytes 184328 | tf_op jit(solution)/shard_map/ppermute | solution.py:23
  12.0 29.8 %collective-permute-start = (f32[120,32,4]{0,1,2:T(8,128)S(1)}, f32[120,32,4]{0,1,2:T(8,128)}, u32[]{:S(2)}, u32[]{:S(2)}) collective-permute-start(f32[120,32,4]{0,1,2:T(8,128)S(1)} %copy.32), channel_id=1, source_target_pairs={{0,8},{8,16},{16,24},{1,9},{9,17},{17,25},{2,10},{10,18},{18,26},{... | collective-permute-start | bytes 184328 | tf_op jit(solution)/shard_map/ppermute | solution.py:22
  19.2 26.3 %collective-permute-start.3 = (f32[120,4,128]{2,1,0:T(4,128)}, f32[120,4,128]{2,1,0:T(4,128)S(1)}, u32[]{:S(2)}, u32[]{:S(2)}) collective-permute-start(f32[120,4,128]{2,1,0:T(4,128)} %get-tuple-element.118), channel_id=1, source_target_pairs={{1,0},{2,1},{3,2},{4,3},{5,4},{6,5},{7,6},{0,7},{9,8},{10,9},{11,1... | collective-permute-start | bytes 737288 | tf_op jit(solution)/shard_map/ppermute | solution.py:23
  22.2 23.3 %collective-permute-start.2 = (f32[120,4,128]{2,1,0:T(4,128)}, f32[120,4,128]{2,1,0:T(4,128)}, u32[]{:S(2)}, u32[]{:S(2)}) collective-permute-start(f32[120,4,128]{2,1,0:T(4,128)} %get-tuple-element.117), channel_id=1, source_target_pairs={{0,1},{1,2},{2,3},{3,4},{4,5},{5,6},{6,7},{7,0},{8,9},{9,10},{10,1... | collective-permute-start | bytes 737288 | tf_op jit(solution)/shard_map/ppermute | solution.py:22
  64.7 5.3 %collective-permute-start.4 = (f32[32,1,128]{2,0,1:T(8,128)}, f32[32,1,128]{2,0,1:T(8,128)}, u32[]{:S(2)}, u32[]{:S(2)}) collective-permute-start(f32[32,1,128]{2,0,1:T(8,128)} %slice_bitcast_fusion.5), channel_id=1, source_target_pairs={{0,1},{1,2},{2,3},{3,4},{4,5},{5,6},{6,7},{7,0},{8,9},{9,10},{10,1... | collective-permute-start | bytes 49160 | tf_op jit(solution)/shard_map/ppermute | solution.py:30
  67.8 16.9 %copy-start.7 = (f32[32]{0:T(128)S(1)}, f32[32]{0:T(128)}, u32[]{:S(2)}) copy-start(f32[32]{0:T(128)} %copy-done.6) | copy-start | bytes 388
  67.9 16.9 %copy-start.9 = (f32[32,1]{0,1:T(1,128)S(1)}, f32[32,1]{0,1:T(1,128)}, u32[]{:S(2)}) copy-start(f32[32,1]{0,1:T(1,128)} %copy-done.8) | copy-start | bytes 388
  67.9 16.9 %copy-start.11 = (f32[32,1]{0,1:T(1,128)S(1)}, f32[32,1]{0,1:T(1,128)}, u32[]{:S(2)}) copy-start(f32[32,1]{0,1:T(1,128)} %copy-done.10) | copy-start | bytes 388
  67.9 16.9 %copy-start.13 = (f32[32,1]{0,1:T(1,128)S(1)}, f32[32,1]{0,1:T(1,128)}, u32[]{:S(2)}) copy-start(f32[32,1]{0,1:T(1,128)} %copy-done.12) | copy-start | bytes 388
  67.9 16.9 %copy-start.18 = (f32[32]{0:T(128)S(1)}, f32[32]{0:T(128)}, u32[]{:S(2)}) copy-start(f32[32]{0:T(128)} %get-tuple-element.129) | copy-start | bytes 388
  67.9 16.9 %copy-start.20 = (f32[32,1]{0,1:T(1,128)S(1)}, f32[32,1]{0,1:T(1,128)}, u32[]{:S(2)}) copy-start(f32[32,1]{0,1:T(1,128)} %copy-done.19) | copy-start | bytes 388
  67.9 16.9 %copy-start.22 = (f32[32,1]{0,1:T(1,128)S(1)}, f32[32,1]{0,1:T(1,128)}, u32[]{:S(2)}) copy-start(f32[32,1]{0,1:T(1,128)} %copy-done.21) | copy-start | bytes 388
  67.9 16.9 %copy-start.24 = (f32[32,1]{0,1:T(1,128)S(1)}, f32[32,1]{0,1:T(1,128)}, u32[]{:S(2)}) copy-start(f32[32,1]{0,1:T(1,128)} %copy-done.23) | copy-start | bytes 388
  67.9 16.9 %copy-start.33 = (f32[32,1]{0,1:T(1,128)S(1)}, f32[32,1]{0,1:T(1,128)}, u32[]{:S(2)}) copy-start(f32[32,1]{0,1:T(1,128)} %get-tuple-element.97) | copy-start | bytes 388
  67.9 16.9 %copy-start.34 = (f32[32,1]{0,1:T(1,128)S(1)}, f32[32,1]{0,1:T(1,128)}, u32[]{:S(2)}) copy-start(f32[32,1]{0,1:T(1,128)} %get-tuple-element.99) | copy-start | bytes 388
  67.9 16.9 %copy-start.35 = (f32[32,1]{0,1:T(1,128)S(1)}, f32[32,1]{0,1:T(1,128)}, u32[]{:S(2)}) copy-start(f32[32,1]{0,1:T(1,128)} %get-tuple-element.101) | copy-start | bytes 388
  68.0 16.9 %copy-start.36 = (f32[32,1]{0,1:T(1,128)S(1)}, f32[32,1]{0,1:T(1,128)}, u32[]{:S(2)}) copy-start(f32[32,1]{0,1:T(1,128)} %get-tuple-element.103) | copy-start | bytes 388
  68.0 16.9 %copy-start.37 = (f32[32]{0:T(128)S(1)}, f32[32]{0:T(128)}, u32[]{:S(2)}) copy-start(f32[32]{0:T(128)} %get-tuple-element.126) | copy-start | bytes 388
  68.0 16.9 %copy-start.38 = (f32[32,1]{0,1:T(1,128)S(1)}, f32[32,1]{0,1:T(1,128)}, u32[]{:S(2)}) copy-start(f32[32,1]{0,1:T(1,128)} %get-tuple-element.87) | copy-start | bytes 388
  68.0 16.9 %copy-start.39 = (f32[32,1]{0,1:T(1,128)S(1)}, f32[32,1]{0,1:T(1,128)}, u32[]{:S(2)}) copy-start(f32[32,1]{0,1:T(1,128)} %get-tuple-element.88) | copy-start | bytes 388
  68.0 17.3 %copy-start.26 = (f32[32,1]{0,1:T(1,128)S(1)}, f32[32,1]{0,1:T(1,128)}, u32[]{:S(2)}) copy-start(f32[32,1]{0,1:T(1,128)} %copy-done.25) | copy-start | bytes 388
  68.0 17.3 %copy-start.41 = (f32[32]{0:T(128)S(1)}, f32[32]{0:T(128)}, u32[]{:S(2)}) copy-start(f32[32]{0:T(128)} %get-tuple-element.78) | copy-start | bytes 388
  68.0 17.3 %copy-start.42 = (f32[32]{0:T(128)S(1)}, f32[32]{0:T(128)}, u32[]{:S(2)}) copy-start(f32[32]{0:T(128)} %get-tuple-element.79) | copy-start | bytes 388
  68.0 17.5 %copy-start.16 = (f32[32,8,1]{0,2,1:T(1,128)S(1)}, f32[32,8,1]{0,2,1:T(1,128)}, u32[]{:S(2)}) copy-start(f32[32,8,1]{0,2,1:T(1,128)} %pad_maximum_fusion.5) | copy-start | bytes 3076
  (28 other events, 186.9 us)
where the time goes:
time: 88.6 us; the launch traced here: 88.1 us
  other arithmetic  33.3 us (38%)
  local copies, waits for them, and re-layouts  27 us (30%)
  blocking collectives  13.9 us (16%)
  starting transfers between devices  10.7 us (12%)
  between operations  1.36 us (2%)
  matrix products  0.94 us (1%)
    select_n x1, other arithmetic, local(): across = jnp.where(fluid_mask, across, 0.0)  14.6 us
    all_gather x1, blocking collectives, local(): cycle_targets = lax.all_gather(target, 'gz', axis=1, tiled=True)  13.9 us
    ppermute x2, starting transfers between devices, padded_2(): before = lax.ppermute(last, axis, up)  6.23 us
    unnamed x99, local copies, waits for them, and re-layouts  6.02 us
    slice x2, local copies, waits for them, and re-layouts, padded_2(): last = lax.slice_in_dim(shard, length - width, length, axis=dim)  5.58 us
    ppermute x2, starting transfers between devices, padded_2(): after = lax.ppermute(first, axis, down)  4.42 us
    ppermute x1, local copies, waits for them, and re-layouts, padded_2(): before = lax.ppermute(last, axis, up)  3.6 us
    mul x1, other arithmetic, normal_term(): face_flux = face_full * (theta[1:] - theta[:-1])  3.5 us
  transfers between devices with their start and end apart: 5, of which 1 were waited for; matrix products, arithmetic and copies ran while one was open for 34% of the time, Pallas kernels for 0%

commit v1 on v0

v1 whole, which is shorter than its diff:
```python
import math

import jax
import jax.numpy as jnp
from jax import lax
from jax.experimental import pallas as pl
from jax.experimental.pallas import tpu as pltpu
from jax.sharding import PartitionSpec as P

keep_factor = -5.0 / 9.0
section_weight = 15.0 / 16.0
stream_courant = 0.4
span_courant = 0.4
damping = 1.0 / 256.0

LB = 8


def pack_kernel(th_ref, xl_ref, xr_ref, zl_ref, zr_ref):
    _, cz, w = th_ref.shape
    i = pl.program_id(0)
    lane = lax.broadcasted_iota(jnp.int32, (cz, w), 1)
    sub8 = lax.broadcasted_iota(jnp.int32, (8, w), 0)

    @pl.when(i % 4 == 0)
    def _():
        xl_ref[...] = jnp.zeros_like(xl_ref)
        xr_ref[...] = jnp.zeros_like(xr_ref)

    acc_l = xl_ref[0]
    acc_r = xr_ref[0]
    for s in range(LB):
        t = th_ref[s]
        slot = (i % 4) * LB + s
        pick = (lane // 4) == slot
        acc_l = jnp.where(pick, pltpu.roll(t, (4 * slot) % w, 1), acc_l)
        acc_r = jnp.where(pick, pltpu.roll(t, (4 * slot + 4) % w, 1), acc_r)
    xl_ref[0] = acc_l
    xr_ref[0] = acc_r
    for p in range(LB // 2):
        a_hi = th_ref[2 * p, cz - 8:cz, :]
        b_hi = th_ref[2 * p + 1, cz - 8:cz, :]
        zl_ref[p] = jnp.where(sub8 < 4, pltpu.roll(a_hi, 4, 0), b_hi)
        a_lo = th_ref[2 * p, 0:8, :]
        b_lo = th_ref[2 * p + 1, 0:8, :]
        zr_ref[p] = jnp.where(sub8 < 4, a_lo, pltpu.roll(b_lo, 4, 0))


def layer_kernel(fluid, block_offset, ny, *refs):
    if fluid:
        (cond_ref, th_ref, prev_ref, next_ref, st_ref, wall_ref, contact_ref,
         u_ref, v_ref, zb_ref, za_ref, xb_ref, xa_ref, _alias_ref,
         sn_ref, tn_ref) = refs
    else:
        (cond_ref, th_ref, prev_ref, next_ref, st_ref, wall_ref, contact_ref,
         bs_ref, sn_ref, int_ref, head_ref) = refs
    _, cz, w = th_ref.shape
    base = (pl.program_id(0) + block_offset) * LB
    wall = wall_ref[...]
    contact = contact_ref[...]

    def cell(y):
        return jnp.where(y < wall, cond_ref[0, y], cond_ref[1, y])

    def face(y):
        yc = jnp.clip(y, 0, ny - 2)
        a = cell(yc)
        b = cell(yc + 1)
        f = 2.0 * a * b / (a + b)
        f = jnp.where(yc == wall - 1, f * contact, f)
        valid = jnp.logical_and(y >= 0, y <= ny - 2)
        return jnp.where(valid, f, 0.0)

    if fluid:
        lane = lax.broadcasted_iota(jnp.int32, (cz, w), 1)
        sub8 = lax.broadcasted_iota(jnp.int32, (8, w), 0)

    heads = []
    face_dn = face(base - 1)
    for s in range(LB):
        y = base + s
        t = th_ref[s]
        tp = th_ref[s - 1] if s > 0 else prev_ref[0]
        tn = th_ref[s + 1] if s < LB - 1 else next_ref[0]
        face_up = face(y)
        normal = face_up * (tn - t) - face_dn * (t - tp)
        face_dn = face_up
        if fluid:
            u = u_ref[s].astype(jnp.float32)
            v = v_ref[s].astype(jnp.float32)
            slot = (pl.program_id(0) % 4) * LB + s
            edge_b = xb_ref[0]
            edge_a = xa_ref[0]
            xm = [None]
            xp = [None]
            for j in range(1, 5):
                xm.append(jnp.where(lane < j, pltpu.roll(edge_b, (w - 4 - 4 * slot + j) % w, 1),
                                    pltpu.roll(t, j, 1)))
                xp.append(jnp.where(lane >= w - j, pltpu.roll(edge_a, (w - j - 4 * slot) % w, 1),
                                    pltpu.roll(t, w - j, 1)))
            packed_b = zb_ref[s // 2]
            packed_a = za_ref[s // 2]
            if s % 2 == 0:
                zb8 = pltpu.roll(packed_b, 4, 0)
                za8 = packed_a
            else:
                zb8 = packed_b
                za8 = pltpu.roll(packed_a, 4, 0)
            zm = [None]
            zp = [None]
            for j in range(1, 5):
                r = pltpu.roll(t, j, 0)
                first = jnp.where(sub8 < j, pltpu.roll(zb8, j, 0), r[0:8])
                zm.append(jnp.concatenate([first, r[8:]], axis=0))
                r = pltpu.roll(t, cz - j, 0)
                last = jnp.where(sub8 >= 8 - j, pltpu.roll(za8, 8 - j, 0), r[cz - 8:])
                zp.append(jnp.concatenate([r[:cz - 8], last], axis=0))

            def slope(m, p):
                acc = -1.0 * m[3] + 9.0 * m[2]
                acc = acc + -45.0 * m[1]
                acc = acc + 45.0 * p[1]
                acc = acc + -9.0 * p[2]
                acc = acc + p[3]
                return acc / 60.0

            def smooth(m, p):
                acc = m[4] + -8.0 * m[3]
                acc = acc + 28.0 * m[2]
                acc = acc + -56.0 * m[1]
                acc = acc + 70.0 * t
                acc = acc + -56.0 * p[1]
                acc = acc + 28.0 * p[2]
                acc = acc + -8.0 * p[3]
                acc = acc + p[4]
                return acc

            span_slope = slope(zm, zp)
            stream_slope = slope(xm, xp)
            smoothing = smooth(zm, zp) + smooth(xm, xp)
            horiz = (-stream_courant * u * stream_slope
                     - span_courant * v * span_slope
                     - damping * smoothing)
            across = jnp.where(y >= wall, horiz, 0.0)
            rate = normal + across
        else:
            rate = normal
        sn = keep_factor * st_ref[s] + rate
        adv = t + section_weight * sn
        sn_ref[s] = sn
        if fluid:
            tn_ref[s] = adv
        else:
            int_ref[s] = jnp.dot(bs_ref[s], adv, precision=lax.Precision.HIGHEST,
                                 preferred_element_type=jnp.float32)
            heads.append(adv[0:1, :])
    if not fluid:
        head_ref[...] = jnp.concatenate(heads, axis=0)


def local(theta, section_store, stream_speed, span_speed, conductivity, wall_layers,
          contact, spanwise_number, block_inverse):
    f32 = jnp.float32
    ny, cz, w = theta.shape
    ns = block_inverse.shape[0]
    nf = ny - ns
    nsb = ns // LB
    nfb = nf // LB
    groups = (nfb + 3) // 4
    ngz = lax.axis_size("gz")
    ngx = lax.axis_size("gx")
    k = lax.axis_index("gz")

    wall2 = jnp.broadcast_to(wall_layers[:, None], (cz, w)).astype(jnp.int32)
    contact2 = jnp.broadcast_to(contact.astype(f32)[None, :], (cz, w))

    smem = pl.BlockSpec(memory_space=pltpu.SMEM)
    blk = lambda off: pl.BlockSpec((LB, cz, w), lambda i: (i + off, 0, 0))
    prev_spec = lambda off: pl.BlockSpec((1, cz, w), lambda i: (jnp.maximum((i + off) * LB - 1, 0), 0, 0))
    next_spec = lambda off: pl.BlockSpec((1, cz, w), lambda i: (jnp.minimum((i + off) * LB + LB, ny - 1), 0, 0))
    full2 = pl.BlockSpec((cz, w), lambda i: (0, 0))

    xl, xr, zl, zr = pl.pallas_call(
        pack_kernel,
        grid=(nfb,),
        in_specs=[blk(nsb)],
        out_specs=[
            pl.BlockSpec((1, cz, w), lambda i: (i // 4, 0, 0)),
            pl.BlockSpec((1, cz, w), lambda i: (i // 4, 0, 0)),
            pl.BlockSpec((LB // 2, 8, w), lambda i: (i, 0, 0)),
            pl.BlockSpec((LB // 2, 8, w), lambda i: (i, 0, 0)),
        ],
        out_shape=[
            jax.ShapeDtypeStruct((groups, cz, w), f32),
            jax.ShapeDtypeStruct((groups, cz, w), f32),
            jax.ShapeDtypeStruct((nf // 2, 8, w), f32),
            jax.ShapeDtypeStruct((nf // 2, 8, w), f32),
        ],
    )(theta)

    xb = lax.ppermute(xr, "gx", [(i, i + 1) for i in range(ngx - 1)])
    xa = lax.ppermute(xl, "gx", [(i + 1, i) for i in range(ngx - 1)])
    zb = lax.ppermute(zl, "gz", [(i, (i + 1) % ngz) for i in range(ngz)])
    za = lax.ppermute(zr, "gz", [((i + 1) % ngz, i) for i in range(ngz)])

    shifted_inverse = jnp.zeros((ns, cz, cz), f32).at[:, 1:, 1:].set(block_inverse)

    sn_part, interior, head = pl.pallas_call(
        lambda *refs: layer_kernel(False, 0, ny, *refs),
        grid=(nsb,),
        in_specs=[smem, blk(0), prev_spec(0), next_spec(0), blk(0), full2, full2,
                  pl.BlockSpec((LB, cz, cz), lambda i: (i, 0, 0))],
        out_specs=[blk(0), blk(0), pl.BlockSpec((LB, w), lambda i: (i, 0))],
        out_shape=[
            jax.ShapeDtypeStruct((ny, cz, w), f32),
            jax.ShapeDtypeStruct((ns, cz, w), f32),
            jax.ShapeDtypeStruct((ns, w), f32),
        ],
    )(conductivity, theta, theta, theta, section_store, wall2, contact2, shifted_inverse)

    number = spanwise_number
    from_left = lax.ppermute(interior[:, cz - 1, :], "gz", [(i, (i + 1) % ngz) for i in range(ngz)])
    target = head + number[:, None] * from_left + number[:, None] * interior[:, 1, :]
    all_targets = lax.all_gather(target, "gz", axis=1, tiled=False)

    square = number * number
    diagonal = 1.0 + 2.0 * number - square * (block_inverse[:, 0, 0] + block_inverse[:, -1, -1])
    beside = square * block_inverse[:, 0, -1]
    q = jnp.arange(ngz, dtype=jnp.int32)
    angle = (2.0 * math.pi / ngz) * q.astype(f32)
    denominator = diagonal[:, None] - 2.0 * beside[:, None] * jnp.cos(angle)[None, :]
    phase = (2.0 * math.pi / ngz) * ((q[:, None] * q[None, :]) % ngz).astype(f32)
    coeff = jnp.sum(jnp.cos(phase)[None, :, :] / denominator[:, :, None], axis=1) / ngz
    own = jnp.take(coeff, (q - k) % ngz, axis=1)
    nxt = jnp.take(coeff, (q - k - 1) % ngz, axis=1)
    head_values = jnp.sum(own[:, :, None] * all_targets, axis=1)
    following = jnp.sum(nxt[:, :, None] * all_targets, axis=1)

    fluid_sn, fluid_tn = pl.pallas_call(
        lambda *refs: layer_kernel(True, nsb, ny, *refs),
        grid=(nfb,),
        in_specs=[smem, blk(nsb), prev_spec(nsb), next_spec(nsb), blk(nsb), full2, full2,
                  blk(nsb), blk(nsb),
                  pl.BlockSpec((LB // 2, 8, w), lambda i: (i, 0, 0)),
                  pl.BlockSpec((LB // 2, 8, w), lambda i: (i, 0, 0)),
                  pl.BlockSpec((1, cz, w), lambda i: (i // 4, 0, 0)),
                  pl.BlockSpec((1, cz, w), lambda i: (i // 4, 0, 0)),
                  pl.BlockSpec(memory_space=pl.ANY)],
        out_specs=[blk(nsb), blk(nsb)],
        out_shape=[
            jax.ShapeDtypeStruct((ny, cz, w), f32),
            jax.ShapeDtypeStruct((ny, cz, w), f32),
        ],
        input_output_aliases={13: 0},
    )(conductivity, theta, theta, theta, section_store, wall2, contact2,
      stream_speed, span_speed, zb, za, xb, xa, sn_part)

    row = jnp.arange(cz, dtype=jnp.int32)
    col0 = jnp.zeros((ns, cz), f32).at[:, 1:].set(block_inverse[:, :, 0])
    col_last = jnp.zeros((ns, cz), f32).at[:, 1:].set(block_inverse[:, :, -1])
    scale = number[:, None, None]
    solved = interior + scale * (col0[:, :, None] * head_values[:, None, :]
                                 + col_last[:, :, None] * following[:, None, :])
    solved = jnp.where((row == 0)[None, :, None], head_values[:, None, :], solved)
    theta_new = lax.dynamic_update_slice_in_dim(fluid_tn, solved, 0, 0)
    return (theta_new, fluid_sn)


def solution(mesh):
    return jax.shard_map(
        local,
        mesh=mesh,
        in_specs=(
            P(None, "gz", "gx"),
            P(None, "gz", "gx"),
            P(None, "gz", "gx"),
            P(None, "gz", "gx"),
            P(),
            P("gz"),
            P("gx"),
            P(),
            P(),
        ),
        out_specs=(P(None, "gz", "gx"), P(None, "gz", "gx")),
        check_vma=False,
    )
```

time: 88.6 us -> 66.5 us (0.75)
  the two profiles are of different devices: /device:TPU:0 before, /device:TPU:5 now
where the time goes in v1:
time: 66.5 us; the launch traced here: 65.7 us
  Pallas kernels  29 us (44%)
  blocking collectives  16.2 us (24%)
  starting transfers between devices  10.4 us (16%)
  local copies, waits for them, and re-layouts  7.17 us (11%)
  other arithmetic  2.06 us (3%)
  between operations  0.88 us (1%)
    all_gather x1, blocking collectives, local(): all_targets = lax.all_gather(target, 'gz', axis=1, tiled=False)  16.2 us
    pallas_call x1, Pallas kernels, local(): pl.pallas_call(lambda *refs: layer_kernel(True, nsb, ny, *refs), grid=(nf...  15.3 us
    pallas_call x1, Pallas kernels, local(): pl.pallas_call(pack_kernel, grid=(nfb,), in_specs=[blk(nsb)], out_specs=[...  9.51 us
    pallas_call x1, Pallas kernels, local(): pl.pallas_call(lambda *refs: layer_kernel(False, 0, ny, *refs), grid=(nsb...  4.2 us
    ppermute x1, starting transfers between devices, local(): xb = lax.ppermute(xr, 'gx', [(i, i + 1) for i in range(ngx - 1)])  3.11 us
    ppermute x1, starting transfers between devices, local(): xa = lax.ppermute(xl, 'gx', [(i + 1, i) for i in range(ngx - 1)])  3.06 us
    ppermute x1, starting transfers between devices, local(): lax.ppermute(interior[:, cz - 1, :], 'gz', [(i, (i + 1) % ngz) for i in r...  2.35 us
    unnamed x24, local copies, waits for them, and re-layouts  1.92 us
  transfers between devices with their start and end apart: 5, of which 0 were waited for; matrix products, arithmetic and copies ran while one was open for 11% of the time, Pallas kernels for 6%

profile of v1, /device:TPU:5, one launch (start us, length us, event | category | flops | bytes accessed | tf_op | source)
XLA Modules:
  0.0 65.7 jit_solution(13268794613405069663)
XLA Ops:
  0.7 9.5 %shard_map.104 = (f32[4,32,128]{2,1,0:T(8,128)}, f32[4,32,128]{2,1,0:T(8,128)}, f32[60,8,128]{2,1,0:T(8,128)}, f32[60,8,128]{2,1,0:T(8,128)}) custom-call(f32[152,32,128]{2,1,0:T(8,128)} %refs_3_.3), custom_call_target="tpu_custom_call" | custom-call | tf_op jit(solution)/shard_map/pallas_call | solution.py:183
  10.2 1.9 %collective-permute-start = (f32[60,8,128]{2,1,0:T(8,128)}, f32[60,8,128]{2,1,0:T(8,128)S(1)}, u32[]{:S(2)}, u32[]{:S(2)}) collective-permute-start(f32[60,8,128]{2,1,0:T(8,128)} %get-tuple-element.48), channel_id=1, source_target_pairs={{0,1},{1,2},{2,3},{3,4},{4,5},{5,6},{6,7},{7,0},{8,9},{9,10},{10,1... | collective-permute-start | bytes 737288 | tf_op jit(solution)/shard_map/ppermute | solution.py:203
  12.0 3.1 %collective-permute-start.2 = (f32[4,32,128]{2,1,0:T(8,128)}, f32[4,32,128]{2,1,0:T(8,128)S(1)}, u32[]{:S(2)}, u32[]{:S(2)}) collective-permute-start(f32[4,32,128]{2,1,0:T(8,128)} %get-tuple-element.50), channel_id=1, source_target_pairs={{0,8},{8,16},{16,24},{1,9},{9,17},{17,25},{2,10},{10,18},{18,26},{... | collective-permute-start | bytes 196616 | tf_op jit(solution)/shard_map/ppermute | solution.py:201
  15.2 3.1 %collective-permute-start.3 = (f32[4,32,128]{2,1,0:T(8,128)}, f32[4,32,128]{2,1,0:T(8,128)S(1)}, u32[]{:S(2)}, u32[]{:S(2)}) collective-permute-start(f32[4,32,128]{2,1,0:T(8,128)} %get-tuple-element.51), channel_id=1, source_target_pairs={{8,0},{16,8},{24,16},{9,1},{17,9},{25,17},{10,2},{18,10},{26,18},{... | collective-permute-start | bytes 196616 | tf_op jit(solution)/shard_map/ppermute | solution.py:202
  18.3 0.3 copy.26
  18.6 1.0 %scatter.10.refs_7_ = f32[32,32,32]{2,1,0:T(8,128)} pad(f32[32,31,31]{2,1,0:T(8,128)S(1)} %copy.26, f32[]{:T(128)} %constant.129.clone.1), padding=0_0x1_0x1_0 | pad | bytes 254084 | tf_op jit(solution)/shard_map/scatter | solution.py:206
  19.6 0.7 %broadcast_in_dim.20.refs_5_ = s32[32,128]{1,0:T(8,128)} broadcast(s32[32]{0:T(128)S(1)} %copy-done.8), dimensions={0} | broadcast | bytes 16512 | tf_op jit(solution)/shard_map/broadcast_in_dim | solution.py:174
  20.2 0.6 broadcast_in_dim.24.refs_6_
  20.8 4.2 %shard_map.105 = (f32[152,32,128]{2,1,0:T(8,128)}, f32[32,32,128]{2,1,0:T(8,128)}, f32[32,128]{1,0:T(8,128)}) custom-call(f32[2,152]{1,0:T(2,128)} %refs_0_.3, f32[152,32,128]{2,1,0:T(8,128)} %refs_3_.3, f32[152,32,128]{2,1,0:T(8,128)} %refs_3_.3, f32[152,32,128]{2,1,0:T(8,128)} %refs_3_.3, f32[152,32,128]{2,1,0:T(8,128)} %refs_4_.3, ...), custom_call_target="tpu_custom_call" | custom-call | tf_op jit(solution)/shard_map/pallas_call | solution.py:208
  25.0 1.4 %copy.28 = f32[32,32,128]{2,0,1:T(8,128)S(1)} copy(f32[32,32,128]{2,1,0:T(8,128)} %get-tuple-element.55) | data formatting | bytes 1048576 | tf_op jit(solution)/shard_map/pallas_call | solution.py:208
  26.4 2.4 %collective-permute-start.4 = (f32[32,128]{1,0:T(8,128)S(1)}, f32[32,128]{1,0:T(8,128)S(1)}, u32[]{:S(2)}, u32[]{:S(2)}) collective-permute-start(f32[32,128]{1,0:T(8,128)S(1)} %slice_bitcast_fusion.1), channel_id=1, source_target_pairs={{0,1},{1,2},{2,3},{3,4},{4,5},{5,6},{6,7},{7,0},{8,9},{9,10},{10,1... | collective-permute-start | bytes 49160 | tf_op jit(solution)/shard_map/ppermute | solution.py:222
  28.8 0.2 add_reduce_fusion
  29.1 0.2 fusion.13
  29.5 0.6 gather_fusion
  30.1 0.6 gather_fusion.1
  30.9 0.4 copy.34
  31.4 0.4 copy.33
  32.0 16.2 %all-gather = f32[32,1024]{1,0:T(8,128)S(1)} all-gather(f32[32,128]{1,0:T(8,128)S(1)} %fusion.3), channel_id=2, replica_groups=mesh['gx'=4,'gz'=8] {'gz'}, dimensions={1}, use_global_device_ids=true | all-gather | bytes 147456 | tf_op jit(solution)/shard_map/all_gather | solution.py:224
  48.2 0.1 fusion
  48.5 0.5 copy-done.4
  49.1 0.1 copy-done.2
  49.2 0.1 copy-done.3
  49.2 15.3 %shard_map.106 = (f32[152,32,128]{2,1,0:T(8,128)}, f32[152,32,128]{2,1,0:T(8,128)}) custom-call(f32[2,152]{1,0:T(2,128)} %refs_0_.3, f32[152,32,128]{2,1,0:T(8,128)} %refs_3_.3, f32[152,32,128]{2,1,0:T(8,128)} %refs_3_.3, f32[152,32,128]{2,1,0:T(8,128)} %refs_3_.3, f32[152,32,128]{2,1,0:T(8,128)} %refs_4_.3, ...), custom_call_target="tpu_custom_call", output_to_operand_aliasing={{0}: (13, {})} | custom-call | tf_op jit(solution)/shard_map/pallas_call | solution.py:239
  64.5 1.2 %select_dynamic-update-slice_fusion = f32[152,32,128]{2,1,0:T(8,128)} fusion(f32[152,32,128]{2,1,0:T(8,128)} %get-tuple-element.53, f32[32,32,128]{2,1,0:T(8,128)S(1)} %copy-done.1, f32[32,128]{1,0:T(8,128)S(1)} %get-tuple-element.60, f32[32,32]{1,0:T(8,128)S(1)} %scatter.14, f32[32,32]{1,0:T(8,128)S(1)} %scatter.11, f32[32]{0:T(128)S(1)} %copy-done.7, ...), kind=kLoop, calls=%fused_computation.2 | loop fusion | flops 786432 | bytes 1089696 | tf_op jit(solution)/shard_map/dynamic_update_slice | solution.py:265
  (44 shorter events, 0.9 us)
Async XLA Ops:
  0.6 17.6 %copy-start.9 = (s32[128]{0:T(128)S(1)}, s32[128]{0:T(128)}, u32[]{:S(2)}) copy-start(s32[128]{0:T(128)} %param.23) | copy-start | bytes 1540
  0.6 17.6 %copy-start = (f32[32,31,31]{2,0,1:T(8,128)S(1)}, f32[32,31,31]{2,0,1:T(8,128)}, u32[]{:S(2)}) copy-start(f32[32,31,31]{2,0,1:T(8,128)} %param.25) | copy-start | bytes 369028
  0.7 18.9 %copy-start.8 = (s32[32]{0:T(128)S(1)}, s32[32]{0:T(128)}, u32[]{:S(2)}) copy-start(s32[32]{0:T(128)} %param.22) | copy-start | bytes 388
  10.2 38.3 %collective-permute-start = (f32[60,8,128]{2,1,0:T(8,128)}, f32[60,8,128]{2,1,0:T(8,128)S(1)}, u32[]{:S(2)}, u32[]{:S(2)}) collective-permute-start(f32[60,8,128]{2,1,0:T(8,128)} %get-tuple-element.48), channel_id=1, source_target_pairs={{0,1},{1,2},{2,3},{3,4},{4,5},{5,6},{6,7},{7,0},{8,9},{9,10},{10,1... | collective-permute-start | bytes 737288 | tf_op jit(solution)/shard_map/ppermute | solution.py:203
  12.0 36.4 %collective-permute-start.1 = (f32[60,8,128]{2,1,0:T(8,128)}, f32[60,8,128]{2,1,0:T(8,128)S(1)}, u32[]{:S(2)}, u32[]{:S(2)}) collective-permute-start(f32[60,8,128]{2,1,0:T(8,128)} %get-tuple-element.49), channel_id=1, source_target_pairs={{1,0},{2,1},{3,2},{4,3},{5,4},{6,5},{7,6},{0,7},{9,8},{10,9},{11,1... | collective-permute-start | bytes 737288 | tf_op jit(solution)/shard_map/ppermute | solution.py:204
  12.0 36.4 %collective-permute-start.2 = (f32[4,32,128]{2,1,0:T(8,128)}, f32[4,32,128]{2,1,0:T(8,128)S(1)}, u32[]{:S(2)}, u32[]{:S(2)}) collective-permute-start(f32[4,32,128]{2,1,0:T(8,128)} %get-tuple-element.50), channel_id=1, source_target_pairs={{0,8},{8,16},{16,24},{1,9},{9,17},{17,25},{2,10},{10,18},{18,26},{... | collective-permute-start | bytes 196616 | tf_op jit(solution)/shard_map/ppermute | solution.py:201
  15.2 33.3 %collective-permute-start.3 = (f32[4,32,128]{2,1,0:T(8,128)}, f32[4,32,128]{2,1,0:T(8,128)S(1)}, u32[]{:S(2)}, u32[]{:S(2)}) collective-permute-start(f32[4,32,128]{2,1,0:T(8,128)} %get-tuple-element.51), channel_id=1, source_target_pairs={{8,0},{16,8},{24,16},{9,1},{17,9},{25,17},{10,2},{18,10},{26,18},{... | collective-permute-start | bytes 196616 | tf_op jit(solution)/shard_map/ppermute | solution.py:202
  25.0 4.3 %copy-start.7 = (f32[32]{0:T(128)S(1)}, f32[32]{0:T(128)}, u32[]{:S(2)}) copy-start(f32[32]{0:T(128)} %param.24) | copy-start | bytes 388
  25.0 6.9 %copy-start.6 = (f32[32,128]{1,0:T(8,128)S(1)}, f32[32,128]{1,0:T(8,128)}, u32[]{:S(2)}) copy-start(f32[32,128]{1,0:T(8,128)} %get-tuple-element.54) | copy-start | bytes 49156
  26.4 5.5 %collective-permute-start.4 = (f32[32,128]{1,0:T(8,128)S(1)}, f32[32,128]{1,0:T(8,128)S(1)}, u32[]{:S(2)}, u32[]{:S(2)}) collective-permute-start(f32[32,128]{1,0:T(8,128)S(1)} %slice_bitcast_fusion.1), channel_id=1, source_target_pairs={{0,1},{1,2},{2,3},{3,4},{4,5},{5,6},{6,7},{7,0},{8,9},{9,10},{10,1... | collective-permute-start | bytes 49160 | tf_op jit(solution)/shard_map/ppermute | solution.py:222
  48.4 0.6 copy-start.4
  48.4 0.6 copy-start.5
  48.5 0.7 %copy-start.2 = (f32[60,8,128]{2,1,0:T(8,128)}, f32[60,8,128]{2,1,0:T(8,128)S(1)}, u32[]{:S(2)}) copy-start(f32[60,8,128]{2,1,0:T(8,128)S(1)} %collective-permute-done.refs_9_) | copy-start | bytes 737284
  48.5 0.8 %copy-start.3 = (f32[60,8,128]{2,1,0:T(8,128)}, f32[60,8,128]{2,1,0:T(8,128)S(1)}, u32[]{:S(2)}) copy-start(f32[60,8,128]{2,1,0:T(8,128)S(1)} %collective-permute-done.1.refs_10_) | copy-start | bytes 737284
  49.2 15.3 %copy-start.1 = (f32[32,32,128]{2,1,0:T(8,128)S(1)}, f32[32,32,128]{2,1,0:T(8,128)}, u32[]{:S(2)}) copy-start(f32[32,32,128]{2,1,0:T(8,128)} %get-tuple-element.55) | copy-start | bytes 1572868

commit v2 on v1

v2 whole, which is shorter than its diff:
```python
import math

import jax
import jax.numpy as jnp
from jax import lax
from jax.experimental import pallas as pl
from jax.experimental.pallas import tpu as pltpu
from jax.sharding import PartitionSpec as P

keep_factor = -5.0 / 9.0
section_weight = 15.0 / 16.0
stream_courant = 0.4
span_courant = 0.4
damping = 1.0 / 256.0

LB = 8


def pack_kernel(th_ref, xl_ref, xr_ref, zl_ref, zr_ref):
    _, cz, w = th_ref.shape
    lane8 = lax.broadcasted_iota(jnp.int32, (8, w), 1)
    sub8 = lax.broadcasted_iota(jnp.int32, (8, w), 0)
    acc_l = jnp.zeros((8, w), jnp.float32)
    acc_r = jnp.zeros((8, w), jnp.float32)
    for s in range(LB):
        for v in range(cz // 8):
            t = th_ref[s, 8 * v:8 * v + 8, :]
            pos = 4 * LB * v + 4 * s
            pick = jnp.logical_and(lane8 >= pos, lane8 < pos + 4)
            acc_l = jnp.where(pick, pltpu.roll(t, pos % w, 1), acc_l)
            acc_r = jnp.where(pick, pltpu.roll(t, (pos + 4) % w, 1), acc_r)
    xl_ref[0] = acc_l
    xr_ref[0] = acc_r
    for p in range(LB // 2):
        a_hi = th_ref[2 * p, cz - 8:cz, :]
        b_hi = th_ref[2 * p + 1, cz - 8:cz, :]
        zl_ref[p] = jnp.where(sub8 < 4, pltpu.roll(a_hi, 4, 0), b_hi)
        a_lo = th_ref[2 * p, 0:8, :]
        b_lo = th_ref[2 * p + 1, 0:8, :]
        zr_ref[p] = jnp.where(sub8 < 4, a_lo, pltpu.roll(b_lo, 4, 0))


def layer_kernel(fluid, block_offset, *refs):
    if fluid:
        (face_ref, th_ref, prev_ref, next_ref, st_ref, wall_ref, contact_ref,
         u_ref, v_ref, zb_ref, za_ref, xb_ref, xa_ref, _alias_ref,
         sn_ref, tn_ref, ext_ref) = refs
    else:
        (face_ref, th_ref, prev_ref, next_ref, st_ref, wall_ref, contact_ref,
         bs_ref, sn_ref, int_ref, head_ref) = refs
    _, cz, w = th_ref.shape
    base = (pl.program_id(0) + block_offset) * LB
    wall = wall_ref[...]
    contact = contact_ref[...]

    def face(y):
        both_solid = face_ref[0, y + 1]
        both_fluid = face_ref[2, y + 1]
        at_wall = face_ref[1, y + 1] * contact
        return jnp.where(y + 1 < wall, both_solid, jnp.where(y >= wall, both_fluid, at_wall))

    if fluid:
        lane = lax.broadcasted_iota(jnp.int32, (8, w), 1)
        nv = cz // 8
        slope_scale = -stream_courant / 60.0

    heads = []
    face_dn = face(base - 1)
    for s in range(LB):
        y = base + s
        t = th_ref[s]
        tp = th_ref[s - 1] if s > 0 else prev_ref[0]
        tn = th_ref[s + 1] if s < LB - 1 else next_ref[0]
        face_up = face(y)
        normal = face_up * (tn - t) - face_dn * (t - tp)
        face_dn = face_up
        if fluid:
            u = u_ref[s].astype(jnp.float32)
            v = v_ref[s].astype(jnp.float32)
            edge_b = xb_ref[0]
            edge_a = xa_ref[0]
            xm = [[None] * nv for _ in range(5)]
            xp = [[None] * nv for _ in range(5)]
            for g in range(nv):
                tg = t[8 * g:8 * g + 8]
                pos = 4 * LB * g + 4 * s
                for j in range(1, 5):
                    xm[j][g] = jnp.where(lane < j, pltpu.roll(edge_b, (j - 4 - pos) % w, 1),
                                         pltpu.roll(tg, j, 1))
                    xp[j][g] = jnp.where(lane >= w - j, pltpu.roll(edge_a, (w - j - pos) % w, 1),
                                         pltpu.roll(tg, w - j, 1))
            xm = [None] + [jnp.concatenate(xm[j], axis=0) for j in range(1, 5)]
            xp = [None] + [jnp.concatenate(xp[j], axis=0) for j in range(1, 5)]
            packed_b = zb_ref[s // 2]
            packed_a = za_ref[s // 2]
            if s % 2 == 0:
                packed_b = pltpu.roll(packed_b, 4, 0)
            else:
                packed_a = pltpu.roll(packed_a, 4, 0)
            ext_ref[0:8, :] = packed_b
            ext_ref[8:8 + cz, :] = t
            ext_ref[8 + cz:16 + cz, :] = packed_a
            zm = [None] + [ext_ref[8 - j:8 - j + cz, :] for j in range(1, 5)]
            zp = [None] + [ext_ref[8 + j:8 + j + cz, :] for j in range(1, 5)]

            def slope(m, p):
                return 45.0 * (p[1] - m[1]) - 9.0 * (p[2] - m[2]) + (p[3] - m[3])

            def smooth(m, p):
                return ((p[4] + m[4]) - 8.0 * (p[3] + m[3]) + 28.0 * (p[2] + m[2])
                        - 56.0 * (p[1] + m[1]))

            smoothing = smooth(zm, zp) + smooth(xm, xp) + 140.0 * t
            horiz = (slope_scale * (u * slope(xm, xp) + v * slope(zm, zp))
                     - damping * smoothing)
            across = jnp.where(y >= wall, horiz, 0.0)
            rate = normal + across
        else:
            rate = normal
        sn = keep_factor * st_ref[s] + rate
        adv = t + section_weight * sn
        sn_ref[s] = sn
        if fluid:
            tn_ref[s] = adv
        else:
            int_ref[s] = jnp.dot(bs_ref[s], adv, precision=lax.Precision.HIGHEST,
                                 preferred_element_type=jnp.float32)
            heads.append(adv[0:1, :])
    if not fluid:
        head_ref[...] = jnp.concatenate(heads, axis=0)


def local(theta, section_store, stream_speed, span_speed, conductivity, wall_layers,
          contact, spanwise_number, block_inverse):
    f32 = jnp.float32
    ny, cz, w = theta.shape
    ns = block_inverse.shape[0]
    nf = ny - ns
    nsb = ns // LB
    nfb = nf // LB
    ngz = lax.axis_size("gz")
    ngx = lax.axis_size("gx")

    wall2 = jnp.broadcast_to(wall_layers[:, None], (cz, w)).astype(jnp.int32)
    contact2 = jnp.broadcast_to(contact.astype(f32)[None, :], (cz, w))

    solid_c = conductivity[0]
    fluid_c = conductivity[1]

    def harmonic(a, b):
        return 2.0 * a * b / (a + b)

    zero = jnp.zeros((1,), f32)
    faces = jnp.stack([
        jnp.concatenate([zero, harmonic(solid_c[:-1], solid_c[1:]), zero]),
        jnp.concatenate([zero, harmonic(solid_c[:-1], fluid_c[1:]), zero]),
        jnp.concatenate([zero, harmonic(fluid_c[:-1], fluid_c[1:]), zero]),
    ])

    smem = pl.BlockSpec(memory_space=pltpu.SMEM)
    blk = lambda off: pl.BlockSpec((LB, cz, w), lambda i: (i + off, 0, 0))
    prev_spec = lambda off: pl.BlockSpec((1, cz, w), lambda i: (jnp.maximum((i + off) * LB - 1, 0), 0, 0))
    next_spec = lambda off: pl.BlockSpec((1, cz, w), lambda i: (jnp.minimum((i + off) * LB + LB, ny - 1), 0, 0))
    full2 = pl.BlockSpec((cz, w), lambda i: (0, 0))
    edge_spec = pl.BlockSpec((1, 8, w), lambda i: (i, 0, 0))
    rows_spec = pl.BlockSpec((LB // 2, 8, w), lambda i: (i, 0, 0))

    xl, xr, zl, zr = pl.pallas_call(
        pack_kernel,
        grid=(nfb,),
        in_specs=[blk(nsb)],
        out_specs=[edge_spec, edge_spec, rows_spec, rows_spec],
        out_shape=[
            jax.ShapeDtypeStruct((nfb, 8, w), f32),
            jax.ShapeDtypeStruct((nfb, 8, w), f32),
            jax.ShapeDtypeStruct((nf // 2, 8, w), f32),
            jax.ShapeDtypeStruct((nf // 2, 8, w), f32),
        ],
    )(theta)

    xb = lax.ppermute(xr, "gx", [(i, i + 1) for i in range(ngx - 1)])
    xa = lax.ppermute(xl, "gx", [(i + 1, i) for i in range(ngx - 1)])
    zb = lax.ppermute(zl, "gz", [(i, (i + 1) % ngz) for i in range(ngz)])
    za = lax.ppermute(zr, "gz", [((i + 1) % ngz, i) for i in range(ngz)])

    shifted_inverse = jnp.zeros((ns, cz, cz), f32).at[:, 1:, 1:].set(block_inverse)

    sn_part, interior, head = pl.pallas_call(
        lambda *refs: layer_kernel(False, 0, *refs),
        grid=(nsb,),
        in_specs=[smem, blk(0), prev_spec(0), next_spec(0), blk(0), full2, full2,
                  pl.BlockSpec((LB, cz, cz), lambda i: (i, 0, 0))],
        out_specs=[blk(0), blk(0), pl.BlockSpec((LB, w), lambda i: (i, 0))],
        out_shape=[
            jax.ShapeDtypeStruct((ny, cz, w), f32),
            jax.ShapeDtypeStruct((ns, cz, w), f32),
            jax.ShapeDtypeStruct((ns, w), f32),
        ],
    )(faces, theta, theta, theta, section_store, wall2, contact2, shifted_inverse)

    number = spanwise_number
    mine = jnp.stack([head, interior[:, 1, :], interior[:, cz - 1, :]])
    gathered = [mine]
    for d in range(1, ngz):
        gathered.append(lax.ppermute(mine, "gz", [(i, (i + d) % ngz) for i in range(ngz)]))
    targets = []
    for d in range(ngz):
        left = gathered[(d + 1) % ngz][2]
        targets.append(gathered[d][0] + number[:, None] * left + number[:, None] * gathered[d][1])

    square = number * number
    diagonal = 1.0 + 2.0 * number - square * (block_inverse[:, 0, 0] + block_inverse[:, -1, -1])
    beside = square * block_inverse[:, 0, -1]
    q = jnp.arange(ngz, dtype=jnp.int32)
    angle = (2.0 * math.pi / ngz) * q.astype(f32)
    denominator = diagonal[:, None] - 2.0 * beside[:, None] * jnp.cos(angle)[None, :]
    phase = (2.0 * math.pi / ngz) * ((q[:, None] * q[None, :]) % ngz).astype(f32)
    coeff = jnp.sum(jnp.cos(phase)[None, :, :] / denominator[:, :, None], axis=1) / ngz
    head_values = sum(coeff[:, (-d) % ngz, None] * targets[d] for d in range(ngz))
    following = sum(coeff[:, (-d - 1) % ngz, None] * targets[d] for d in range(ngz))

    fluid_sn, fluid_tn = pl.pallas_call(
        lambda *refs: layer_kernel(True, nsb, *refs),
        grid=(nfb,),
        in_specs=[smem, blk(nsb), prev_spec(nsb), next_spec(nsb), blk(nsb), full2, full2,
                  blk(nsb), blk(nsb), rows_spec, rows_spec, edge_spec, edge_spec,
                  pl.BlockSpec(memory_space=pl.ANY)],
        out_specs=[blk(nsb), blk(nsb)],
        out_shape=[
            jax.ShapeDtypeStruct((ny, cz, w), f32),
            jax.ShapeDtypeStruct((ny, cz, w), f32),
        ],
        scratch_shapes=[pltpu.VMEM((cz + 16, w), f32)],
        input_output_aliases={13: 0},
    )(faces, theta, theta, theta, section_store, wall2, contact2,
      stream_speed, span_speed, zb, za, xb, xa, sn_part)

    row = jnp.arange(cz, dtype=jnp.int32)
    col0 = jnp.zeros((ns, cz), f32).at[:, 1:].set(block_inverse[:, :, 0])
    col_last = jnp.zeros((ns, cz), f32).at[:, 1:].set(block_inverse[:, :, -1])
    scale = number[:, None, None]
    solved = interior + scale * (col0[:, :, None] * head_values[:, None, :]
                                 + col_last[:, :, None] * following[:, None, :])
    solved = jnp.where((row == 0)[None, :, None], head_values[:, None, :], solved)
    theta_new = lax.dynamic_update_slice_in_dim(fluid_tn, solved, 0, 0)
    return (theta_new, fluid_sn)


def solution(mesh):
    return jax.shard_map(
        local,
        mesh=mesh,
        in_specs=(
            P(None, "gz", "gx"),
            P(None, "gz", "gx"),
            P(None, "gz", "gx"),
            P(None, "gz", "gx"),
            P(),
            P("gz"),
            P("gx"),
            P(),
            P(),
        ),
        out_specs=(P(None, "gz", "gx"), P(None, "gz", "gx")),
        check_vma=False,
    )
```

time: 66.5 us -> 66.8 us (level)
  the two profiles are of different devices: /device:TPU:5 before, /device:TPU:0 now
where the time goes in v2:
time: 66.8 us; the launch traced here: 65.9 us
  Pallas kernels  28.7 us (43%)
  starting transfers between devices  19.1 us (29%)
  local copies, waits for them, and re-layouts  8.53 us (13%)
  waiting for transfers between devices  4.8 us (7%)
  other arithmetic  4.01 us (6%)
  between operations  0.82 us (1%)
    pallas_call x1, Pallas kernels, local(): pl.pallas_call(lambda *refs: layer_kernel(True, nsb, *refs), grid=(nfb,),...  15.1 us
    ppermute x7, starting transfers between devices, local(): lax.ppermute(mine, 'gz', [(i, (i + d) % ngz) for i in range(ngz)])  10.8 us
    pallas_call x1, Pallas kernels, local(): pl.pallas_call(pack_kernel, grid=(nfb,), in_specs=[blk(nsb)], out_specs=[...  9.36 us
    ppermute x1, waiting for transfers between devices, local(): xa = lax.ppermute(xl, 'gx', [(i + 1, i) for i in range(ngx - 1)])  4.17 us
    pallas_call x1, Pallas kernels, local(): pl.pallas_call(lambda *refs: layer_kernel(False, 0, *refs), grid=(nsb,),...  4.16 us
    ppermute x1, starting transfers between devices, local(): za = lax.ppermute(zr, 'gz', [((i + 1) % ngz, i) for i in range(ngz)])  3.54 us
    ppermute x1, starting transfers between devices, local(): xb = lax.ppermute(xr, 'gx', [(i, i + 1) for i in range(ngx - 1)])  3.39 us
    unnamed x19, local copies, waits for them, and re-layouts  2.97 us
  transfers between devices with their start and end apart: 11, of which 2 were waited for; matrix products, arithmetic and copies ran while one was open for 3% of the time, Pallas kernels for 14%

profile of v2, /device:TPU:0, one launch (start us, length us, event | category | flops | bytes accessed | tf_op | source)
XLA Modules:
  0.0 65.9 jit_solution(9130126219217798905)
XLA Ops:
  0.6 0.9 %fusion.46 = (f32[1,151]{1,0:T(1,128)S(1)}, f32[1,151]{1,0:T(1,128)S(1)}, f32[1,151]{1,0:T(1,128)S(1)}, f32[1,151]{1,0:T(1,128)S(1)}) fusion(f32[2,152]{1,0:T(2,128)} %param.19), kind=kLoop, calls=%fused_computation.97 | loop fusion | bytes 4832 | tf_op jit(solution)/shard_map/slice | solution.py:155
  1.5 0.7 convert_element_type.17
  2.2 1.3 %copy.22 = f32[32,31,31]{2,1,0:T(8,128)S(1)} copy(f32[32,31,31]{2,0,1:T(8,128)} %param.23) | data formatting | bytes 246016 | tf_op args[8]
  3.7 1.0 %scatter.10.refs_7_ = f32[32,32,32]{2,1,0:T(8,128)} pad(f32[32,31,31]{2,1,0:T(8,128)S(1)} %copy.22, f32[]{:T(128)} %constant.105.clone.1), padding=0_0x1_0x1_0 | pad | bytes 254084 | tf_op jit(solution)/shard_map/scatter | solution.py:186
  4.7 0.6 pad_maximum_fusion.1.refs_0_
  5.3 1.3 %broadcast_in_dim.14.refs_5_ = s32[32,128]{1,0:T(8,128)} broadcast(s32[32]{0:T(128)} %param.20), dimensions={0} | broadcast | bytes 16512 | tf_op jit(solution)/shard_map/broadcast_in_dim | solution.py:144
  6.6 0.6 broadcast_in_dim.15.refs_6_
  7.2 4.2 %shard_map.105 = (f32[152,32,128]{2,1,0:T(8,128)}, f32[32,32,128]{2,1,0:T(8,128)}, f32[32,128]{1,0:T(8,128)}) custom-call(f32[3,153]{1,0:T(4,128)} %pad_maximum_fusion.1.refs_0_, f32[152,32,128]{2,1,0:T(8,128)} %refs_3_.3, f32[152,32,128]{2,1,0:T(8,128)} %refs_3_.3, f32[152,32,128]{2,1,0:T(8,128)} %refs_3_.3, f32[152,32,128]{2,1,0:T(8,128)} %refs_4_.3, ...), custom_call_target="tpu_custom_call" | custom-call | tf_op jit(solution)/shard_map/pallas_call | solution.py:188
  11.4 1.4 %copy.23 = f32[32,32,128]{2,0,1:T(8,128)S(1)} copy(f32[32,32,128]{2,1,0:T(8,128)} %get-tuple-element.54) | data formatting | bytes 1048576 | tf_op jit(solution)/shard_map/pallas_call | solution.py:188
  12.8 0.7 %pad_maximum_fusion = f32[3,32,128]{2,1,0:T(8,128)S(1)} fusion(f32[1,32,128]{2,1,0:T(8,128)S(1)} %get-tuple-element.68, f32[1,32,128]{2,1,0:T(8,128)S(1)} %get-tuple-element.67, f32[1,32,128]{2,1,0:T(8,128)} %bitcast.191), kind=kLoop, calls=%fused_computation.1 | loop fusion | flops 24576 | bytes 98304 | tf_op jit(solution)/shard_map/stack | solution.py:202
  13.9 2.6 %collective-permute-start.5 = (f32[3,32,128]{2,1,0:T(8,128)S(1)}, f32[3,32,128]{2,1,0:T(8,128)S(1)}, u32[]{:S(2)}, u32[]{:S(2)}) collective-permute-start(f32[3,32,128]{2,1,0:T(8,128)S(1)} %pad_maximum_fusion), channel_id=1, source_target_pairs={{0,2},{1,3},{2,4},{3,5},{4,6},{5,7},{6,0},{7,1},{8,10},{9,11},{10,... | collective-permute-start | bytes 147464 | tf_op jit(solution)/shard_map/ppermute | solution.py:205
  16.6 2.6 %collective-permute-start.6 = (f32[3,32,128]{2,1,0:T(8,128)S(1)}, f32[3,32,128]{2,1,0:T(8,128)S(1)}, u32[]{:S(2)}, u32[]{:S(2)}) collective-permute-start(f32[3,32,128]{2,1,0:T(8,128)S(1)} %pad_maximum_fusion), channel_id=1, source_target_pairs={{0,3},{1,4},{2,5},{3,6},{4,7},{5,0},{6,1},{7,2},{8,11},{9,12},{10,... | collective-permute-start | bytes 147464 | tf_op jit(solution)/shard_map/ppermute | solution.py:205
  19.1 1.2 %collective-permute-start.7 = (f32[3,32,128]{2,1,0:T(8,128)S(1)}, f32[3,32,128]{2,1,0:T(8,128)S(1)}, u32[]{:S(2)}, u32[]{:S(2)}) collective-permute-start(f32[3,32,128]{2,1,0:T(8,128)S(1)} %pad_maximum_fusion), channel_id=1, source_target_pairs={{0,4},{1,5},{2,6},{3,7},{4,0},{5,1},{6,2},{7,3},{8,12},{9,13},{10,... | collective-permute-start | bytes 147464 | tf_op jit(solution)/shard_map/ppermute | solution.py:205
  20.4 1.2 %collective-permute-start.8 = (f32[3,32,128]{2,1,0:T(8,128)S(1)}, f32[3,32,128]{2,1,0:T(8,128)S(1)}, u32[]{:S(2)}, u32[]{:S(2)}) collective-permute-start(f32[3,32,128]{2,1,0:T(8,128)S(1)} %pad_maximum_fusion), channel_id=1, source_target_pairs={{0,5},{1,6},{2,7},{3,0},{4,1},{5,2},{6,3},{7,4},{8,13},{9,14},{10,... | collective-permute-start | bytes 147464 | tf_op jit(solution)/shard_map/ppermute | solution.py:205
  22.2 1.4 %collective-permute-start.9 = (f32[3,32,128]{2,1,0:T(8,128)S(1)}, f32[3,32,128]{2,1,0:T(8,128)S(1)}, u32[]{:S(2)}, u32[]{:S(2)}) collective-permute-start(f32[3,32,128]{2,1,0:T(8,128)S(1)} %pad_maximum_fusion), channel_id=1, source_target_pairs={{0,6},{1,7},{2,0},{3,1},{4,2},{5,3},{6,4},{7,5},{8,14},{9,15},{10,... | collective-permute-start | bytes 147464 | tf_op jit(solution)/shard_map/ppermute | solution.py:205
  23.6 1.4 %collective-permute-start.10 = (f32[3,32,128]{2,1,0:T(8,128)S(1)}, f32[3,32,128]{2,1,0:T(8,128)S(1)}, u32[]{:S(2)}, u32[]{:S(2)}) collective-permute-start(f32[3,32,128]{2,1,0:T(8,128)S(1)} %pad_maximum_fusion), channel_id=1, source_target_pairs={{0,7},{1,0},{2,1},{3,2},{4,3},{5,4},{6,5},{7,6},{8,15},{9,8},{10,9... | collective-permute-start | bytes 147464 | tf_op jit(solution)/shard_map/ppermute | solution.py:205
  25.1 9.4 %shard_map.104 = (f32[15,8,128]{2,1,0:T(8,128)}, f32[15,8,128]{2,1,0:T(8,128)}, f32[60,8,128]{2,1,0:T(8,128)}, f32[60,8,128]{2,1,0:T(8,128)}) custom-call(f32[152,32,128]{2,1,0:T(8,128)} %refs_3_.3), custom_call_target="tpu_custom_call" | custom-call | tf_op jit(solution)/shard_map/pallas_call | solution.py:168
  35.4 3.5 %collective-permute-start.1 = (f32[60,8,128]{2,1,0:T(8,128)}, f32[60,8,128]{2,1,0:T(8,128)S(1)}, u32[]{:S(2)}, u32[]{:S(2)}) collective-permute-start(f32[60,8,128]{2,1,0:T(8,128)} %get-tuple-element.48), channel_id=1, source_target_pairs={{1,0},{2,1},{3,2},{4,3},{5,4},{6,5},{7,6},{0,7},{9,8},{10,9},{11,1... | collective-permute-start | bytes 737288 | tf_op jit(solution)/shard_map/ppermute | solution.py:184
  39.0 3.4 %collective-permute-start.2 = (f32[15,8,128]{2,1,0:T(8,128)}, f32[15,8,128]{2,1,0:T(8,128)S(1)}, u32[]{:S(2)}, u32[]{:S(2)}) collective-permute-start(f32[15,8,128]{2,1,0:T(8,128)} %get-tuple-element.49), channel_id=1, source_target_pairs={{0,8},{8,16},{16,24},{1,9},{9,17},{17,25},{2,10},{10,18},{18,26},{... | collective-permute-start | bytes 184328 | tf_op jit(solution)/shard_map/ppermute | solution.py:181
  42.4 1.3 %collective-permute-start.3 = (f32[15,8,128]{2,1,0:T(8,128)}, f32[15,8,128]{2,1,0:T(8,128)S(1)}, u32[]{:S(2)}, u32[]{:S(2)}) collective-permute-start(f32[15,8,128]{2,1,0:T(8,128)} %get-tuple-element.50), channel_id=1, source_target_pairs={{8,0},{16,8},{24,16},{9,1},{17,9},{25,17},{10,2},{18,10},{26,18},{... | collective-permute-start | bytes 184328 | tf_op jit(solution)/shard_map/ppermute | solution.py:182
  43.9 0.6 collective-permute-done.2.refs_11_
  44.5 4.2 %collective-permute-done.3.refs_12_ = f32[15,8,128]{2,1,0:T(8,128)S(1)} collective-permute-done((f32[15,8,128]{2,1,0:T(8,128)}, f32[15,8,128]{2,1,0:T(8,128)S(1)}, u32[]{:S(2)}, u32[]{:S(2)}) %collective-permute-start.3) | collective-permute-done | bytes 61472 | tf_op jit(solution)/shard_map/ppermute | solution.py:182
  49.5 15.1 %shard_map.106 = (f32[152,32,128]{2,1,0:T(8,128)}, f32[152,32,128]{2,1,0:T(8,128)}) custom-call(f32[3,153]{1,0:T(4,128)} %pad_maximum_fusion.1.refs_0_, f32[152,32,128]{2,1,0:T(8,128)} %refs_3_.3, f32[152,32,128]{2,1,0:T(8,128)} %refs_3_.3, f32[152,32,128]{2,1,0:T(8,128)} %refs_3_.3, f32[152,32,128]{2,1,0:T(8,128)} %refs_4_.3, ...), custom_call_target="tpu_custom_call", output_to_operand_aliasing={{0}: (13, {})} | custom-call | tf_op jit(solution)/shard_map/pallas_call | solution.py:222
  64.7 1.2 %select_dynamic-update-slice_fusion = f32[152,32,128]{2,1,0:T(8,128)} fusion(f32[152,32,128]{2,1,0:T(8,128)} %get-tuple-element.52, f32[32,32,128]{2,1,0:T(8,128)S(1)} %copy-done.1, f32[32,128]{1,0:T(8,128)S(1)} %multiply_add_fusion, f32[32,32]{1,0:T(8,128)S(1)} %scatter.14, f32[32,32]{1,0:T(8,128)S(1)} %scatter.11, f32[32]{0:T(128)S(1)} %copy-done.7, ...), kind=kLoop, calls=%fused_computation | loop fusion | flops 786432 | bytes 1089696 | tf_op jit(solution)/shard_map/dynamic_update_slice | solution.py:245
  (47 shorter events, 3.3 us)
Async XLA Ops:
  7.2 14.3 %copy-start = (f32[32,31,31]{2,0,1:T(8,128)S(1)}, f32[32,31,31]{2,0,1:T(8,128)}, u32[]{:S(2)}) copy-start(f32[32,31,31]{2,0,1:T(8,128)} %param.23) | copy-start | bytes 369028
  11.4 10.6 %copy-start.7 = (f32[32]{0:T(128)S(1)}, f32[32]{0:T(128)}, u32[]{:S(2)}) copy-start(f32[32]{0:T(128)} %param.22) | copy-start | bytes 388
  13.5 8.7 %collective-permute-start.4 = (f32[3,32,128]{2,1,0:T(8,128)S(1)}, f32[3,32,128]{2,1,0:T(8,128)S(1)}, u32[]{:S(2)}, u32[]{:S(2)}) collective-permute-start(f32[3,32,128]{2,1,0:T(8,128)S(1)} %pad_maximum_fusion), channel_id=1, source_target_pairs={{0,1},{1,2},{2,3},{3,4},{4,5},{5,6},{6,7},{7,0},{8,9},{9,10},{10,1... | collective-permute-start | bytes 147464 | tf_op jit(solution)/shard_map/ppermute | solution.py:205
  13.9 9.7 %collective-permute-start.5 = (f32[3,32,128]{2,1,0:T(8,128)S(1)}, f32[3,32,128]{2,1,0:T(8,128)S(1)}, u32[]{:S(2)}, u32[]{:S(2)}) collective-permute-start(f32[3,32,128]{2,1,0:T(8,128)S(1)} %pad_maximum_fusion), channel_id=1, source_target_pairs={{0,2},{1,3},{2,4},{3,5},{4,6},{5,7},{6,0},{7,1},{8,10},{9,11},{10,... | collective-permute-start | bytes 147464 | tf_op jit(solution)/shard_map/ppermute | solution.py:205
  16.6 18.9 %collective-permute-start.6 = (f32[3,32,128]{2,1,0:T(8,128)S(1)}, f32[3,32,128]{2,1,0:T(8,128)S(1)}, u32[]{:S(2)}, u32[]{:S(2)}) collective-permute-start(f32[3,32,128]{2,1,0:T(8,128)S(1)} %pad_maximum_fusion), channel_id=1, source_target_pairs={{0,3},{1,4},{2,5},{3,6},{4,7},{5,0},{6,1},{7,2},{8,11},{9,12},{10,... | collective-permute-start | bytes 147464 | tf_op jit(solution)/shard_map/ppermute | solution.py:205
  19.1 16.3 %collective-permute-start.7 = (f32[3,32,128]{2,1,0:T(8,128)S(1)}, f32[3,32,128]{2,1,0:T(8,128)S(1)}, u32[]{:S(2)}, u32[]{:S(2)}) collective-permute-start(f32[3,32,128]{2,1,0:T(8,128)S(1)} %pad_maximum_fusion), channel_id=1, source_target_pairs={{0,4},{1,5},{2,6},{3,7},{4,0},{5,1},{6,2},{7,3},{8,12},{9,13},{10,... | collective-permute-start | bytes 147464 | tf_op jit(solution)/shard_map/ppermute | solution.py:205
  20.4 18.6 %collective-permute-start.8 = (f32[3,32,128]{2,1,0:T(8,128)S(1)}, f32[3,32,128]{2,1,0:T(8,128)S(1)}, u32[]{:S(2)}, u32[]{:S(2)}) collective-permute-start(f32[3,32,128]{2,1,0:T(8,128)S(1)} %pad_maximum_fusion), channel_id=1, source_target_pairs={{0,5},{1,6},{2,7},{3,0},{4,1},{5,2},{6,3},{7,4},{8,13},{9,14},{10,... | collective-permute-start | bytes 147464 | tf_op jit(solution)/shard_map/ppermute | solution.py:205
  21.8 21.9 %copy-start.4 = (f32[32,128]{1,0:T(8,128)S(1)}, f32[32,128]{1,0:T(8,128)}, u32[]{:S(2)}) copy-start(f32[32,128]{1,0:T(8,128)} %get-tuple-element.53) | copy-start | bytes 49156
  22.2 20.2 %collective-permute-start.9 = (f32[3,32,128]{2,1,0:T(8,128)S(1)}, f32[3,32,128]{2,1,0:T(8,128)S(1)}, u32[]{:S(2)}, u32[]{:S(2)}) collective-permute-start(f32[3,32,128]{2,1,0:T(8,128)S(1)} %pad_maximum_fusion), channel_id=1, source_target_pairs={{0,6},{1,7},{2,0},{3,1},{4,2},{5,3},{6,4},{7,5},{8,14},{9,15},{10,... | collective-permute-start | bytes 147464 | tf_op jit(solution)/shard_map/ppermute | solution.py:205
  23.6 20.1 %collective-permute-start.10 = (f32[3,32,128]{2,1,0:T(8,128)S(1)}, f32[3,32,128]{2,1,0:T(8,128)S(1)}, u32[]{:S(2)}, u32[]{:S(2)}) collective-permute-start(f32[3,32,128]{2,1,0:T(8,128)S(1)} %pad_maximum_fusion), channel_id=1, source_target_pairs={{0,7},{1,0},{2,1},{3,2},{4,3},{5,4},{6,5},{7,6},{8,15},{9,8},{10,9... | collective-permute-start | bytes 147464 | tf_op jit(solution)/shard_map/ppermute | solution.py:205
  35.4 13.3 %collective-permute-start = (f32[60,8,128]{2,1,0:T(8,128)}, f32[60,8,128]{2,1,0:T(8,128)S(1)}, u32[]{:S(2)}, u32[]{:S(2)}) collective-permute-start(f32[60,8,128]{2,1,0:T(8,128)} %get-tuple-element.47), channel_id=1, source_target_pairs={{0,1},{1,2},{2,3},{3,4},{4,5},{5,6},{6,7},{7,0},{8,9},{9,10},{10,1... | collective-permute-start | bytes 737288 | tf_op jit(solution)/shard_map/ppermute | solution.py:183
  35.4 13.3 %collective-permute-start.1 = (f32[60,8,128]{2,1,0:T(8,128)}, f32[60,8,128]{2,1,0:T(8,128)S(1)}, u32[]{:S(2)}, u32[]{:S(2)}) collective-permute-start(f32[60,8,128]{2,1,0:T(8,128)} %get-tuple-element.48), channel_id=1, source_target_pairs={{1,0},{2,1},{3,2},{4,3},{5,4},{6,5},{7,6},{0,7},{9,8},{10,9},{11,1... | collective-permute-start | bytes 737288 | tf_op jit(solution)/shard_map/ppermute | solution.py:184
  39.0 5.6 %collective-permute-start.2 = (f32[15,8,128]{2,1,0:T(8,128)}, f32[15,8,128]{2,1,0:T(8,128)S(1)}, u32[]{:S(2)}, u32[]{:S(2)}) collective-permute-start(f32[15,8,128]{2,1,0:T(8,128)} %get-tuple-element.49), channel_id=1, source_target_pairs={{0,8},{8,16},{16,24},{1,9},{9,17},{17,25},{2,10},{10,18},{18,26},{... | collective-permute-start | bytes 184328 | tf_op jit(solution)/shard_map/ppermute | solution.py:181
  42.4 6.3 %collective-permute-start.3 = (f32[15,8,128]{2,1,0:T(8,128)}, f32[15,8,128]{2,1,0:T(8,128)S(1)}, u32[]{:S(2)}, u32[]{:S(2)}) collective-permute-start(f32[15,8,128]{2,1,0:T(8,128)} %get-tuple-element.50), channel_id=1, source_target_pairs={{8,0},{16,8},{24,16},{9,1},{17,9},{25,17},{10,2},{18,10},{26,18},{... | collective-permute-start | bytes 184328 | tf_op jit(solution)/shard_map/ppermute | solution.py:182
  44.5 4.2 %copy-start.5 = (f32[15,8,128]{2,1,0:T(8,128)}, f32[15,8,128]{2,1,0:T(8,128)S(1)}, u32[]{:S(2)}) copy-start(f32[15,8,128]{2,1,0:T(8,128)S(1)} %collective-permute-done.2.refs_11_) | copy-start | bytes 184324
  48.7 0.6 copy-start.6
  48.7 0.7 %copy-start.2 = (f32[60,8,128]{2,1,0:T(8,128)}, f32[60,8,128]{2,1,0:T(8,128)S(1)}, u32[]{:S(2)}) copy-start(f32[60,8,128]{2,1,0:T(8,128)S(1)} %collective-permute-done.refs_9_) | copy-start | bytes 737284
  48.7 0.8 %copy-start.3 = (f32[60,8,128]{2,1,0:T(8,128)}, f32[60,8,128]{2,1,0:T(8,128)S(1)}, u32[]{:S(2)}) copy-start(f32[60,8,128]{2,1,0:T(8,128)S(1)} %collective-permute-done.1.refs_10_) | copy-start | bytes 737284
  49.5 15.1 %copy-start.1 = (f32[32,32,128]{2,1,0:T(8,128)S(1)}, f32[32,32,128]{2,1,0:T(8,128)}, u32[]{:S(2)}) copy-start(f32[32,32,128]{2,1,0:T(8,128)} %get-tuple-element.54) | copy-start | bytes 1572868

commit v3 on v2

--- a/solution.py
+++ b/solution.py
@@ -17,41 +17,63 @@
 
 
 def pack_kernel(th_ref, xl_ref, xr_ref, zl_ref, zr_ref):
-    _, cz, w = th_ref.shape
+    ny, cz, w = th_ref.shape
+    nblocks = xl_ref.shape[0]
+    skip = ny - nblocks * LB
     lane8 = lax.broadcasted_iota(jnp.int32, (8, w), 1)
     sub8 = lax.broadcasted_iota(jnp.int32, (8, w), 0)
-    acc_l = jnp.zeros((8, w), jnp.float32)
-    acc_r = jnp.zeros((8, w), jnp.float32)
-    for s in range(LB):
-        for v in range(cz // 8):
-            t = th_ref[s, 8 * v:8 * v + 8, :]
-            pos = 4 * LB * v + 4 * s
-            pick = jnp.logical_and(lane8 >= pos, lane8 < pos + 4)
-            acc_l = jnp.where(pick, pltpu.roll(t, pos % w, 1), acc_l)
-            acc_r = jnp.where(pick, pltpu.roll(t, (pos + 4) % w, 1), acc_r)
-    xl_ref[0] = acc_l
-    xr_ref[0] = acc_r
-    for p in range(LB // 2):
-        a_hi = th_ref[2 * p, cz - 8:cz, :]
-        b_hi = th_ref[2 * p + 1, cz - 8:cz, :]
-        zl_ref[p] = jnp.where(sub8 < 4, pltpu.roll(a_hi, 4, 0), b_hi)
-        a_lo = th_ref[2 * p, 0:8, :]
-        b_lo = th_ref[2 * p + 1, 0:8, :]
-        zr_ref[p] = jnp.where(sub8 < 4, a_lo, pltpu.roll(b_lo, 4, 0))
+
+    def block(b, carry):
+        first = skip + b * LB
+        acc_l = jnp.zeros((8, w), jnp.float32)
+        acc_r = jnp.zeros((8, w), jnp.float32)
+        for s in range(LB):
+            for v in range(cz // 8):
+                t = th_ref[first + s, 8 * v:8 * v + 8, :]
+                pos = 4 * LB * v + 4 * s
+                pick = jnp.logical_and(lane8 >= pos, lane8 < pos + 4)
+                acc_l = jnp.where(pick, pltpu.roll(t, pos % w, 1), acc_l)
+                acc_r = jnp.where(pick, pltpu.roll(t, (pos + 4) % w, 1), acc_r)
+        xl_ref[b] = acc_l
+        xr_ref[b] = acc_r
+        for p in range(LB // 2):
+            a_hi = th_ref[first + 2 * p, cz - 8:cz, :]
+            b_hi = th_ref[first + 2 * p + 1, cz - 8:cz, :]
+            zl_ref[b * (LB // 2) + p] = jnp.where(sub8 < 4, pltpu.roll(a_hi, 4, 0), b_hi)
+            a_lo = th_ref[first + 2 * p, 0:8, :]
+            b_lo = th_ref[first + 2 * p + 1, 0:8, :]
+            zr_ref[b * (LB // 2) + p] = jnp.where(sub8 < 4, a_lo, pltpu.roll(b_lo, 4, 0))
+        return carry
+
+    lax.fori_loop(0, nblocks, block, 0)
 
 
 def layer_kernel(fluid, block_offset, *refs):
     if fluid:
-        (face_ref, th_ref, prev_ref, next_ref, st_ref, wall_ref, contact_ref,
+        (face_ref, wall_ref, contact_ref, th_ref, prev_ref, next_ref, st_ref,
          u_ref, v_ref, zb_ref, za_ref, xb_ref, xa_ref, _alias_ref,
-         sn_ref, tn_ref, ext_ref) = refs
+         sn_ref, tn_ref, wallv_ref, contv_ref, ext_ref) = refs
     else:
-        (face_ref, th_ref, prev_ref, next_ref, st_ref, wall_ref, contact_ref,
-         bs_ref, sn_ref, int_ref, head_ref) = refs
+        (face_ref, wall_ref, contact_ref, th_ref, prev_ref, next_ref, st_ref,
+         bs_ref, sn_ref, int_ref, mine_ref, wallv_ref, contv_ref) = refs
     _, cz, w = th_ref.shape
     base = (pl.program_id(0) + block_offset) * LB
-    wall = wall_ref[...]
-    contact = contact_ref[...]
+
+    @pl.when(pl.program_id(0) == 0)
+    def _():
+        sub = lax.broadcasted_iota(jnp.int32, (cz, w), 0)
+        acc = jnp.zeros((cz, w), jnp.int32)
+        for z in range(cz):
+            acc = jnp.where(sub == z, wall_ref[z], acc)
+        wallv_ref[...] = acc
+        lane = lax.broadcasted_iota(jnp.int32, (cz, w), 1)
+        cacc = jnp.zeros((cz, w), jnp.float32)
+        for x in range(w):
+            cacc = jnp.where(lane == x, contact_ref[x].astype(jnp.float32), cacc)
+        contv_ref[...] = cacc
+
+    wall = wallv_ref[...]
+    contact = contv_ref[...]
 
     def face(y):
         both_solid = face_ref[0, y + 1]
@@ -123,11 +145,13 @@
         if fluid:
             tn_ref[s] = adv
         else:
-            int_ref[s] = jnp.dot(bs_ref[s], adv, precision=lax.Precision.HIGHEST,
-                                 preferred_element_type=jnp.float32)
-            heads.append(adv[0:1, :])
+            inner = jnp.dot(bs_ref[s], adv, precision=lax.Precision.HIGHEST,
+                            preferred_element_type=jnp.float32)
+            int_ref[s] = inner
+            heads.append((adv[0:1, :], inner[1:2, :], inner[cz - 1:cz, :]))
     if not fluid:
-        head_ref[...] = jnp.concatenate(heads, axis=0)
+        for part in range(3):
+            mine_ref[part] = jnp.concatenate([h[part] for h in heads], axis=0)
 
 
 def local(theta, section_store, stream_speed, span_speed, conductivity, wall_layers,
@@ -141,8 +165,6 @@
     ngz = lax.axis_size("gz")
     ngx = lax.axis_size("gx")
 
-    wall2 = jnp.broadcast_to(wall_layers[:, None], (cz, w)).astype(jnp.int32)
-    contact2 = jnp.broadcast_to(contact.astype(f32)[None, :], (cz, w))
 
     solid_c = conductivity[0]
     fluid_c = conductivity[1]
@@ -161,15 +183,17 @@
     blk = lambda off: pl.BlockSpec((LB, cz, w), lambda i: (i + off, 0, 0))
     prev_spec = lambda off: pl.BlockSpec((1, cz, w), lambda i: (jnp.maximum((i + off) * LB - 1, 0), 0, 0))
     next_spec = lambda off: pl.BlockSpec((1, cz, w), lambda i: (jnp.minimum((i + off) * LB + LB, ny - 1), 0, 0))
-    full2 = pl.BlockSpec((cz, w), lambda i: (0, 0))
     edge_spec = pl.BlockSpec((1, 8, w), lambda i: (i, 0, 0))
     rows_spec = pl.BlockSpec((LB // 2, 8, w), lambda i: (i, 0, 0))
 
     xl, xr, zl, zr = pl.pallas_call(
         pack_kernel,
-        grid=(nfb,),
-        in_specs=[blk(nsb)],
-        out_specs=[edge_spec, edge_spec, rows_spec, rows_spec],
+        grid=(1,),
+        in_specs=[pl.BlockSpec((ny, cz, w), lambda i: (0, 0, 0))],
+        out_specs=[pl.BlockSpec((nfb, 8, w), lambda i: (0, 0, 0)),
+                   pl.BlockSpec((nfb, 8, w), lambda i: (0, 0, 0)),
+                   pl.BlockSpec((nf // 2, 8, w), lambda i: (0, 0, 0)),
+                   pl.BlockSpec((nf // 2, 8, w), lambda i: (0, 0, 0))],
         out_shape=[
             jax.ShapeDtypeStruct((nfb, 8, w), f32),
             jax.ShapeDtypeStruct((nfb, 8, w), f32),
@@ -183,23 +207,23 @@
     zb = lax.ppermute(zl, "gz", [(i, (i + 1) % ngz) for i in range(ngz)])
     za = lax.ppermute(zr, "gz", [((i + 1) % ngz, i) for i in range(ngz)])
 
-    shifted_inverse = jnp.zeros((ns, cz, cz), f32).at[:, 1:, 1:].set(block_inverse)
-
-    sn_part, interior, head = pl.pallas_call(
+    shifted_inverse = jnp.pad(block_inverse, ((0, 0), (1, 0), (1, 0)))
+
+    sn_part, interior, mine = pl.pallas_call(
         lambda *refs: layer_kernel(False, 0, *refs),
         grid=(nsb,),
-        in_specs=[smem, blk(0), prev_spec(0), next_spec(0), blk(0), full2, full2,
+        in_specs=[smem, smem, smem, blk(0), prev_spec(0), next_spec(0), blk(0),
                   pl.BlockSpec((LB, cz, cz), lambda i: (i, 0, 0))],
-        out_specs=[blk(0), blk(0), pl.BlockSpec((LB, w), lambda i: (i, 0))],
+        out_specs=[blk(0), blk(0), pl.BlockSpec((3, LB, w), lambda i: (0, i, 0))],
         out_shape=[
             jax.ShapeDtypeStruct((ny, cz, w), f32),
             jax.ShapeDtypeStruct((ns, cz, w), f32),
-            jax.ShapeDtypeStruct((ns, w), f32),
+            jax.ShapeDtypeStruct((3, ns, w), f32),
         ],
-    )(faces, theta, theta, theta, section_store, wall2, contact2, shifted_inverse)
+        scratch_shapes=[pltpu.VMEM((cz, w), jnp.int32), pltpu.VMEM((cz, w), f32)],
+    )(faces, wall_layers, contact, theta, theta, theta, section_store, shifted_inverse)
 
     number = spanwise_number
-    mine = jnp.stack([head, interior[:, 1, :], interior[:, cz - 1, :]])
     gathered = [mine]
     for d in range(1, ngz):
         gathered.append(lax.ppermute(mine, "gz", [(i, (i + d) % ngz) for i in range(ngz)]))
@@ -222,7 +246,7 @@
     fluid_sn, fluid_tn = pl.pallas_call(
         lambda *refs: layer_kernel(True, nsb, *refs),
         grid=(nfb,),
-        in_specs=[smem, blk(nsb), prev_spec(nsb), next_spec(nsb), blk(nsb), full2, full2,
+        in_specs=[smem, smem, smem, blk(nsb), prev_spec(nsb), next_spec(nsb), blk(nsb),
                   blk(nsb), blk(nsb), rows_spec, rows_spec, edge_spec, edge_spec,
                   pl.BlockSpec(memory_space=pl.ANY)],
         out_specs=[blk(nsb), blk(nsb)],
@@ -230,9 +254,10 @@
             jax.ShapeDtypeStruct((ny, cz, w), f32),
             jax.ShapeDtypeStruct((ny, cz, w), f32),
         ],
-        scratch_shapes=[pltpu.VMEM((cz + 16, w), f32)],
+        scratch_shapes=[pltpu.VMEM((cz, w), jnp.int32), pltpu.VMEM((cz, w), f32),
+                        pltpu.VMEM((cz + 16, w), f32)],
         input_output_aliases={13: 0},
-    )(faces, theta, theta, theta, section_store, wall2, contact2,
+    )(faces, wall_layers, contact, theta, theta, theta, section_store,
       stream_speed, span_speed, zb, za, xb, xa, sn_part)
 
     row = jnp.arange(cz, dtype=jnp.int32)

time: 66.8 us -> 57.6 us (0.86)
  Pallas kernels: 28.7 us -> 23.9 us
  local copies, waits for them, and re-layouts: 8.53 us -> 5.23 us
  other arithmetic: 4.01 us -> 2.63 us
    pallas_call x1, Pallas kernels: 9.36 us -> 4.45 us  [local(): pl.pallas_call(pack_kernel, grid=(1,), in_specs=[pl.BlockSpec((ny, cz, w)...]
    broadcast_in_dim x2 -> x0, local copies, waits for them, and re-layouts: 1.93 us -> none  [the longest x1 1.32 us: local(): wall2 = jnp.broadcast_to(wall_layers[:, None], (cz, w)).astype(jnp.int32)]
    pallas_call x1 -> x0, local copies, waits for them, and re-layouts: 1.36 us -> none  [local(): pl.pallas_call(lambda *refs: layer_kernel(False, 0, *refs), grid=(nsb,),...]
    pad x0 -> x1, local copies, waits for them, and re-layouts: none -> 1 us  [local(): shifted_inverse = jnp.pad(block_inverse, ((0, 0), (1, 0), (1, 0)))]
    scatter x1 -> x0, local copies, waits for them, and re-layouts: 1 us -> none  [local(): jnp.zeros((ns, cz, cz), f32).at[:, 1:, 1:].set(block_inverse)]
    another operation x1 -> x0, other arithmetic: 0.72 us -> none  [local(): mine = jnp.stack([head, interior[:, 1, :], interior[:, cz - 1, :]])]
  transfers between devices with their start and end apart: 11 -> 11, of which waited for: 2 -> 3; matrix products, arithmetic and copies ran while one was open for 3% -> 3% of each run, Pallas kernels for 14% -> 8%
where the time goes in v3:
time: 57.6 us; the launch traced here: 56.9 us
  Pallas kernels  23.9 us (41%)
  starting transfers between devices  19 us (33%)
  waiting for transfers between devices  5.42 us (9%)
  local copies, waits for them, and re-layouts  5.23 us (9%)
  other arithmetic  2.63 us (5%)
  between operations  0.8 us (1%)
    pallas_call x1, Pallas kernels, local(): pl.pallas_call(lambda *refs: layer_kernel(True, nsb, *refs), grid=(nfb,),...  15.2 us
    ppermute x7, starting transfers between devices, local(): lax.ppermute(mine, 'gz', [(i, (i + d) % ngz) for i in range(ngz)])  10.7 us
    pallas_call x1, Pallas kernels, local(): pl.pallas_call(pack_kernel, grid=(1,), in_specs=[pl.BlockSpec((ny, cz, w)...  4.45 us
    pallas_call x1, Pallas kernels, local(): pl.pallas_call(lambda *refs: layer_kernel(False, 0, *refs), grid=(nsb,),...  4.23 us
    ppermute x1, waiting for transfers between devices, local(): xa = lax.ppermute(xl, 'gx', [(i + 1, i) for i in range(ngx - 1)])  4.17 us
    ppermute x1, starting transfers between devices, local(): za = lax.ppermute(zr, 'gz', [((i + 1) % ngz, i) for i in range(ngz)])  3.5 us
    ppermute x1, starting transfers between devices, local(): xb = lax.ppermute(xr, 'gx', [(i, i + 1) for i in range(ngx - 1)])  3.4 us
    unnamed x19, local copies, waits for them, and re-layouts  2.96 us
  transfers between devices with their start and end apart: 11, of which 3 were waited for; matrix products, arithmetic and copies ran while one was open for 3% of the time, Pallas kernels for 8%

profile of v3, /device:TPU:0, one launch (start us, length us, event | category | flops | bytes accessed | tf_op | source)
XLA Modules:
  0.0 56.9 jit_solution(9660942148977629174)
XLA Ops:
  0.6 0.9 %fusion.46 = (f32[1,151]{1,0:T(1,128)S(1)}, f32[1,151]{1,0:T(1,128)S(1)}, f32[1,151]{1,0:T(1,128)S(1)}, f32[1,151]{1,0:T(1,128)S(1)}) fusion(f32[2,152]{1,0:T(2,128)} %param.17), kind=kLoop, calls=%fused_computation.94 | loop fusion | bytes 4832 | tf_op jit(solution)/shard_map/slice | solution.py:177
  1.5 1.3 %copy.18 = f32[32,31,31]{2,1,0:T(8,128)S(1)} copy(f32[32,31,31]{2,0,1:T(8,128)} %param.21) | data formatting | bytes 246016 | tf_op args[8]
  3.0 1.0 %pad.10.refs_7_ = f32[32,32,32]{2,1,0:T(8,128)} pad(f32[32,31,31]{2,1,0:T(8,128)S(1)} %copy.18, f32[]{:T(128)} %constant.77.clone.1), padding=0_0x1_0x1_0 | pad | bytes 254084 | tf_op jit(solution)/shard_map/jit(_pad)/pad | solution.py:210
  4.0 0.6 %pad_maximum_fusion.refs_0_ = f32[3,153]{1,0:T(4,128)} fusion(f32[1,153]{1,0:T(1,128)S(1)} %bitcast.190, f32[1,153]{1,0:T(1,128)S(1)} %bitcast.191, f32[1,153]{1,0:T(1,128)S(1)} %bitcast.189), kind=kLoop, calls=%fused_computation.66 | loop fusion | flops 918 | bytes 3672 | tf_op jit(solution)/shard_map/stack | solution.py:176
  4.6 4.2 %shard_map.105 = (f32[152,32,128]{2,1,0:T(8,128)}, f32[32,32,128]{2,1,0:T(8,128)}, f32[3,32,128]{2,1,0:T(8,128)}) custom-call(f32[3,153]{1,0:T(4,128)} %pad_maximum_fusion.refs_0_, s32[32]{0:T(128)} %refs_1_.3, s32[128]{0:T(128)} %refs_2_.3, f32[152,32,128]{2,1,0:T(8,128)} %refs_5_.3, f32[152,32,128]{2,1,0:T(8,128)} %refs_5_.3, f32[152,32,128]{2,1,0:T(8,128)} %refs_5_.3, ...), custom_call_target="tpu_custom_call" | custom-call | tf_op jit(solution)/shard_map/pallas_call | solution.py:212
  8.9 4.5 %collective-permute-start.10 = (f32[3,32,128]{2,1,0:T(8,128)}, f32[3,32,128]{2,1,0:T(8,128)S(1)}, u32[]{:S(2)}, u32[]{:S(2)}) collective-permute-start(f32[3,32,128]{2,1,0:T(8,128)} %get-tuple-element.41), channel_id=1, source_target_pairs={{0,7},{1,0},{2,1},{3,2},{4,3},{5,4},{6,5},{7,6},{8,15},{9,8},{10,9... | collective-permute-start | bytes 147464 | tf_op jit(solution)/shard_map/ppermute | solution.py:229
  13.4 1.2 %collective-permute-start.6 = (f32[3,32,128]{2,1,0:T(8,128)}, f32[3,32,128]{2,1,0:T(8,128)S(1)}, u32[]{:S(2)}, u32[]{:S(2)}) collective-permute-start(f32[3,32,128]{2,1,0:T(8,128)} %get-tuple-element.41), channel_id=1, source_target_pairs={{0,3},{1,4},{2,5},{3,6},{4,7},{5,0},{6,1},{7,2},{8,11},{9,12},{10,... | collective-permute-start | bytes 147464 | tf_op jit(solution)/shard_map/ppermute | solution.py:229
  14.6 2.9 %collective-permute-start.7 = (f32[3,32,128]{2,1,0:T(8,128)}, f32[3,32,128]{2,1,0:T(8,128)S(1)}, u32[]{:S(2)}, u32[]{:S(2)}) collective-permute-start(f32[3,32,128]{2,1,0:T(8,128)} %get-tuple-element.41), channel_id=1, source_target_pairs={{0,4},{1,5},{2,6},{3,7},{4,0},{5,1},{6,2},{7,3},{8,12},{9,13},{10,... | collective-permute-start | bytes 147464 | tf_op jit(solution)/shard_map/ppermute | solution.py:229
  17.5 0.2 add_reduce_fusion
  17.8 0.2 fusion.45
  18.3 0.6 %collective-permute-done.4 = f32[3,32,128]{2,1,0:T(8,128)S(1)} collective-permute-done((f32[3,32,128]{2,1,0:T(8,128)}, f32[3,32,128]{2,1,0:T(8,128)S(1)}, u32[]{:S(2)}, u32[]{:S(2)}) %collective-permute-start.4) | collective-permute-done | bytes 49184 | tf_op jit(solution)/shard_map/ppermute | solution.py:229
  18.9 2.1 %collective-permute-start.9 = (f32[3,32,128]{2,1,0:T(8,128)}, f32[3,32,128]{2,1,0:T(8,128)S(1)}, u32[]{:S(2)}, u32[]{:S(2)}) collective-permute-start(f32[3,32,128]{2,1,0:T(8,128)} %get-tuple-element.41), channel_id=1, source_target_pairs={{0,6},{1,7},{2,0},{3,1},{4,2},{5,3},{6,4},{7,5},{8,14},{9,15},{10,... | collective-permute-start | bytes 147464 | tf_op jit(solution)/shard_map/ppermute | solution.py:229
  21.0 4.5 %shard_map.104 = (f32[15,8,128]{2,1,0:T(8,128)}, f32[15,8,128]{2,1,0:T(8,128)}, f32[60,8,128]{2,1,0:T(8,128)}, f32[60,8,128]{2,1,0:T(8,128)}) custom-call(f32[152,32,128]{2,1,0:T(8,128)} %refs_5_.3), custom_call_target="tpu_custom_call" | custom-call | tf_op jit(solution)/shard_map/pallas_call | solution.py:189
  25.4 0.4 copy.21
  25.9 0.4 copy.22
  26.5 3.5 %collective-permute-start.1 = (f32[60,8,128]{2,1,0:T(8,128)}, f32[60,8,128]{2,1,0:T(8,128)S(1)}, u32[]{:S(2)}, u32[]{:S(2)}) collective-permute-start(f32[60,8,128]{2,1,0:T(8,128)} %get-tuple-element.36), channel_id=1, source_target_pairs={{1,0},{2,1},{3,2},{4,3},{5,4},{6,5},{7,6},{0,7},{9,8},{10,9},{11,1... | collective-permute-start | bytes 737288 | tf_op jit(solution)/shard_map/ppermute | solution.py:208
  30.0 3.4 %collective-permute-start.2 = (f32[15,8,128]{2,1,0:T(8,128)}, f32[15,8,128]{2,1,0:T(8,128)S(1)}, u32[]{:S(2)}, u32[]{:S(2)}) collective-permute-start(f32[15,8,128]{2,1,0:T(8,128)} %get-tuple-element.37), channel_id=1, source_target_pairs={{0,8},{8,16},{16,24},{1,9},{9,17},{17,25},{2,10},{10,18},{18,26},{... | collective-permute-start | bytes 184328 | tf_op jit(solution)/shard_map/ppermute | solution.py:205
  33.4 1.3 %collective-permute-start.3 = (f32[15,8,128]{2,1,0:T(8,128)}, f32[15,8,128]{2,1,0:T(8,128)S(1)}, u32[]{:S(2)}, u32[]{:S(2)}) collective-permute-start(f32[15,8,128]{2,1,0:T(8,128)} %get-tuple-element.38), channel_id=1, source_target_pairs={{8,0},{16,8},{24,16},{9,1},{17,9},{25,17},{10,2},{18,10},{26,18},{... | collective-permute-start | bytes 184328 | tf_op jit(solution)/shard_map/ppermute | solution.py:206
  34.7 0.1 multiply_add_fusion.1
  34.9 0.6 %collective-permute-done.2.refs_11_ = f32[15,8,128]{2,1,0:T(8,128)S(1)} collective-permute-done((f32[15,8,128]{2,1,0:T(8,128)}, f32[15,8,128]{2,1,0:T(8,128)S(1)}, u32[]{:S(2)}, u32[]{:S(2)}) %collective-permute-start.2) | collective-permute-done | bytes 61472 | tf_op jit(solution)/shard_map/ppermute | solution.py:205
  35.6 4.2 %collective-permute-done.3.refs_12_ = f32[15,8,128]{2,1,0:T(8,128)S(1)} collective-permute-done((f32[15,8,128]{2,1,0:T(8,128)}, f32[15,8,128]{2,1,0:T(8,128)S(1)}, u32[]{:S(2)}, u32[]{:S(2)}) %collective-permute-start.3) | collective-permute-done | bytes 61472 | tf_op jit(solution)/shard_map/ppermute | solution.py:206
  39.8 0.6 %copy-done.5 = f32[15,8,128]{2,1,0:T(8,128)} copy-done((f32[15,8,128]{2,1,0:T(8,128)}, f32[15,8,128]{2,1,0:T(8,128)S(1)}, u32[]{:S(2)}) %copy-start.5) | copy-done | bytes 61464
  40.5 15.2 %shard_map.106 = (f32[152,32,128]{2,1,0:T(8,128)}, f32[152,32,128]{2,1,0:T(8,128)}) custom-call(f32[3,153]{1,0:T(4,128)} %pad_maximum_fusion.refs_0_, s32[32]{0:T(128)} %refs_1_.3, s32[128]{0:T(128)} %refs_2_.3, f32[152,32,128]{2,1,0:T(8,128)} %refs_5_.3, f32[152,32,128]{2,1,0:T(8,128)} %refs_5_.3, ...), custom_call_target="tpu_custom_call", output_to_operand_aliasing={{0}: (13, {})} | custom-call | tf_op jit(solution)/shard_map/pallas_call | solution.py:246
  55.7 1.2 %select_dynamic-update-slice_fusion = f32[152,32,128]{2,1,0:T(8,128)} fusion(f32[152,32,128]{2,1,0:T(8,128)} %get-tuple-element.40, f32[32,32,128]{2,1,0:T(8,128)S(1)} %copy-done.1, f32[32,128]{1,0:T(8,128)S(1)} %multiply_add_fusion, f32[32,32]{1,0:T(8,128)S(1)} %scatter.9, f32[32,32]{1,0:T(8,128)S(1)} %scatter.6, f32[32]{0:T(128)S(1)} %copy-done.7, ...), kind=kLoop, calls=%fused_computation | loop fusion | flops 786432 | bytes 1089696 | tf_op jit(solution)/shard_map/dynamic_update_slice | solution.py:270
  (41 shorter events, 1.0 us)
Async XLA Ops:
  4.6 12.9 %copy-start = (f32[32,31,31]{2,0,1:T(8,128)S(1)}, f32[32,31,31]{2,0,1:T(8,128)}, u32[]{:S(2)}) copy-start(f32[32,31,31]{2,0,1:T(8,128)} %param.21) | copy-start | bytes 369028
  4.6 13.4 %copy-start.7 = (f32[32]{0:T(128)S(1)}, f32[32]{0:T(128)}, u32[]{:S(2)}) copy-start(f32[32]{0:T(128)} %param.20) | copy-start | bytes 388
  8.9 9.3 %collective-permute-start.10 = (f32[3,32,128]{2,1,0:T(8,128)}, f32[3,32,128]{2,1,0:T(8,128)S(1)}, u32[]{:S(2)}, u32[]{:S(2)}) collective-permute-start(f32[3,32,128]{2,1,0:T(8,128)} %get-tuple-element.41), channel_id=1, source_target_pairs={{0,7},{1,0},{2,1},{3,2},{4,3},{5,4},{6,5},{7,6},{8,15},{9,8},{10,9... | collective-permute-start | bytes 147464 | tf_op jit(solution)/shard_map/ppermute | solution.py:229
  13.4 5.5 %collective-permute-start.4 = (f32[3,32,128]{2,1,0:T(8,128)}, f32[3,32,128]{2,1,0:T(8,128)S(1)}, u32[]{:S(2)}, u32[]{:S(2)}) collective-permute-start(f32[3,32,128]{2,1,0:T(8,128)} %get-tuple-element.41), channel_id=1, source_target_pairs={{0,1},{1,2},{2,3},{3,4},{4,5},{5,6},{6,7},{7,0},{8,9},{9,10},{10,1... | collective-permute-start | bytes 147464 | tf_op jit(solution)/shard_map/ppermute | solution.py:229
  13.4 13.0 %collective-permute-start.5 = (f32[3,32,128]{2,1,0:T(8,128)}, f32[3,32,128]{2,1,0:T(8,128)S(1)}, u32[]{:S(2)}, u32[]{:S(2)}) collective-permute-start(f32[3,32,128]{2,1,0:T(8,128)} %get-tuple-element.41), channel_id=1, source_target_pairs={{0,2},{1,3},{2,4},{3,5},{4,6},{5,7},{6,0},{7,1},{8,10},{9,11},{10,... | collective-permute-start | bytes 147464 | tf_op jit(solution)/shard_map/ppermute | solution.py:229
  13.4 13.1 %collective-permute-start.6 = (f32[3,32,128]{2,1,0:T(8,128)}, f32[3,32,128]{2,1,0:T(8,128)S(1)}, u32[]{:S(2)}, u32[]{:S(2)}) collective-permute-start(f32[3,32,128]{2,1,0:T(8,128)} %get-tuple-element.41), channel_id=1, source_target_pairs={{0,3},{1,4},{2,5},{3,6},{4,7},{5,0},{6,1},{7,2},{8,11},{9,12},{10,... | collective-permute-start | bytes 147464 | tf_op jit(solution)/shard_map/ppermute | solution.py:229
  14.6 15.4 %collective-permute-start.7 = (f32[3,32,128]{2,1,0:T(8,128)}, f32[3,32,128]{2,1,0:T(8,128)S(1)}, u32[]{:S(2)}, u32[]{:S(2)}) collective-permute-start(f32[3,32,128]{2,1,0:T(8,128)} %get-tuple-element.41), channel_id=1, source_target_pairs={{0,4},{1,5},{2,6},{3,7},{4,0},{5,1},{6,2},{7,3},{8,12},{9,13},{10,... | collective-permute-start | bytes 147464 | tf_op jit(solution)/shard_map/ppermute | solution.py:229
  17.8 16.9 %copy-start.6 = (f32[3,32,128]{2,1,0:T(8,128)S(1)}, f32[3,32,128]{2,1,0:T(8,128)}, u32[]{:S(2)}) copy-start(f32[3,32,128]{2,1,0:T(8,128)} %get-tuple-element.41) | copy-start | bytes 147460
  18.2 15.2 %collective-permute-start.8 = (f32[3,32,128]{2,1,0:T(8,128)}, f32[3,32,128]{2,1,0:T(8,128)S(1)}, u32[]{:S(2)}, u32[]{:S(2)}) collective-permute-start(f32[3,32,128]{2,1,0:T(8,128)} %get-tuple-element.41), channel_id=1, source_target_pairs={{0,5},{1,6},{2,7},{3,0},{4,1},{5,2},{6,3},{7,4},{8,13},{9,14},{10,... | collective-permute-start | bytes 147464 | tf_op jit(solution)/shard_map/ppermute | solution.py:229
  18.9 15.8 %collective-permute-start.9 = (f32[3,32,128]{2,1,0:T(8,128)}, f32[3,32,128]{2,1,0:T(8,128)S(1)}, u32[]{:S(2)}, u32[]{:S(2)}) collective-permute-start(f32[3,32,128]{2,1,0:T(8,128)} %get-tuple-element.41), channel_id=1, source_target_pairs={{0,6},{1,7},{2,0},{3,1},{4,2},{5,3},{6,4},{7,5},{8,14},{9,15},{10,... | collective-permute-start | bytes 147464 | tf_op jit(solution)/shard_map/ppermute | solution.py:229
  26.4 13.3 %collective-permute-start = (f32[60,8,128]{2,1,0:T(8,128)}, f32[60,8,128]{2,1,0:T(8,128)S(1)}, u32[]{:S(2)}, u32[]{:S(2)}) collective-permute-start(f32[60,8,128]{2,1,0:T(8,128)} %get-tuple-element.35), channel_id=1, source_target_pairs={{0,1},{1,2},{2,3},{3,4},{4,5},{5,6},{6,7},{7,0},{8,9},{9,10},{10,1... | collective-permute-start | bytes 737288 | tf_op jit(solution)/shard_map/ppermute | solution.py:207
  26.5 13.2 %collective-permute-start.1 = (f32[60,8,128]{2,1,0:T(8,128)}, f32[60,8,128]{2,1,0:T(8,128)S(1)}, u32[]{:S(2)}, u32[]{:S(2)}) collective-permute-start(f32[60,8,128]{2,1,0:T(8,128)} %get-tuple-element.36), channel_id=1, source_target_pairs={{1,0},{2,1},{3,2},{4,3},{5,4},{6,5},{7,6},{0,7},{9,8},{10,9},{11,1... | collective-permute-start | bytes 737288 | tf_op jit(solution)/shard_map/ppermute | solution.py:208
  30.0 5.6 %collective-permute-start.2 = (f32[15,8,128]{2,1,0:T(8,128)}, f32[15,8,128]{2,1,0:T(8,128)S(1)}, u32[]{:S(2)}, u32[]{:S(2)}) collective-permute-start(f32[15,8,128]{2,1,0:T(8,128)} %get-tuple-element.37), channel_id=1, source_target_pairs={{0,8},{8,16},{16,24},{1,9},{9,17},{17,25},{2,10},{10,18},{18,26},{... | collective-permute-start | bytes 184328 | tf_op jit(solution)/shard_map/ppermute | solution.py:205
  33.4 6.3 %collective-permute-start.3 = (f32[15,8,128]{2,1,0:T(8,128)}, f32[15,8,128]{2,1,0:T(8,128)S(1)}, u32[]{:S(2)}, u32[]{:S(2)}) collective-permute-start(f32[15,8,128]{2,1,0:T(8,128)} %get-tuple-element.38), channel_id=1, source_target_pairs={{8,0},{16,8},{24,16},{9,1},{17,9},{25,17},{10,2},{18,10},{26,18},{... | collective-permute-start | bytes 184328 | tf_op jit(solution)/shard_map/ppermute | solution.py:206
  35.5 4.2 %copy-start.4 = (f32[15,8,128]{2,1,0:T(8,128)}, f32[15,8,128]{2,1,0:T(8,128)S(1)}, u32[]{:S(2)}) copy-start(f32[15,8,128]{2,1,0:T(8,128)S(1)} %collective-permute-done.2.refs_11_) | copy-start | bytes 184324
  39.7 0.6 %copy-start.5 = (f32[15,8,128]{2,1,0:T(8,128)}, f32[15,8,128]{2,1,0:T(8,128)S(1)}, u32[]{:S(2)}) copy-start(f32[15,8,128]{2,1,0:T(8,128)S(1)} %collective-permute-done.3.refs_12_) | copy-start | bytes 184324
  39.7 0.7 %copy-start.2 = (f32[60,8,128]{2,1,0:T(8,128)}, f32[60,8,128]{2,1,0:T(8,128)S(1)}, u32[]{:S(2)}) copy-start(f32[60,8,128]{2,1,0:T(8,128)S(1)} %collective-permute-done.refs_9_) | copy-start | bytes 737284
  39.7 0.8 %copy-start.3 = (f32[60,8,128]{2,1,0:T(8,128)}, f32[60,8,128]{2,1,0:T(8,128)S(1)}, u32[]{:S(2)}) copy-start(f32[60,8,128]{2,1,0:T(8,128)S(1)} %collective-permute-done.1.refs_10_) | copy-start | bytes 737284
  40.5 15.2 %copy-start.1 = (f32[32,32,128]{2,1,0:T(8,128)S(1)}, f32[32,32,128]{2,1,0:T(8,128)}, u32[]{:S(2)}) copy-start(f32[32,32,128]{2,1,0:T(8,128)} %get-tuple-element.42) | copy-start | bytes 1572868

commit v4 on v3

--- a/solution.py
+++ b/solution.py
@@ -55,7 +55,7 @@
          sn_ref, tn_ref, wallv_ref, contv_ref, ext_ref) = refs
     else:
         (face_ref, wall_ref, contact_ref, th_ref, prev_ref, next_ref, st_ref,
-         bs_ref, sn_ref, int_ref, mine_ref, wallv_ref, contv_ref) = refs
+         bs_ref, _order_ref, sn_ref, int_ref, mine_ref, wallv_ref, contv_ref) = refs
     _, cz, w = th_ref.shape
     base = (pl.program_id(0) + block_offset) * LB
 
@@ -213,7 +213,8 @@
         lambda *refs: layer_kernel(False, 0, *refs),
         grid=(nsb,),
         in_specs=[smem, smem, smem, blk(0), prev_spec(0), next_spec(0), blk(0),
-                  pl.BlockSpec((LB, cz, cz), lambda i: (i, 0, 0))],
+                  pl.BlockSpec((LB, cz, cz), lambda i: (i, 0, 0)),
+                  pl.BlockSpec(memory_space=pl.ANY)],
         out_specs=[blk(0), blk(0), pl.BlockSpec((3, LB, w), lambda i: (0, i, 0))],
         out_shape=[
             jax.ShapeDtypeStruct((ny, cz, w), f32),
@@ -221,16 +222,13 @@
             jax.ShapeDtypeStruct((3, ns, w), f32),
         ],
         scratch_shapes=[pltpu.VMEM((cz, w), jnp.int32), pltpu.VMEM((cz, w), f32)],
-    )(faces, wall_layers, contact, theta, theta, theta, section_store, shifted_inverse)
+    )(faces, wall_layers, contact, theta, theta, theta, section_store, shifted_inverse, zr)
 
     number = spanwise_number
-    gathered = [mine]
-    for d in range(1, ngz):
-        gathered.append(lax.ppermute(mine, "gz", [(i, (i + d) % ngz) for i in range(ngz)]))
-    targets = []
-    for d in range(ngz):
-        left = gathered[(d + 1) % ngz][2]
-        targets.append(gathered[d][0] + number[:, None] * left + number[:, None] * gathered[d][1])
+    spread = jnp.broadcast_to(mine[None], (ngz,) + mine.shape)
+    blocks = lax.all_to_all(spread, "gz", 0, 0, tiled=True)
+    left = jnp.roll(blocks[:, 2], 1, axis=0)
+    targets = blocks[:, 0] + number[None, :, None] * left + number[None, :, None] * blocks[:, 1]
 
     square = number * number
     diagonal = 1.0 + 2.0 * number - square * (block_inverse[:, 0, 0] + block_inverse[:, -1, -1])
@@ -238,10 +236,15 @@
     q = jnp.arange(ngz, dtype=jnp.int32)
     angle = (2.0 * math.pi / ngz) * q.astype(f32)
     denominator = diagonal[:, None] - 2.0 * beside[:, None] * jnp.cos(angle)[None, :]
-    phase = (2.0 * math.pi / ngz) * ((q[:, None] * q[None, :]) % ngz).astype(f32)
-    coeff = jnp.sum(jnp.cos(phase)[None, :, :] / denominator[:, :, None], axis=1) / ngz
-    head_values = sum(coeff[:, (-d) % ngz, None] * targets[d] for d in range(ngz))
-    following = sum(coeff[:, (-d - 1) % ngz, None] * targets[d] for d in range(ngz))
+    k = lax.axis_index("gz")
+
+    def weights(shift):
+        m = (q - shift) % ngz
+        phase = (2.0 * math.pi / ngz) * ((q[:, None] * m[None, :]) % ngz).astype(f32)
+        return jnp.sum(jnp.cos(phase)[None, :, :] / denominator[:, :, None], axis=1) / ngz
+
+    head_values = jnp.sum(weights(k).T[:, :, None] * targets, axis=0)
+    following = jnp.sum(weights(k + 1).T[:, :, None] * targets, axis=0)
 
     fluid_sn, fluid_tn = pl.pallas_call(
         lambda *refs: layer_kernel(True, nsb, *refs),

time: 57.6 us -> 53.2 us (0.924)
  starting transfers between devices: 19 us -> 13 us
  waiting for transfers between devices: 5.42 us -> 7.11 us
    ppermute x7 -> x0, starting transfers between devices: 10.7 us -> none  [local(): lax.ppermute(mine, 'gz', [(i, (i + d) % ngz) for i in range(ngz)])]
    ppermute x1, waiting for transfers between devices: 0.01 us -> 3.74 us  [local(): zb = lax.ppermute(zl, 'gz', [(i, (i + 1) % ngz) for i in range(ngz)])]
    all_to_all x0 -> x1, starting transfers between devices: none -> 3.45 us  [local(): blocks = lax.all_to_all(spread, 'gz', 0, 0, tiled=True)]
    broadcast_in_dim x0 -> x1, local copies, waits for them, and re-layouts: none -> 1.59 us  [local(): spread = jnp.broadcast_to(mine[None], (ngz,) + mine.shape)]
    unnamed x19 -> x25, local copies, waits for them, and re-layouts: 2.96 us -> 1.87 us
    ppermute x1, starting transfers between devices: 3.5 us -> 4.49 us  [local(): za = lax.ppermute(zr, 'gz', [((i + 1) % ngz, i) for i in range(ngz)])]
    slice x1, local copies, waits for them, and re-layouts: 0.9 us -> 0.07 us  [local(): solid_c[1:]]
    ppermute x1, waiting for transfers between devices: 4.17 us -> 3.36 us  [local(): xa = lax.ppermute(xl, 'gx', [(i + 1, i) for i in range(ngx - 1)])]
  transfers between devices with their start and end apart: 11 -> 5, of which waited for: 3 -> 2; matrix products, arithmetic and copies ran while one was open for 3% -> 10% of each run, Pallas kernels for 8% -> 37%
where the time goes in v4:
time: 53.2 us; the launch traced here: 52.4 us
  Pallas kernels  23.9 us (45%)
  starting transfers between devices  13 us (24%)
  waiting for transfers between devices  7.11 us (13%)
  local copies, waits for them, and re-layouts  4.9 us (9%)
  other arithmetic  2.62 us (5%)
  between operations  0.84 us (2%)
    pallas_call x1, Pallas kernels, local(): pl.pallas_call(lambda *refs: layer_kernel(True, nsb, *refs), grid=(nfb,),...  15.2 us
    pallas_call x1, Pallas kernels, local(): pl.pallas_call(pack_kernel, grid=(1,), in_specs=[pl.BlockSpec((ny, cz, w)...  4.53 us
    ppermute x1, starting transfers between devices, local(): za = lax.ppermute(zr, 'gz', [((i + 1) % ngz, i) for i in range(ngz)])  4.49 us
    pallas_call x1, Pallas kernels, local(): pl.pallas_call(lambda *refs: layer_kernel(False, 0, *refs), grid=(nsb,),...  4.22 us
    ppermute x1, waiting for transfers between devices, local(): zb = lax.ppermute(zl, 'gz', [(i, (i + 1) % ngz) for i in range(ngz)])  3.74 us
    all_to_all x1, starting transfers between devices, local(): blocks = lax.all_to_all(spread, 'gz', 0, 0, tiled=True)  3.45 us
    ppermute x1, starting transfers between devices, local(): xb = lax.ppermute(xr, 'gx', [(i, i + 1) for i in range(ngx - 1)])  3.39 us
    ppermute x1, waiting for transfers between devices, local(): xa = lax.ppermute(xl, 'gx', [(i + 1, i) for i in range(ngx - 1)])  3.36 us
  transfers between devices with their start and end apart: 5, of which 2 were waited for; matrix products, arithmetic and copies ran while one was open for 10% of the time, Pallas kernels for 37%

profile of v4, /device:TPU:0, one launch (start us, length us, event | category | flops | bytes accessed | tf_op | source)
XLA Modules:
  0.0 52.4 jit_solution(2432130448929760163)
XLA Ops:
  0.6 4.5 %shard_map.104 = (f32[15,8,128]{2,1,0:T(8,128)}, f32[15,8,128]{2,1,0:T(8,128)}, f32[60,8,128]{2,1,0:T(8,128)}, f32[60,8,128]{2,1,0:T(8,128)}) custom-call(f32[152,32,128]{2,1,0:T(8,128)} %refs_5_.3), custom_call_target="tpu_custom_call" | custom-call | tf_op jit(solution)/shard_map/pallas_call | solution.py:189
  5.2 4.5 %collective-permute-start.1 = (f32[60,8,128]{2,1,0:T(8,128)}, f32[60,8,128]{2,1,0:T(8,128)S(1)}, u32[]{:S(2)}, u32[]{:S(2)}) collective-permute-start(f32[60,8,128]{2,1,0:T(8,128)} %get-tuple-element.36.refs_8_), channel_id=1, source_target_pairs={{1,0},{2,1},{3,2},{4,3},{5,4},{6,5},{7,6},{0,7},{9,8},{10,9},{11,1... | collective-permute-start | bytes 737288 | tf_op jit(solution)/shard_map/ppermute | solution.py:208
  9.7 0.3 copy.29
  10.2 1.0 %pad.10.refs_7_ = f32[32,32,32]{2,1,0:T(8,128)} pad(f32[32,31,31]{2,1,0:T(8,128)S(1)} %copy.29, f32[]{:T(128)} %constant.100.clone.1), padding=0_0x1_0x1_0 | pad | bytes 254084 | tf_op jit(solution)/shard_map/jit(_pad)/pad | solution.py:210
  11.2 0.6 %pad_maximum_fusion.refs_0_ = f32[3,153]{1,0:T(4,128)} fusion(f32[1,153]{1,0:T(1,128)S(1)} %bitcast.36, f32[1,153]{1,0:T(1,128)S(1)} %bitcast.37, f32[1,153]{1,0:T(1,128)S(1)} %bitcast.35), kind=kLoop, calls=%fused_computation.29 | loop fusion | flops 918 | bytes 3672 | tf_op jit(solution)/shard_map/stack | solution.py:176
  11.8 4.2 %shard_map.105 = (f32[152,32,128]{2,1,0:T(8,128)}, f32[32,32,128]{2,1,0:T(8,128)}, f32[3,32,128]{2,1,0:T(8,128)}) custom-call(f32[3,153]{1,0:T(4,128)} %pad_maximum_fusion.refs_0_, s32[32]{0:T(128)} %refs_1_.3, s32[128]{0:T(128)} %refs_2_.3, f32[152,32,128]{2,1,0:T(8,128)} %refs_5_.3, f32[152,32,128]{2,1,0:T(8,128)} %refs_5_.3, f32[152,32,128]{2,1,0:T(8,128)} %refs_5_.3, ...), custom_call_target="tpu_custom_call" | custom-call | tf_op jit(solution)/shard_map/pallas_call | solution.py:212
  16.0 1.6 %broadcast_in_dim.13 = f32[8,3,32,128]{3,2,1,0:T(8,128)} broadcast(f32[3,32,128]{2,1,0:T(8,128)} %get-tuple-element.41), dimensions={1,2,3} | broadcast | bytes 442368 | tf_op jit(solution)/shard_map/broadcast_in_dim | solution.py:228
  17.6 3.5 %all-to-all-start = ((f32[8,3,32,128]{3,2,1,0:T(8,128)}), f32[8,3,32,128]{3,2,1,0:T(8,128)S(1)}, u32[]{:S(2)}, u32[]{:S(2)}) async-start(f32[8,3,32,128]{3,2,1,0:T(8,128)} %broadcast_in_dim.13), calls=%async_computation | async-start | bytes 786432 | tf_op jit(solution)/shard_map/all_to_all | solution.py:229
  21.1 0.4 collective-permute-start
  21.5 3.4 %collective-permute-start.2 = (f32[15,8,128]{2,1,0:T(8,128)S(1)}, f32[15,8,128]{2,1,0:T(8,128)S(1)}, u32[]{:S(2)}, u32[]{:S(2)}) collective-permute-start(f32[15,8,128]{2,1,0:T(8,128)S(1)} %copy-done.10), channel_id=1, source_target_pairs={{0,8},{8,16},{16,24},{1,9},{9,17},{17,25},{2,10},{10,18},{18,26},{... | collective-permute-start | bytes 184328 | tf_op jit(solution)/shard_map/ppermute | solution.py:205
  24.9 1.3 %collective-permute-start.3 = (f32[15,8,128]{2,1,0:T(8,128)S(1)}, f32[15,8,128]{2,1,0:T(8,128)S(1)}, u32[]{:S(2)}, u32[]{:S(2)}) collective-permute-start(f32[15,8,128]{2,1,0:T(8,128)S(1)} %copy-done.9), channel_id=1, source_target_pairs={{8,0},{16,8},{24,16},{9,1},{17,9},{25,17},{10,2},{18,10},{26,18},{... | collective-permute-start | bytes 184328 | tf_op jit(solution)/shard_map/ppermute | solution.py:206
  26.2 0.2 add_reduce_fusion
  26.4 0.2 fusion.19
  26.8 0.4 copy.36
  27.2 0.1 scatter.6
  27.3 0.4 copy.37
  27.7 0.1 scatter.9
  27.9 0.1 divide_reduce_fusion.1
  28.0 3.4 %collective-permute-done.3.refs_12_ = f32[15,8,128]{2,1,0:T(8,128)S(1)} collective-permute-done((f32[15,8,128]{2,1,0:T(8,128)S(1)}, f32[15,8,128]{2,1,0:T(8,128)S(1)}, u32[]{:S(2)}, u32[]{:S(2)}) %collective-permute-start.3) | collective-permute-done | bytes 61472 | tf_op jit(solution)/shard_map/ppermute | solution.py:206
  31.4 3.7 %collective-permute-done.refs_9_ = f32[60,8,128]{2,1,0:T(8,128)S(1)} collective-permute-done((f32[60,8,128]{2,1,0:T(8,128)S(1)}, f32[60,8,128]{2,1,0:T(8,128)S(1)}, u32[]{:S(2)}, u32[]{:S(2)}) %collective-permute-start) | collective-permute-done | bytes 245792 | tf_op jit(solution)/shard_map/ppermute | solution.py:207
  35.1 0.7 %copy-done.3 = f32[60,8,128]{2,1,0:T(8,128)} copy-done((f32[60,8,128]{2,1,0:T(8,128)}, f32[60,8,128]{2,1,0:T(8,128)S(1)}, u32[]{:S(2)}) %copy-start.3) | copy-done | bytes 245784
  35.8 15.2 %shard_map.106 = (f32[152,32,128]{2,1,0:T(8,128)}, f32[152,32,128]{2,1,0:T(8,128)}) custom-call(f32[3,153]{1,0:T(4,128)} %pad_maximum_fusion.refs_0_, s32[32]{0:T(128)} %refs_1_.3, s32[128]{0:T(128)} %refs_2_.3, f32[152,32,128]{2,1,0:T(8,128)} %refs_5_.3, f32[152,32,128]{2,1,0:T(8,128)} %refs_5_.3, ...), custom_call_target="tpu_custom_call", output_to_operand_aliasing={{0}: (13, {})} | custom-call | tf_op jit(solution)/shard_map/pallas_call | solution.py:249
  51.1 0.1 multiply_reduce_fusion.1
  51.2 1.2 %select_dynamic-update-slice_fusion = f32[152,32,128]{2,1,0:T(8,128)} fusion(f32[152,32,128]{2,1,0:T(8,128)} %get-tuple-element.40, f32[32,32,128]{2,1,0:T(8,128)S(1)} %copy-done.1, f32[32,128]{1,0:T(8,128)S(1)} %get-tuple-element.47, f32[32,32]{1,0:T(8,128)S(1)} %scatter.9, f32[32,32]{1,0:T(8,128)S(1)} %scatter.6, f32[32]{0:T(128)S(1)} %copy-done.7, ...), kind=kLoop, calls=%fused_computation | loop fusion | flops 786432 | bytes 1089696 | tf_op jit(solution)/shard_map/dynamic_update_slice | solution.py:273
  (39 shorter events, 0.5 us)
Async XLA Ops:
  0.6 9.0 %copy-start.6 = (f32[2,152]{1,0:T(2,128)S(1)}, f32[2,152]{1,0:T(2,128)}, u32[]{:S(2)}) copy-start(f32[2,152]{1,0:T(2,128)} %param.17) | copy-start | bytes 3652
  0.6 9.1 %copy-start = (f32[32,31,31]{2,0,1:T(8,128)S(1)}, f32[32,31,31]{2,0,1:T(8,128)}, u32[]{:S(2)}) copy-start(f32[32,31,31]{2,0,1:T(8,128)} %param.21) | copy-start | bytes 369028
  5.2 26.2 %collective-permute-start.1 = (f32[60,8,128]{2,1,0:T(8,128)}, f32[60,8,128]{2,1,0:T(8,128)S(1)}, u32[]{:S(2)}, u32[]{:S(2)}) collective-permute-start(f32[60,8,128]{2,1,0:T(8,128)} %get-tuple-element.36.refs_8_), channel_id=1, source_target_pairs={{1,0},{2,1},{3,2},{4,3},{5,4},{6,5},{7,6},{0,7},{9,8},{10,9},{11,1... | collective-permute-start | bytes 737288 | tf_op jit(solution)/shard_map/ppermute | solution.py:208
  11.8 9.3 %copy-start.8 = (f32[60,8,128]{2,1,0:T(8,128)S(1)}, f32[60,8,128]{2,1,0:T(8,128)}, u32[]{:S(2)}) copy-start(f32[60,8,128]{2,1,0:T(8,128)} %get-tuple-element.35) | copy-start | bytes 737284
  11.8 9.7 %copy-start.10 = (f32[15,8,128]{2,1,0:T(8,128)S(1)}, f32[15,8,128]{2,1,0:T(8,128)}, u32[]{:S(2)}) copy-start(f32[15,8,128]{2,1,0:T(8,128)} %get-tuple-element.37) | copy-start | bytes 184324
  11.8 13.1 %copy-start.9 = (f32[15,8,128]{2,1,0:T(8,128)S(1)}, f32[15,8,128]{2,1,0:T(8,128)}, u32[]{:S(2)}) copy-start(f32[15,8,128]{2,1,0:T(8,128)} %get-tuple-element.38) | copy-start | bytes 184324
  16.0 10.7 %copy-start.7 = (f32[32]{0:T(128)S(1)}, f32[32]{0:T(128)}, u32[]{:S(2)}) copy-start(f32[32]{0:T(128)} %param.20) | copy-start | bytes 388
  17.6 33.4 %all-to-all-start = ((f32[8,3,32,128]{3,2,1,0:T(8,128)}), f32[8,3,32,128]{3,2,1,0:T(8,128)S(1)}, u32[]{:S(2)}, u32[]{:S(2)}) async-start(f32[8,3,32,128]{3,2,1,0:T(8,128)} %broadcast_in_dim.13), calls=%async_computation | async-start | bytes 786432 | tf_op jit(solution)/shard_map/all_to_all | solution.py:229
  21.1 14.0 %collective-permute-start = (f32[60,8,128]{2,1,0:T(8,128)S(1)}, f32[60,8,128]{2,1,0:T(8,128)S(1)}, u32[]{:S(2)}, u32[]{:S(2)}) collective-permute-start(f32[60,8,128]{2,1,0:T(8,128)S(1)} %copy-done.8), channel_id=1, source_target_pairs={{0,1},{1,2},{2,3},{3,4},{4,5},{5,6},{6,7},{7,0},{8,9},{9,10},{10,1... | collective-permute-start | bytes 737288 | tf_op jit(solution)/shard_map/ppermute | solution.py:207
  21.5 6.5 %collective-permute-start.2 = (f32[15,8,128]{2,1,0:T(8,128)S(1)}, f32[15,8,128]{2,1,0:T(8,128)S(1)}, u32[]{:S(2)}, u32[]{:S(2)}) collective-permute-start(f32[15,8,128]{2,1,0:T(8,128)S(1)} %copy-done.10), channel_id=1, source_target_pairs={{0,8},{8,16},{16,24},{1,9},{9,17},{17,25},{2,10},{10,18},{18,26},{... | collective-permute-start | bytes 184328 | tf_op jit(solution)/shard_map/ppermute | solution.py:205
  24.9 6.5 %collective-permute-start.3 = (f32[15,8,128]{2,1,0:T(8,128)S(1)}, f32[15,8,128]{2,1,0:T(8,128)S(1)}, u32[]{:S(2)}, u32[]{:S(2)}) collective-permute-start(f32[15,8,128]{2,1,0:T(8,128)S(1)} %copy-done.9), channel_id=1, source_target_pairs={{8,0},{16,8},{24,16},{9,1},{17,9},{25,17},{10,2},{18,10},{26,18},{... | collective-permute-start | bytes 184328 | tf_op jit(solution)/shard_map/ppermute | solution.py:206
  28.0 7.1 %copy-start.4 = (f32[15,8,128]{2,1,0:T(8,128)}, f32[15,8,128]{2,1,0:T(8,128)S(1)}, u32[]{:S(2)}) copy-start(f32[15,8,128]{2,1,0:T(8,128)S(1)} %collective-permute-done.2.refs_11_) | copy-start | bytes 184324
  31.4 3.8 %copy-start.5 = (f32[15,8,128]{2,1,0:T(8,128)}, f32[15,8,128]{2,1,0:T(8,128)S(1)}, u32[]{:S(2)}) copy-start(f32[15,8,128]{2,1,0:T(8,128)S(1)} %collective-permute-done.3.refs_12_) | copy-start | bytes 184324
  31.4 3.8 %copy-start.2 = (f32[60,8,128]{2,1,0:T(8,128)}, f32[60,8,128]{2,1,0:T(8,128)S(1)}, u32[]{:S(2)}) copy-start(f32[60,8,128]{2,1,0:T(8,128)S(1)} %collective-permute-done.1.refs_10_) | copy-start | bytes 737284
  35.1 0.7 %copy-start.3 = (f32[60,8,128]{2,1,0:T(8,128)}, f32[60,8,128]{2,1,0:T(8,128)S(1)}, u32[]{:S(2)}) copy-start(f32[60,8,128]{2,1,0:T(8,128)S(1)} %collective-permute-done.refs_9_) | copy-start | bytes 737284
  35.8 15.4 %copy-start.1 = (f32[32,32,128]{2,1,0:T(8,128)S(1)}, f32[32,32,128]{2,1,0:T(8,128)}, u32[]{:S(2)}) copy-start(f32[32,32,128]{2,1,0:T(8,128)} %get-tuple-element.42) | copy-start | bytes 1572868

commit v5 on v4

--- a/solution.py
+++ b/solution.py
@@ -16,7 +16,7 @@
 LB = 8
 
 
-def pack_kernel(th_ref, xl_ref, xr_ref, zl_ref, zr_ref):
+def pack_kernel(th_ref, u_ref, xl_ref, xr_ref, ul_ref, ur_ref, zl_ref, zr_ref):
     ny, cz, w = th_ref.shape
     nblocks = xl_ref.shape[0]
     skip = ny - nblocks * LB
@@ -27,15 +27,25 @@
         first = skip + b * LB
         acc_l = jnp.zeros((8, w), jnp.float32)
         acc_r = jnp.zeros((8, w), jnp.float32)
+        uacc_l = jnp.zeros((8, w), jnp.float32)
+        uacc_r = jnp.zeros((8, w), jnp.float32)
         for s in range(LB):
+            speed = u_ref[first + s].astype(jnp.float32)
             for v in range(cz // 8):
                 t = th_ref[first + s, 8 * v:8 * v + 8, :]
                 pos = 4 * LB * v + 4 * s
-                pick = jnp.logical_and(lane8 >= pos, lane8 < pos + 4)
-                acc_l = jnp.where(pick, pltpu.roll(t, pos % w, 1), acc_l)
-                acc_r = jnp.where(pick, pltpu.roll(t, (pos + 4) % w, 1), acc_r)
+                moved = pltpu.roll(t, pos % w, 1)
+                umoved = pltpu.roll(speed[8 * v:8 * v + 8], pos % w, 1)
+                pick_l = jnp.logical_and(lane8 >= pos, lane8 < pos + 4)
+                pick_r = jnp.logical_and(lane8 >= (pos - 4) % w, lane8 < (pos - 4) % w + 4)
+                acc_l = jnp.where(pick_l, moved, acc_l)
+                acc_r = jnp.where(pick_r, moved, acc_r)
+                uacc_l = jnp.where(pick_l, umoved, uacc_l)
+                uacc_r = jnp.where(pick_r, umoved, uacc_r)
         xl_ref[b] = acc_l
         xr_ref[b] = acc_r
+        ul_ref[b] = uacc_l
+        ur_ref[b] = uacc_r
         for p in range(LB // 2):
             a_hi = th_ref[first + 2 * p, cz - 8:cz, :]
             b_hi = th_ref[first + 2 * p + 1, cz - 8:cz, :]
@@ -51,8 +61,8 @@
 def layer_kernel(fluid, block_offset, *refs):
     if fluid:
         (face_ref, wall_ref, contact_ref, th_ref, prev_ref, next_ref, st_ref,
-         u_ref, v_ref, zb_ref, za_ref, xb_ref, xa_ref, _alias_ref,
-         sn_ref, tn_ref, wallv_ref, contv_ref, ext_ref) = refs
+         u_ref, v_ref, zb_ref, za_ref, xb_ref, xa_ref, xl_ref, xr_ref, ul_ref, ur_ref,
+         _alias_ref, sn_ref, tn_ref, wallv_ref, contv_ref, ext_ref) = refs
     else:
         (face_ref, wall_ref, contact_ref, th_ref, prev_ref, next_ref, st_ref,
          bs_ref, _order_ref, sn_ref, int_ref, mine_ref, wallv_ref, contv_ref) = refs
@@ -85,6 +95,24 @@
         lane = lax.broadcasted_iota(jnp.int32, (8, w), 1)
         nv = cz // 8
         slope_scale = -stream_courant / 60.0
+        quarter = lane % 4
+        miss_l = xb_ref[0] - xr_ref[0]
+        miss_r = xa_ref[0] - xl_ref[0]
+
+        def edge(miss, weights, left):
+            acc = jnp.zeros((8, w), jnp.float32)
+            for j, c in weights:
+                if left:
+                    term = jnp.where(quarter < j, pltpu.roll(miss, j, 1), 0.0)
+                else:
+                    term = jnp.where(quarter >= 4 - j, pltpu.roll(miss, w - j, 1), 0.0)
+                acc = acc + c * term
+            return acc
+
+        fix_l = (slope_scale * ul_ref[0] * edge(miss_l, ((1, -45.0), (2, 9.0), (3, -1.0)), True)
+                 - damping * edge(miss_l, ((1, -56.0), (2, 28.0), (3, -8.0), (4, 1.0)), True))
+        fix_r = (slope_scale * ur_ref[0] * edge(miss_r, ((1, 45.0), (2, -9.0), (3, 1.0)), False)
+                 - damping * edge(miss_r, ((1, -56.0), (2, 28.0), (3, -8.0), (4, 1.0)), False))
 
     heads = []
     face_dn = face(base - 1)
@@ -99,20 +127,16 @@
         if fluid:
             u = u_ref[s].astype(jnp.float32)
             v = v_ref[s].astype(jnp.float32)
-            edge_b = xb_ref[0]
-            edge_a = xa_ref[0]
-            xm = [[None] * nv for _ in range(5)]
-            xp = [[None] * nv for _ in range(5)]
+            xm = [None] + [pltpu.roll(t, j, 1) for j in range(1, 5)]
+            xp = [None] + [pltpu.roll(t, w - j, 1) for j in range(1, 5)]
+            fixes = []
             for g in range(nv):
-                tg = t[8 * g:8 * g + 8]
                 pos = 4 * LB * g + 4 * s
-                for j in range(1, 5):
-                    xm[j][g] = jnp.where(lane < j, pltpu.roll(edge_b, (j - 4 - pos) % w, 1),
-                                         pltpu.roll(tg, j, 1))
-                    xp[j][g] = jnp.where(lane >= w - j, pltpu.roll(edge_a, (w - j - pos) % w, 1),
-                                         pltpu.roll(tg, w - j, 1))
-            xm = [None] + [jnp.concatenate(xm[j], axis=0) for j in range(1, 5)]
-            xp = [None] + [jnp.concatenate(xp[j], axis=0) for j in range(1, 5)]
+                at_l = jnp.logical_and(lane >= pos, lane < pos + 4)
+                at_r = jnp.logical_and(lane >= (pos - 4) % w, lane < (pos - 4) % w + 4)
+                picked = jnp.where(at_l, fix_l, jnp.where(at_r, fix_r, 0.0))
+                fixes.append(pltpu.roll(picked, (w - pos) % w, 1))
+            fix = jnp.concatenate(fixes, axis=0)
             packed_b = zb_ref[s // 2]
             packed_a = za_ref[s // 2]
             if s % 2 == 0:
@@ -134,7 +158,7 @@
 
             smoothing = smooth(zm, zp) + smooth(xm, xp) + 140.0 * t
             horiz = (slope_scale * (u * slope(xm, xp) + v * slope(zm, zp))
-                     - damping * smoothing)
+                     - damping * smoothing) + fix
             across = jnp.where(y >= wall, horiz, 0.0)
             rate = normal + across
         else:
@@ -186,21 +210,15 @@
     edge_spec = pl.BlockSpec((1, 8, w), lambda i: (i, 0, 0))
     rows_spec = pl.BlockSpec((LB // 2, 8, w), lambda i: (i, 0, 0))
 
-    xl, xr, zl, zr = pl.pallas_call(
+    xl, xr, ul, ur, zl, zr = pl.pallas_call(
         pack_kernel,
         grid=(1,),
-        in_specs=[pl.BlockSpec((ny, cz, w), lambda i: (0, 0, 0))],
-        out_specs=[pl.BlockSpec((nfb, 8, w), lambda i: (0, 0, 0)),
-                   pl.BlockSpec((nfb, 8, w), lambda i: (0, 0, 0)),
-                   pl.BlockSpec((nf // 2, 8, w), lambda i: (0, 0, 0)),
-                   pl.BlockSpec((nf // 2, 8, w), lambda i: (0, 0, 0))],
-        out_shape=[
-            jax.ShapeDtypeStruct((nfb, 8, w), f32),
-            jax.ShapeDtypeStruct((nfb, 8, w), f32),
-            jax.ShapeDtypeStruct((nf // 2, 8, w), f32),
-            jax.ShapeDtypeStruct((nf // 2, 8, w), f32),
-        ],
-    )(theta)
+        in_specs=[pl.BlockSpec((ny, cz, w), lambda i: (0, 0, 0))] * 2,
+        out_specs=[pl.BlockSpec((nfb, 8, w), lambda i: (0, 0, 0))] * 4
+        + [pl.BlockSpec((nf // 2, 8, w), lambda i: (0, 0, 0))] * 2,
+        out_shape=[jax.ShapeDtypeStruct((nfb, 8, w), f32)] * 4
+        + [jax.ShapeDtypeStruct((nf // 2, 8, w), f32)] * 2,
+    )(theta, stream_speed)
 
     xb = lax.ppermute(xr, "gx", [(i, i + 1) for i in range(ngx - 1)])
     xa = lax.ppermute(xl, "gx", [(i + 1, i) for i in range(ngx - 1)])
@@ -251,6 +269,7 @@
         grid=(nfb,),
         in_specs=[smem, smem, smem, blk(nsb), prev_spec(nsb), next_spec(nsb), blk(nsb),
                   blk(nsb), blk(nsb), rows_spec, rows_spec, edge_spec, edge_spec,
+                  edge_spec, edge_spec, edge_spec, edge_spec,
                   pl.BlockSpec(memory_space=pl.ANY)],
         out_specs=[blk(nsb), blk(nsb)],
         out_shape=[
@@ -259,9 +278,9 @@
         ],
         scratch_shapes=[pltpu.VMEM((cz, w), jnp.int32), pltpu.VMEM((cz, w), f32),
                         pltpu.VMEM((cz + 16, w), f32)],
-        input_output_aliases={13: 0},
+        input_output_aliases={17: 0},
     )(faces, wall_layers, contact, theta, theta, theta, section_store,
-      stream_speed, span_speed, zb, za, xb, xa, sn_part)
+      stream_speed, span_speed, zb, za, xb, xa, xl, xr, ul, ur, sn_part)
 
     row = jnp.arange(cz, dtype=jnp.int32)
     col0 = jnp.zeros((ns, cz), f32).at[:, 1:].set(block_inverse[:, :, 0])

time: 53.2 us -> 52.1 us (0.979)
  Pallas kernels: 23.9 us -> 23 us
    pallas_call x1, Pallas kernels: 15.2 us -> 13.7 us  [local(): pl.pallas_call(lambda *refs: layer_kernel(True, nsb, *refs), grid=(nfb,),...]
    ppermute x1, waiting for transfers between devices: 3.74 us -> 4.46 us  [local(): zb = lax.ppermute(zl, 'gz', [(i, (i + 1) % ngz) for i in range(ngz)])]
    ppermute x1, waiting for transfers between devices: 3.36 us -> 2.81 us  [local(): xa = lax.ppermute(xl, 'gx', [(i + 1, i) for i in range(ngx - 1)])]
  transfers between devices with their start and end apart: 5 -> 5, of which waited for: 2 -> 2; matrix products, arithmetic and copies ran while one was open for 10% -> 11% of each run, Pallas kernels for 37% -> 35%
where the time goes in v5:
time: 52.1 us; the launch traced here: 51.5 us
  Pallas kernels  23 us (44%)
  starting transfers between devices  12.8 us (25%)
  waiting for transfers between devices  7.29 us (14%)
  local copies, waits for them, and re-layouts  4.95 us (10%)
  other arithmetic  2.62 us (5%)
  between operations  0.85 us (2%)
    pallas_call x1, Pallas kernels, local(): pl.pallas_call(lambda *refs: layer_kernel(True, nsb, *refs), grid=(nfb,),...  13.7 us
    pallas_call x1, Pallas kernels, local(): pl.pallas_call(pack_kernel, grid=(1,), in_specs=[pl.BlockSpec((ny, cz, w)...  4.95 us
    ppermute x1, starting transfers between devices, local(): za = lax.ppermute(zr, 'gz', [((i + 1) % ngz, i) for i in range(ngz)])  4.49 us
    ppermute x1, waiting for transfers between devices, local(): zb = lax.ppermute(zl, 'gz', [(i, (i + 1) % ngz) for i in range(ngz)])  4.46 us
    pallas_call x1, Pallas kernels, local(): pl.pallas_call(lambda *refs: layer_kernel(False, 0, *refs), grid=(nsb,),...  4.32 us
    all_to_all x1, starting transfers between devices, local(): blocks = lax.all_to_all(spread, 'gz', 0, 0, tiled=True)  3.45 us
    ppermute x1, starting transfers between devices, local(): xb = lax.ppermute(xr, 'gx', [(i, i + 1) for i in range(ngx - 1)])  3.42 us
    ppermute x1, waiting for transfers between devices, local(): xa = lax.ppermute(xl, 'gx', [(i + 1, i) for i in range(ngx - 1)])  2.81 us
  transfers between devices with their start and end apart: 5, of which 2 were waited for; matrix products, arithmetic and copies ran while one was open for 11% of the time, Pallas kernels for 35%

profile of v5, /device:TPU:0, one launch (start us, length us, event | category | flops | bytes accessed | tf_op | source)
XLA Modules:
  0.0 51.5 jit_solution(14372806242235006809)
XLA Ops:
  0.6 5.0 %shard_map.104 = (f32[15,8,128]{2,1,0:T(8,128)}, f32[15,8,128]{2,1,0:T(8,128)}, f32[15,8,128]{2,1,0:T(8,128)}, f32[15,8,128]{2,1,0:T(8,128)}, f32[60,8,128]{2,1,0:T(8,128)}, /*index=5*/f32[60,8,128]{2,1,0:T(8,128)}) custom-call(f32[152,32,128]{2,1,0:T(8,128)} %refs_5_.3, bf16[152,32,128]{2,1,0:T(8,128)(2,1)} %refs_7_.1), custom_call_target="tpu_custom_call" | custom-call | tf_op jit(solution)/shard_map/pallas_call | solution.py:213
  5.6 4.5 %collective-permute-start.1 = (f32[60,8,128]{2,1,0:T(8,128)}, f32[60,8,128]{2,1,0:T(8,128)S(1)}, u32[]{:S(2)}, u32[]{:S(2)}) collective-permute-start(f32[60,8,128]{2,1,0:T(8,128)} %get-tuple-element.38.refs_8_), channel_id=1, source_target_pairs={{1,0},{2,1},{3,2},{4,3},{5,4},{6,5},{7,6},{0,7},{9,8},{10,9},{11,1... | collective-permute-start | bytes 737288 | tf_op jit(solution)/shard_map/ppermute | solution.py:226
  10.2 0.3 copy.29
  10.6 1.0 %pad.10.refs_7_ = f32[32,32,32]{2,1,0:T(8,128)} pad(f32[32,31,31]{2,1,0:T(8,128)S(1)} %copy.29, f32[]{:T(128)} %constant.100.clone.1), padding=0_0x1_0x1_0 | pad | bytes 254084 | tf_op jit(solution)/shard_map/jit(_pad)/pad | solution.py:228
  11.6 0.6 %pad_maximum_fusion.refs_0_ = f32[3,153]{1,0:T(4,128)} fusion(f32[1,153]{1,0:T(1,128)S(1)} %bitcast.36, f32[1,153]{1,0:T(1,128)S(1)} %bitcast.37, f32[1,153]{1,0:T(1,128)S(1)} %bitcast.35), kind=kLoop, calls=%fused_computation.29 | loop fusion | flops 918 | bytes 3672 | tf_op jit(solution)/shard_map/stack | solution.py:200
  12.2 4.3 %shard_map.105 = (f32[152,32,128]{2,1,0:T(8,128)}, f32[32,32,128]{2,1,0:T(8,128)}, f32[3,32,128]{2,1,0:T(8,128)}) custom-call(f32[3,153]{1,0:T(4,128)} %pad_maximum_fusion.refs_0_, s32[32]{0:T(128)} %refs_1_.3, s32[128]{0:T(128)} %refs_2_.3, f32[152,32,128]{2,1,0:T(8,128)} %refs_5_.3, f32[152,32,128]{2,1,0:T(8,128)} %refs_5_.3, f32[152,32,128]{2,1,0:T(8,128)} %refs_5_.3, ...), custom_call_target="tpu_custom_call" | custom-call | tf_op jit(solution)/shard_map/pallas_call | solution.py:230
  16.6 1.6 %broadcast_in_dim.13 = f32[8,3,32,128]{3,2,1,0:T(8,128)} broadcast(f32[3,32,128]{2,1,0:T(8,128)} %get-tuple-element.45), dimensions={1,2,3} | broadcast | bytes 442368 | tf_op jit(solution)/shard_map/broadcast_in_dim | solution.py:246
  18.2 3.5 %all-to-all-start = ((f32[8,3,32,128]{3,2,1,0:T(8,128)}), f32[8,3,32,128]{3,2,1,0:T(8,128)S(1)}, u32[]{:S(2)}, u32[]{:S(2)}) async-start(f32[8,3,32,128]{3,2,1,0:T(8,128)} %broadcast_in_dim.13), calls=%async_computation | async-start | bytes 786432 | tf_op jit(solution)/shard_map/all_to_all | solution.py:247
  21.6 3.4 %collective-permute-start.2 = (f32[15,8,128]{2,1,0:T(8,128)S(1)}, f32[15,8,128]{2,1,0:T(8,128)S(1)}, u32[]{:S(2)}, u32[]{:S(2)}) collective-permute-start(f32[15,8,128]{2,1,0:T(8,128)S(1)} %copy-done.5), channel_id=1, source_target_pairs={{0,8},{8,16},{16,24},{1,9},{9,17},{17,25},{2,10},{10,18},{18,26},{... | collective-permute-start | bytes 184328 | tf_op jit(solution)/shard_map/ppermute | solution.py:223
  25.1 1.3 %collective-permute-start.3 = (f32[15,8,128]{2,1,0:T(8,128)S(1)}, f32[15,8,128]{2,1,0:T(8,128)S(1)}, u32[]{:S(2)}, u32[]{:S(2)}) collective-permute-start(f32[15,8,128]{2,1,0:T(8,128)S(1)} %copy-done.4), channel_id=1, source_target_pairs={{8,0},{16,8},{24,16},{9,1},{17,9},{25,17},{10,2},{18,10},{26,18},{... | collective-permute-start | bytes 184328 | tf_op jit(solution)/shard_map/ppermute | solution.py:224
  26.4 0.1 collective-permute-start
  26.5 0.2 add_reduce_fusion
  26.7 0.2 fusion.19
  27.1 0.4 copy.36
  27.6 0.1 scatter.6
  27.6 0.4 copy.37
  28.1 0.1 scatter.9
  28.2 0.1 divide_reduce_fusion.1
  28.4 2.8 %collective-permute-done.3.refs_12_ = f32[15,8,128]{2,1,0:T(8,128)S(1)} collective-permute-done((f32[15,8,128]{2,1,0:T(8,128)S(1)}, f32[15,8,128]{2,1,0:T(8,128)S(1)}, u32[]{:S(2)}, u32[]{:S(2)}) %collective-permute-start.3) | collective-permute-done | bytes 61472 | tf_op jit(solution)/shard_map/ppermute | solution.py:224
  31.2 4.5 %collective-permute-done.refs_9_ = f32[60,8,128]{2,1,0:T(8,128)S(1)} collective-permute-done((f32[60,8,128]{2,1,0:T(8,128)S(1)}, f32[60,8,128]{2,1,0:T(8,128)S(1)}, u32[]{:S(2)}, u32[]{:S(2)}) %collective-permute-start) | collective-permute-done | bytes 245792 | tf_op jit(solution)/shard_map/ppermute | solution.py:225
  35.7 0.7 %copy-done.3 = f32[60,8,128]{2,1,0:T(8,128)} copy-done((f32[60,8,128]{2,1,0:T(8,128)}, f32[60,8,128]{2,1,0:T(8,128)S(1)}, u32[]{:S(2)}) %copy-start.3) | copy-done | bytes 245784
  36.4 13.7 %shard_map.106 = (f32[152,32,128]{2,1,0:T(8,128)}, f32[152,32,128]{2,1,0:T(8,128)}) custom-call(f32[3,153]{1,0:T(4,128)} %pad_maximum_fusion.refs_0_, s32[32]{0:T(128)} %refs_1_.3, s32[128]{0:T(128)} %refs_2_.3, f32[152,32,128]{2,1,0:T(8,128)} %refs_5_.3, f32[152,32,128]{2,1,0:T(8,128)} %refs_5_.3, ...), custom_call_target="tpu_custom_call", output_to_operand_aliasing={{0}: (17, {})} | custom-call | tf_op jit(solution)/shard_map/pallas_call | solution.py:267
  50.1 0.1 multiply_reduce_fusion.1
  50.3 1.2 %select_dynamic-update-slice_fusion = f32[152,32,128]{2,1,0:T(8,128)} fusion(f32[152,32,128]{2,1,0:T(8,128)} %get-tuple-element.44, f32[32,32,128]{2,1,0:T(8,128)S(1)} %copy-done.1, f32[32,128]{1,0:T(8,128)S(1)} %get-tuple-element.51, f32[32,32]{1,0:T(8,128)S(1)} %scatter.9, f32[32,32]{1,0:T(8,128)S(1)} %scatter.6, f32[32]{0:T(128)S(1)} %copy-done.9, ...), kind=kLoop, calls=%fused_computation | loop fusion | flops 786432 | bytes 1089696 | tf_op jit(solution)/shard_map/dynamic_update_slice | solution.py:292
  (39 shorter events, 0.5 us)
Async XLA Ops:
  0.6 9.5 %copy-start.8 = (f32[2,152]{1,0:T(2,128)S(1)}, f32[2,152]{1,0:T(2,128)}, u32[]{:S(2)}) copy-start(f32[2,152]{1,0:T(2,128)} %param.17) | copy-start | bytes 3652
  0.6 9.5 %copy-start = (f32[32,31,31]{2,0,1:T(8,128)S(1)}, f32[32,31,31]{2,0,1:T(8,128)}, u32[]{:S(2)}) copy-start(f32[32,31,31]{2,0,1:T(8,128)} %param.21) | copy-start | bytes 369028
  5.6 25.6 %collective-permute-start.1 = (f32[60,8,128]{2,1,0:T(8,128)}, f32[60,8,128]{2,1,0:T(8,128)S(1)}, u32[]{:S(2)}, u32[]{:S(2)}) collective-permute-start(f32[60,8,128]{2,1,0:T(8,128)} %get-tuple-element.38.refs_8_), channel_id=1, source_target_pairs={{1,0},{2,1},{3,2},{4,3},{5,4},{6,5},{7,6},{0,7},{9,8},{10,9},{11,1... | collective-permute-start | bytes 737288 | tf_op jit(solution)/shard_map/ppermute | solution.py:226
  12.2 9.4 %copy-start.5 = (f32[15,8,128]{2,1,0:T(8,128)S(1)}, f32[15,8,128]{2,1,0:T(8,128)}, u32[]{:S(2)}) copy-start(f32[15,8,128]{2,1,0:T(8,128)} %get-tuple-element.39.refs_14_) | copy-start | bytes 184324
  12.2 12.8 %copy-start.4 = (f32[15,8,128]{2,1,0:T(8,128)S(1)}, f32[15,8,128]{2,1,0:T(8,128)}, u32[]{:S(2)}) copy-start(f32[15,8,128]{2,1,0:T(8,128)} %get-tuple-element.40.refs_13_) | copy-start | bytes 184324
  12.2 14.1 %copy-start.10 = (f32[60,8,128]{2,1,0:T(8,128)S(1)}, f32[60,8,128]{2,1,0:T(8,128)}, u32[]{:S(2)}) copy-start(f32[60,8,128]{2,1,0:T(8,128)} %get-tuple-element.37) | copy-start | bytes 737284
  16.6 10.5 %copy-start.9 = (f32[32]{0:T(128)S(1)}, f32[32]{0:T(128)}, u32[]{:S(2)}) copy-start(f32[32]{0:T(128)} %param.20) | copy-start | bytes 388
  18.2 31.9 %all-to-all-start = ((f32[8,3,32,128]{3,2,1,0:T(8,128)}), f32[8,3,32,128]{3,2,1,0:T(8,128)S(1)}, u32[]{:S(2)}, u32[]{:S(2)}) async-start(f32[8,3,32,128]{3,2,1,0:T(8,128)} %broadcast_in_dim.13), calls=%async_computation | async-start | bytes 786432 | tf_op jit(solution)/shard_map/all_to_all | solution.py:247
  21.6 6.7 %collective-permute-start.2 = (f32[15,8,128]{2,1,0:T(8,128)S(1)}, f32[15,8,128]{2,1,0:T(8,128)S(1)}, u32[]{:S(2)}, u32[]{:S(2)}) collective-permute-start(f32[15,8,128]{2,1,0:T(8,128)S(1)} %copy-done.5), channel_id=1, source_target_pairs={{0,8},{8,16},{16,24},{1,9},{9,17},{17,25},{2,10},{10,18},{18,26},{... | collective-permute-start | bytes 184328 | tf_op jit(solution)/shard_map/ppermute | solution.py:223
  25.1 6.1 %collective-permute-start.3 = (f32[15,8,128]{2,1,0:T(8,128)S(1)}, f32[15,8,128]{2,1,0:T(8,128)S(1)}, u32[]{:S(2)}, u32[]{:S(2)}) collective-permute-start(f32[15,8,128]{2,1,0:T(8,128)S(1)} %copy-done.4), channel_id=1, source_target_pairs={{8,0},{16,8},{24,16},{9,1},{17,9},{25,17},{10,2},{18,10},{26,18},{... | collective-permute-start | bytes 184328 | tf_op jit(solution)/shard_map/ppermute | solution.py:224
  26.4 9.3 %collective-permute-start = (f32[60,8,128]{2,1,0:T(8,128)S(1)}, f32[60,8,128]{2,1,0:T(8,128)S(1)}, u32[]{:S(2)}, u32[]{:S(2)}) collective-permute-start(f32[60,8,128]{2,1,0:T(8,128)S(1)} %copy-done.10), channel_id=1, source_target_pairs={{0,1},{1,2},{2,3},{3,4},{4,5},{5,6},{6,7},{7,0},{8,9},{9,10},{10,1... | collective-permute-start | bytes 737288 | tf_op jit(solution)/shard_map/ppermute | solution.py:225
  28.4 7.3 %copy-start.6 = (f32[15,8,128]{2,1,0:T(8,128)}, f32[15,8,128]{2,1,0:T(8,128)S(1)}, u32[]{:S(2)}) copy-start(f32[15,8,128]{2,1,0:T(8,128)S(1)} %collective-permute-done.2.refs_11_) | copy-start | bytes 184324
  31.2 4.5 %copy-start.7 = (f32[15,8,128]{2,1,0:T(8,128)}, f32[15,8,128]{2,1,0:T(8,128)S(1)}, u32[]{:S(2)}) copy-start(f32[15,8,128]{2,1,0:T(8,128)S(1)} %collective-permute-done.3.refs_12_) | copy-start | bytes 184324
  31.2 4.5 %copy-start.2 = (f32[60,8,128]{2,1,0:T(8,128)}, f32[60,8,128]{2,1,0:T(8,128)S(1)}, u32[]{:S(2)}) copy-start(f32[60,8,128]{2,1,0:T(8,128)S(1)} %collective-permute-done.1.refs_10_) | copy-start | bytes 737284
  35.7 0.7 %copy-start.3 = (f32[60,8,128]{2,1,0:T(8,128)}, f32[60,8,128]{2,1,0:T(8,128)S(1)}, u32[]{:S(2)}) copy-start(f32[60,8,128]{2,1,0:T(8,128)S(1)} %collective-permute-done.refs_9_) | copy-start | bytes 737284
  36.4 13.9 %copy-start.1 = (f32[32,32,128]{2,1,0:T(8,128)S(1)}, f32[32,32,128]{2,1,0:T(8,128)}, u32[]{:S(2)}) copy-start(f32[32,32,128]{2,1,0:T(8,128)} %get-tuple-element.46) | copy-start | bytes 1572868

commit v6 on v5

--- a/solution.py
+++ b/solution.py
@@ -58,7 +58,7 @@
     lax.fori_loop(0, nblocks, block, 0)
 
 
-def layer_kernel(fluid, block_offset, *refs):
+def layer_kernel(fluid, block_offset, lb, *refs):
     if fluid:
         (face_ref, wall_ref, contact_ref, th_ref, prev_ref, next_ref, st_ref,
          u_ref, v_ref, zb_ref, za_ref, xb_ref, xa_ref, xl_ref, xr_ref, ul_ref, ur_ref,
@@ -67,7 +67,7 @@
         (face_ref, wall_ref, contact_ref, th_ref, prev_ref, next_ref, st_ref,
          bs_ref, _order_ref, sn_ref, int_ref, mine_ref, wallv_ref, contv_ref) = refs
     _, cz, w = th_ref.shape
-    base = (pl.program_id(0) + block_offset) * LB
+    base = (pl.program_id(0) + block_offset) * lb
 
     @pl.when(pl.program_id(0) == 0)
     def _():
@@ -116,11 +116,11 @@
 
     heads = []
     face_dn = face(base - 1)
-    for s in range(LB):
+    for s in range(lb):
         y = base + s
         t = th_ref[s]
         tp = th_ref[s - 1] if s > 0 else prev_ref[0]
-        tn = th_ref[s + 1] if s < LB - 1 else next_ref[0]
+        tn = th_ref[s + 1] if s < lb - 1 else next_ref[0]
         face_up = face(y)
         normal = face_up * (tn - t) - face_dn * (t - tp)
         face_dn = face_up
@@ -169,13 +169,16 @@
         if fluid:
             tn_ref[s] = adv
         else:
-            inner = jnp.dot(bs_ref[s], adv, precision=lax.Precision.HIGHEST,
+            inner = jnp.dot(bs_ref[s], adv[1:], precision=lax.Precision.HIGHEST,
                             preferred_element_type=jnp.float32)
+            inner = jnp.concatenate([jnp.zeros((1, w), jnp.float32), inner], axis=0)
             int_ref[s] = inner
             heads.append((adv[0:1, :], inner[1:2, :], inner[cz - 1:cz, :]))
     if not fluid:
         for part in range(3):
-            mine_ref[part] = jnp.concatenate([h[part] for h in heads], axis=0)
+            rows = jnp.concatenate([h[part] for h in heads], axis=0)
+            for n in range(mine_ref.shape[0]):
+                mine_ref[n, part] = rows
 
 
 def local(theta, section_store, stream_speed, span_speed, conductivity, wall_layers,
@@ -225,25 +228,28 @@
     zb = lax.ppermute(zl, "gz", [(i, (i + 1) % ngz) for i in range(ngz)])
     za = lax.ppermute(zr, "gz", [((i + 1) % ngz, i) for i in range(ngz)])
 
-    shifted_inverse = jnp.pad(block_inverse, ((0, 0), (1, 0), (1, 0)))
-
-    sn_part, interior, mine = pl.pallas_call(
-        lambda *refs: layer_kernel(False, 0, *refs),
-        grid=(nsb,),
-        in_specs=[smem, smem, smem, blk(0), prev_spec(0), next_spec(0), blk(0),
-                  pl.BlockSpec((LB, cz, cz), lambda i: (i, 0, 0)),
+
+    sb = 2 * LB if ns % (2 * LB) == 0 else LB
+    sblk = pl.BlockSpec((sb, cz, w), lambda i: (i, 0, 0))
+    sn_part, interior, spread = pl.pallas_call(
+        lambda *refs: layer_kernel(False, 0, sb, *refs),
+        grid=(ns // sb,),
+        in_specs=[smem, smem, smem, sblk,
+                  pl.BlockSpec((1, cz, w), lambda i: (jnp.maximum(i * sb - 1, 0), 0, 0)),
+                  pl.BlockSpec((1, cz, w), lambda i: (jnp.minimum(i * sb + sb, ny - 1), 0, 0)),
+                  sblk,
+                  pl.BlockSpec((sb, cz - 1, cz - 1), lambda i: (i, 0, 0)),
                   pl.BlockSpec(memory_space=pl.ANY)],
-        out_specs=[blk(0), blk(0), pl.BlockSpec((3, LB, w), lambda i: (0, i, 0))],
+        out_specs=[sblk, sblk, pl.BlockSpec((ngz, 3, sb, w), lambda i: (0, 0, i, 0))],
         out_shape=[
             jax.ShapeDtypeStruct((ny, cz, w), f32),
             jax.ShapeDtypeStruct((ns, cz, w), f32),
-            jax.ShapeDtypeStruct((3, ns, w), f32),
+            jax.ShapeDtypeStruct((ngz, 3, ns, w), f32),
         ],
         scratch_shapes=[pltpu.VMEM((cz, w), jnp.int32), pltpu.VMEM((cz, w), f32)],
-    )(faces, wall_layers, contact, theta, theta, theta, section_store, shifted_inverse, zr)
+    )(faces, wall_layers, contact, theta, theta, theta, section_store, block_inverse, zr)
 
     number = spanwise_number
-    spread = jnp.broadcast_to(mine[None], (ngz,) + mine.shape)
     blocks = lax.all_to_all(spread, "gz", 0, 0, tiled=True)
     left = jnp.roll(blocks[:, 2], 1, axis=0)
     targets = blocks[:, 0] + number[None, :, None] * left + number[None, :, None] * blocks[:, 1]
@@ -265,7 +271,7 @@
     following = jnp.sum(weights(k + 1).T[:, :, None] * targets, axis=0)
 
     fluid_sn, fluid_tn = pl.pallas_call(
-        lambda *refs: layer_kernel(True, nsb, *refs),
+        lambda *refs: layer_kernel(True, nsb, LB, *refs),
         grid=(nfb,),
         in_specs=[smem, smem, smem, blk(nsb), prev_spec(nsb), next_spec(nsb), blk(nsb),
                   blk(nsb), blk(nsb), rows_spec, rows_spec, edge_spec, edge_spec,

time: 52.1 us -> 49.3 us (0.946)
  local copies, waits for them, and re-layouts: 4.95 us -> 3.06 us
  Pallas kernels: 23 us -> 21.9 us
    broadcast_in_dim x1 -> x0, local copies, waits for them, and re-layouts: 1.59 us -> none  [local(): spread = jnp.broadcast_to(mine[None], (ngz,) + mine.shape)]
    pallas_call x2, Pallas kernels: 18 us -> 17 us  [the longest x1 13.7 us: local(): pl.pallas_call(lambda *refs: layer_kernel(True, nsb, LB, *refs), grid=(nf...]
    pad x1 -> x0, local copies, waits for them, and re-layouts: 1 us -> none  [local(): shifted_inverse = jnp.pad(block_inverse, ((0, 0), (1, 0), (1, 0)))]
    unnamed x25, local copies, waits for them, and re-layouts: 1.92 us -> 2.62 us
  transfers between devices with their start and end apart: 5 -> 5, of which waited for: 2 -> 2; matrix products, arithmetic and copies ran while one was open for 11% -> 7% of each run, Pallas kernels for 35% -> 35%
where the time goes in v6:
time: 49.3 us; the launch traced here: 48.8 us
  Pallas kernels  21.9 us (44%)
  starting transfers between devices  12.9 us (26%)
  waiting for transfers between devices  7.36 us (15%)
  local copies, waits for them, and re-layouts  3.06 us (6%)
  other arithmetic  2.63 us (5%)
  between operations  0.83 us (2%)
    pallas_call x1, Pallas kernels, local(): pl.pallas_call(lambda *refs: layer_kernel(True, nsb, LB, *refs), grid=(nf...  13.7 us
    pallas_call x1, Pallas kernels, local(): pl.pallas_call(pack_kernel, grid=(1,), in_specs=[pl.BlockSpec((ny, cz, w)...  4.95 us
    ppermute x1, starting transfers between devices, local(): za = lax.ppermute(zr, 'gz', [((i + 1) % ngz, i) for i in range(ngz)])  4.49 us
    ppermute x1, waiting for transfers between devices, local(): zb = lax.ppermute(zl, 'gz', [(i, (i + 1) % ngz) for i in range(ngz)])  4.45 us
    all_to_all x1, starting transfers between devices, local(): blocks = lax.all_to_all(spread, 'gz', 0, 0, tiled=True)  3.59 us
    ppermute x1, starting transfers between devices, local(): xb = lax.ppermute(xr, 'gx', [(i, i + 1) for i in range(ngx - 1)])  3.44 us
    pallas_call x1, Pallas kernels, local(): pl.pallas_call(lambda *refs: layer_kernel(False, 0, sb, *refs), grid=(ns...  3.29 us
    ppermute x1, waiting for transfers between devices, local(): xa = lax.ppermute(xl, 'gx', [(i + 1, i) for i in range(ngx - 1)])  2.91 us
  transfers between devices with their start and end apart: 5, of which 2 were waited for; matrix products, arithmetic and copies ran while one was open for 7% of the time, Pallas kernels for 35%

profile of v6, /device:TPU:0, one launch (start us, length us, event | category | flops | bytes accessed | tf_op | source)
XLA Modules:
  0.0 48.8 jit_solution(12713561606389749143)
XLA Ops:
  0.6 5.0 %shard_map.104 = (f32[15,8,128]{2,1,0:T(8,128)}, f32[15,8,128]{2,1,0:T(8,128)}, f32[15,8,128]{2,1,0:T(8,128)}, f32[15,8,128]{2,1,0:T(8,128)}, f32[60,8,128]{2,1,0:T(8,128)}, /*index=5*/f32[60,8,128]{2,1,0:T(8,128)}) custom-call(f32[152,32,128]{2,1,0:T(8,128)} %refs_5_.3, bf16[152,32,128]{2,1,0:T(8,128)(2,1)} %refs_7_.2), custom_call_target="tpu_custom_call" | custom-call | tf_op jit(solution)/shard_map/pallas_call | solution.py:216
  5.6 4.5 %collective-permute-start.1 = (f32[60,8,128]{2,1,0:T(8,128)}, f32[60,8,128]{2,1,0:T(8,128)S(1)}, u32[]{:S(2)}, u32[]{:S(2)}) collective-permute-start(f32[60,8,128]{2,1,0:T(8,128)} %get-tuple-element.38.refs_8_), channel_id=1, source_target_pairs={{1,0},{2,1},{3,2},{4,3},{5,4},{6,5},{7,6},{0,7},{9,8},{10,9},{11,1... | collective-permute-start | bytes 737288 | tf_op jit(solution)/shard_map/ppermute | solution.py:229
  10.2 1.1 %copy.22.refs_7_ = f32[32,31,31]{2,1,0:T(8,128)} copy(f32[32,31,31]{2,0,1:T(8,128)S(1)} %copy-done) | data formatting | bytes 246016 | tf_op args[8]
  11.3 0.1 pad_maximum_fusion.3
  11.4 0.1 pad_maximum_fusion.1
  11.4 0.6 %pad_maximum_fusion.refs_0_ = f32[3,153]{1,0:T(4,128)} fusion(f32[1,153]{1,0:T(1,128)S(1)} %bitcast.36, f32[1,153]{1,0:T(1,128)S(1)} %bitcast.37, f32[1,153]{1,0:T(1,128)S(1)} %bitcast.35), kind=kLoop, calls=%fused_computation.29 | loop fusion | flops 918 | bytes 3672 | tf_op jit(solution)/shard_map/stack | solution.py:203
  12.0 3.3 %shard_map.105 = (f32[152,32,128]{2,1,0:T(8,128)}, f32[32,32,128]{2,1,0:T(8,128)}, f32[8,3,32,128]{3,2,1,0:T(8,128)}) custom-call(f32[3,153]{1,0:T(4,128)} %pad_maximum_fusion.refs_0_, s32[32]{0:T(128)} %refs_1_.3, s32[128]{0:T(128)} %refs_2_.3, f32[152,32,128]{2,1,0:T(8,128)} %refs_5_.3, f32[152,32,128]{2,1,0:T(8,128)} %refs_5_.3, f32[152,32,128]{2,1,0:T(8,128)} %refs_5_.3, ...), custom_call_target="tpu_custom_call" | custom-call | tf_op jit(solution)/shard_map/pallas_call | solution.py:234
  15.3 3.6 %all-to-all-start = ((f32[8,3,32,128]{3,2,1,0:T(8,128)}), f32[8,3,32,128]{3,2,1,0:T(8,128)S(1)}, u32[]{:S(2)}, u32[]{:S(2)}) async-start(f32[8,3,32,128]{3,2,1,0:T(8,128)} %get-tuple-element.45), calls=%async_computation | async-start | bytes 786432 | tf_op jit(solution)/shard_map/all_to_all | solution.py:253
  18.9 3.4 %collective-permute-start.2 = (f32[15,8,128]{2,1,0:T(8,128)S(1)}, f32[15,8,128]{2,1,0:T(8,128)S(1)}, u32[]{:S(2)}, u32[]{:S(2)}) collective-permute-start(f32[15,8,128]{2,1,0:T(8,128)S(1)} %copy-done.5), channel_id=1, source_target_pairs={{0,8},{8,16},{16,24},{1,9},{9,17},{17,25},{2,10},{10,18},{18,26},{... | collective-permute-start | bytes 184328 | tf_op jit(solution)/shard_map/ppermute | solution.py:226
  22.4 1.3 %collective-permute-start.3 = (f32[15,8,128]{2,1,0:T(8,128)S(1)}, f32[15,8,128]{2,1,0:T(8,128)S(1)}, u32[]{:S(2)}, u32[]{:S(2)}) collective-permute-start(f32[15,8,128]{2,1,0:T(8,128)S(1)} %copy-done.4), channel_id=1, source_target_pairs={{8,0},{16,8},{24,16},{9,1},{17,9},{25,17},{10,2},{18,10},{26,18},{... | collective-permute-start | bytes 184328 | tf_op jit(solution)/shard_map/ppermute | solution.py:227
  23.7 0.1 collective-permute-start
  23.8 0.2 add_reduce_fusion
  24.0 0.2 fusion.19
  24.4 0.4 copy.29
  24.8 0.4 copy.30
  25.2 0.1 scatter.6
  25.3 0.1 scatter.9
  25.5 0.1 divide_reduce_fusion.1
  25.6 2.9 %collective-permute-done.3.refs_12_ = f32[15,8,128]{2,1,0:T(8,128)S(1)} collective-permute-done((f32[15,8,128]{2,1,0:T(8,128)S(1)}, f32[15,8,128]{2,1,0:T(8,128)S(1)}, u32[]{:S(2)}, u32[]{:S(2)}) %collective-permute-start.3) | collective-permute-done | bytes 61472 | tf_op jit(solution)/shard_map/ppermute | solution.py:227
  28.5 4.4 %collective-permute-done.refs_9_ = f32[60,8,128]{2,1,0:T(8,128)S(1)} collective-permute-done((f32[60,8,128]{2,1,0:T(8,128)S(1)}, f32[60,8,128]{2,1,0:T(8,128)S(1)}, u32[]{:S(2)}, u32[]{:S(2)}) %collective-permute-start) | collective-permute-done | bytes 245792 | tf_op jit(solution)/shard_map/ppermute | solution.py:228
  33.0 0.7 %copy-done.3 = f32[60,8,128]{2,1,0:T(8,128)} copy-done((f32[60,8,128]{2,1,0:T(8,128)}, f32[60,8,128]{2,1,0:T(8,128)S(1)}, u32[]{:S(2)}) %copy-start.3) | copy-done | bytes 245784
  33.7 13.7 %shard_map.106 = (f32[152,32,128]{2,1,0:T(8,128)}, f32[152,32,128]{2,1,0:T(8,128)}) custom-call(f32[3,153]{1,0:T(4,128)} %pad_maximum_fusion.refs_0_, s32[32]{0:T(128)} %refs_1_.3, s32[128]{0:T(128)} %refs_2_.3, f32[152,32,128]{2,1,0:T(8,128)} %refs_5_.3, f32[152,32,128]{2,1,0:T(8,128)} %refs_5_.3, ...), custom_call_target="tpu_custom_call", output_to_operand_aliasing={{0}: (17, {})} | custom-call | tf_op jit(solution)/shard_map/pallas_call | solution.py:273
  47.4 0.1 multiply_reduce_fusion.1
  47.6 1.2 %select_dynamic-update-slice_fusion = f32[152,32,128]{2,1,0:T(8,128)} fusion(f32[152,32,128]{2,1,0:T(8,128)} %get-tuple-element.44, f32[32,32,128]{2,1,0:T(8,128)S(1)} %copy-done.1, f32[32,128]{1,0:T(8,128)S(1)} %get-tuple-element.51, f32[32,32]{1,0:T(8,128)S(1)} %scatter.9, f32[32,32]{1,0:T(8,128)S(1)} %scatter.6, f32[32]{0:T(128)S(1)} %copy-done.9, ...), kind=kLoop, calls=%fused_computation | loop fusion | flops 786432 | bytes 1089696 | tf_op jit(solution)/shard_map/dynamic_update_slice | solution.py:298
  (37 shorter events, 0.4 us)
Async XLA Ops:
  0.6 9.5 %copy-start.8 = (f32[2,152]{1,0:T(2,128)S(1)}, f32[2,152]{1,0:T(2,128)}, u32[]{:S(2)}) copy-start(f32[2,152]{1,0:T(2,128)} %param.17) | copy-start | bytes 3652
  0.6 9.5 %copy-start = (f32[32,31,31]{2,0,1:T(8,128)S(1)}, f32[32,31,31]{2,0,1:T(8,128)}, u32[]{:S(2)}) copy-start(f32[32,31,31]{2,0,1:T(8,128)} %param.21) | copy-start | bytes 369028
  5.6 22.9 %collective-permute-start.1 = (f32[60,8,128]{2,1,0:T(8,128)}, f32[60,8,128]{2,1,0:T(8,128)S(1)}, u32[]{:S(2)}, u32[]{:S(2)}) collective-permute-start(f32[60,8,128]{2,1,0:T(8,128)} %get-tuple-element.38.refs_8_), channel_id=1, source_target_pairs={{1,0},{2,1},{3,2},{4,3},{5,4},{6,5},{7,6},{0,7},{9,8},{10,9},{11,1... | collective-permute-start | bytes 737288 | tf_op jit(solution)/shard_map/ppermute | solution.py:229
  12.0 6.9 %copy-start.5 = (f32[15,8,128]{2,1,0:T(8,128)S(1)}, f32[15,8,128]{2,1,0:T(8,128)}, u32[]{:S(2)}) copy-start(f32[15,8,128]{2,1,0:T(8,128)} %get-tuple-element.39.refs_14_) | copy-start | bytes 184324
  12.0 10.4 %copy-start.4 = (f32[15,8,128]{2,1,0:T(8,128)S(1)}, f32[15,8,128]{2,1,0:T(8,128)}, u32[]{:S(2)}) copy-start(f32[15,8,128]{2,1,0:T(8,128)} %get-tuple-element.40.refs_13_) | copy-start | bytes 184324
  12.0 11.7 %copy-start.10 = (f32[60,8,128]{2,1,0:T(8,128)S(1)}, f32[60,8,128]{2,1,0:T(8,128)}, u32[]{:S(2)}) copy-start(f32[60,8,128]{2,1,0:T(8,128)} %get-tuple-element.37) | copy-start | bytes 737284
  15.3 9.1 %copy-start.9 = (f32[32]{0:T(128)S(1)}, f32[32]{0:T(128)}, u32[]{:S(2)}) copy-start(f32[32]{0:T(128)} %param.20) | copy-start | bytes 388
  15.3 32.0 %all-to-all-start = ((f32[8,3,32,128]{3,2,1,0:T(8,128)}), f32[8,3,32,128]{3,2,1,0:T(8,128)S(1)}, u32[]{:S(2)}, u32[]{:S(2)}) async-start(f32[8,3,32,128]{3,2,1,0:T(8,128)} %get-tuple-element.45), calls=%async_computation | async-start | bytes 786432 | tf_op jit(solution)/shard_map/all_to_all | solution.py:253
  18.9 6.7 %collective-permute-start.2 = (f32[15,8,128]{2,1,0:T(8,128)S(1)}, f32[15,8,128]{2,1,0:T(8,128)S(1)}, u32[]{:S(2)}, u32[]{:S(2)}) collective-permute-start(f32[15,8,128]{2,1,0:T(8,128)S(1)} %copy-done.5), channel_id=1, source_target_pairs={{0,8},{8,16},{16,24},{1,9},{9,17},{17,25},{2,10},{10,18},{18,26},{... | collective-permute-start | bytes 184328 | tf_op jit(solution)/shard_map/ppermute | solution.py:226
  22.4 6.1 %collective-permute-start.3 = (f32[15,8,128]{2,1,0:T(8,128)S(1)}, f32[15,8,128]{2,1,0:T(8,128)S(1)}, u32[]{:S(2)}, u32[]{:S(2)}) collective-permute-start(f32[15,8,128]{2,1,0:T(8,128)S(1)} %copy-done.4), channel_id=1, source_target_pairs={{8,0},{16,8},{24,16},{9,1},{17,9},{25,17},{10,2},{18,10},{26,18},{... | collective-permute-start | bytes 184328 | tf_op jit(solution)/shard_map/ppermute | solution.py:227
  23.7 9.3 %collective-permute-start = (f32[60,8,128]{2,1,0:T(8,128)S(1)}, f32[60,8,128]{2,1,0:T(8,128)S(1)}, u32[]{:S(2)}, u32[]{:S(2)}) collective-permute-start(f32[60,8,128]{2,1,0:T(8,128)S(1)} %copy-done.10), channel_id=1, source_target_pairs={{0,1},{1,2},{2,3},{3,4},{4,5},{5,6},{6,7},{7,0},{8,9},{9,10},{10,1... | collective-permute-start | bytes 737288 | tf_op jit(solution)/shard_map/ppermute | solution.py:228
  25.6 7.4 %copy-start.6 = (f32[15,8,128]{2,1,0:T(8,128)}, f32[15,8,128]{2,1,0:T(8,128)S(1)}, u32[]{:S(2)}) copy-start(f32[15,8,128]{2,1,0:T(8,128)S(1)} %collective-permute-done.2.refs_11_) | copy-start | bytes 184324
  28.5 4.5 %copy-start.7 = (f32[15,8,128]{2,1,0:T(8,128)}, f32[15,8,128]{2,1,0:T(8,128)S(1)}, u32[]{:S(2)}) copy-start(f32[15,8,128]{2,1,0:T(8,128)S(1)} %collective-permute-done.3.refs_12_) | copy-start | bytes 184324
  28.5 4.5 %copy-start.2 = (f32[60,8,128]{2,1,0:T(8,128)}, f32[60,8,128]{2,1,0:T(8,128)S(1)}, u32[]{:S(2)}) copy-start(f32[60,8,128]{2,1,0:T(8,128)S(1)} %collective-permute-done.1.refs_10_) | copy-start | bytes 737284
  33.0 0.7 %copy-start.3 = (f32[60,8,128]{2,1,0:T(8,128)}, f32[60,8,128]{2,1,0:T(8,128)S(1)}, u32[]{:S(2)}) copy-start(f32[60,8,128]{2,1,0:T(8,128)S(1)} %collective-permute-done.refs_9_) | copy-start | bytes 737284
  33.7 13.9 %copy-start.1 = (f32[32,32,128]{2,1,0:T(8,128)S(1)}, f32[32,32,128]{2,1,0:T(8,128)}, u32[]{:S(2)}) copy-start(f32[32,32,128]{2,1,0:T(8,128)} %get-tuple-element.46) | copy-start | bytes 1572868

commit v7 on v6

--- a/solution.py
+++ b/solution.py
@@ -16,12 +16,11 @@
 LB = 8
 
 
-def pack_kernel(th_ref, u_ref, xl_ref, xr_ref, ul_ref, ur_ref, zl_ref, zr_ref):
+def pack_kernel(th_ref, u_ref, xl_ref, xr_ref, ul_ref, ur_ref):
     ny, cz, w = th_ref.shape
     nblocks = xl_ref.shape[0]
     skip = ny - nblocks * LB
     lane8 = lax.broadcasted_iota(jnp.int32, (8, w), 1)
-    sub8 = lax.broadcasted_iota(jnp.int32, (8, w), 0)
 
     def block(b, carry):
         first = skip + b * LB
@@ -46,13 +45,6 @@
         xr_ref[b] = acc_r
         ul_ref[b] = uacc_l
         ur_ref[b] = uacc_r
-        for p in range(LB // 2):
-            a_hi = th_ref[first + 2 * p, cz - 8:cz, :]
-            b_hi = th_ref[first + 2 * p + 1, cz - 8:cz, :]
-            zl_ref[b * (LB // 2) + p] = jnp.where(sub8 < 4, pltpu.roll(a_hi, 4, 0), b_hi)
-            a_lo = th_ref[first + 2 * p, 0:8, :]
-            b_lo = th_ref[first + 2 * p + 1, 0:8, :]
-            zr_ref[b * (LB // 2) + p] = jnp.where(sub8 < 4, a_lo, pltpu.roll(b_lo, 4, 0))
         return carry
 
     lax.fori_loop(0, nblocks, block, 0)
@@ -137,15 +129,9 @@
                 picked = jnp.where(at_l, fix_l, jnp.where(at_r, fix_r, 0.0))
                 fixes.append(pltpu.roll(picked, (w - pos) % w, 1))
             fix = jnp.concatenate(fixes, axis=0)
-            packed_b = zb_ref[s // 2]
-            packed_a = za_ref[s // 2]
-            if s % 2 == 0:
-                packed_b = pltpu.roll(packed_b, 4, 0)
-            else:
-                packed_a = pltpu.roll(packed_a, 4, 0)
-            ext_ref[0:8, :] = packed_b
+            ext_ref[0:8, :] = zb_ref[s]
             ext_ref[8:8 + cz, :] = t
-            ext_ref[8 + cz:16 + cz, :] = packed_a
+            ext_ref[8 + cz:16 + cz, :] = za_ref[s]
             zm = [None] + [ext_ref[8 - j:8 - j + cz, :] for j in range(1, 5)]
             zp = [None] + [ext_ref[8 + j:8 + j + cz, :] for j in range(1, 5)]
 
@@ -211,23 +197,21 @@
     prev_spec = lambda off: pl.BlockSpec((1, cz, w), lambda i: (jnp.maximum((i + off) * LB - 1, 0), 0, 0))
     next_spec = lambda off: pl.BlockSpec((1, cz, w), lambda i: (jnp.minimum((i + off) * LB + LB, ny - 1), 0, 0))
     edge_spec = pl.BlockSpec((1, 8, w), lambda i: (i, 0, 0))
-    rows_spec = pl.BlockSpec((LB // 2, 8, w), lambda i: (i, 0, 0))
-
-    xl, xr, ul, ur, zl, zr = pl.pallas_call(
+    rows_spec = pl.BlockSpec((LB, 8, w), lambda i: (i, 0, 0))
+
+    zb = lax.ppermute(theta[ns:, cz - 8:, :], "gz", [(i, (i + 1) % ngz) for i in range(ngz)])
+    za = lax.ppermute(theta[ns:, :8, :], "gz", [((i + 1) % ngz, i) for i in range(ngz)])
+
+    xl, xr, ul, ur = pl.pallas_call(
         pack_kernel,
         grid=(1,),
         in_specs=[pl.BlockSpec((ny, cz, w), lambda i: (0, 0, 0))] * 2,
-        out_specs=[pl.BlockSpec((nfb, 8, w), lambda i: (0, 0, 0))] * 4
-        + [pl.BlockSpec((nf // 2, 8, w), lambda i: (0, 0, 0))] * 2,
-        out_shape=[jax.ShapeDtypeStruct((nfb, 8, w), f32)] * 4
-        + [jax.ShapeDtypeStruct((nf // 2, 8, w), f32)] * 2,
+        out_specs=[pl.BlockSpec((nfb, 8, w), lambda i: (0, 0, 0))] * 4,
+        out_shape=[jax.ShapeDtypeStruct((nfb, 8, w), f32)] * 4,
     )(theta, stream_speed)
 
     xb = lax.ppermute(xr, "gx", [(i, i + 1) for i in range(ngx - 1)])
     xa = lax.ppermute(xl, "gx", [(i + 1, i) for i in range(ngx - 1)])
-    zb = lax.ppermute(zl, "gz", [(i, (i + 1) % ngz) for i in range(ngz)])
-    za = lax.ppermute(zr, "gz", [((i + 1) % ngz, i) for i in range(ngz)])
-
 
     sb = 2 * LB if ns % (2 * LB) == 0 else LB
     sblk = pl.BlockSpec((sb, cz, w), lambda i: (i, 0, 0))
@@ -247,7 +231,7 @@
             jax.ShapeDtypeStruct((ngz, 3, ns, w), f32),
         ],
         scratch_shapes=[pltpu.VMEM((cz, w), jnp.int32), pltpu.VMEM((cz, w), f32)],
-    )(faces, wall_layers, contact, theta, theta, theta, section_store, block_inverse, zr)
+    )(faces, wall_layers, contact, theta, theta, theta, section_store, block_inverse, xr)
 
     number = spanwise_number
     blocks = lax.all_to_all(spread, "gz", 0, 0, tiled=True)

time: 49.3 us -> 58.5 us (1.19)
  waiting for transfers between devices: 7.36 us -> 12.8 us
  local copies, waits for them, and re-layouts: 3.06 us -> 5.36 us
  starting transfers between devices: 12.9 us -> 14.7 us
    ppermute x2, waiting for transfers between devices: 4.45 us -> 12.8 us  [the longest x1 12.8 us: local(): lax.ppermute(theta[ns:, cz - 8:, :], 'gz', [(i, (i + 1) % ngz) for i in r...]
    ppermute x1, waiting for transfers between devices: 2.91 us -> 0.01 us  [local(): xa = lax.ppermute(xl, 'gx', [(i + 1, i) for i in range(ngx - 1)])]
    slice x0 -> x1, local copies, waits for them, and re-layouts: none -> 2.03 us  [local(): theta[ns:, :8, :]]
    all_to_all x1, starting transfers between devices: 3.59 us -> 5.01 us  [local(): blocks = lax.all_to_all(spread, 'gz', 0, 0, tiled=True)]
    ppermute x1, starting transfers between devices: 3.44 us -> 4.83 us  [local(): xb = lax.ppermute(xr, 'gx', [(i, i + 1) for i in range(ngx - 1)])]
    ppermute x2, starting transfers between devices: 4.62 us -> 3.56 us  [the longest x1 3.07 us: local(): lax.ppermute(theta[ns:, :8, :], 'gz', [((i + 1) % ngz, i) for i in range(...]
    unnamed x25 -> x19, local copies, waits for them, and re-layouts: 2.62 us -> 2.89 us
  transfers between devices with their start and end apart: 5 -> 5, of which waited for: 2 -> 1; matrix products, arithmetic and copies ran while one was open for 7% -> 10% of each run, Pallas kernels for 35% -> 29%
where the time goes in v7:
time: 58.5 us; the launch traced here: 57.9 us
  Pallas kernels  21.7 us (37%)
  starting transfers between devices  14.7 us (25%)
  waiting for transfers between devices  12.8 us (22%)
  local copies, waits for them, and re-layouts  5.36 us (9%)
  other arithmetic  2.63 us (4%)
  between operations  0.81 us (1%)
    pallas_call x1, Pallas kernels, local(): pl.pallas_call(lambda *refs: layer_kernel(True, nsb, LB, *refs), grid=(nf...  13.6 us
    ppermute x1, waiting for transfers between devices, local(): lax.ppermute(theta[ns:, cz - 8:, :], 'gz', [(i, (i + 1) % ngz) for i in r...  12.8 us
    all_to_all x1, starting transfers between devices, local(): blocks = lax.all_to_all(spread, 'gz', 0, 0, tiled=True)  5.01 us
    ppermute x1, starting transfers between devices, local(): xb = lax.ppermute(xr, 'gx', [(i, i + 1) for i in range(ngx - 1)])  4.83 us
    pallas_call x1, Pallas kernels, local(): pl.pallas_call(pack_kernel, grid=(1,), in_specs=[pl.BlockSpec((ny, cz, w)...  4.82 us
    pallas_call x1, Pallas kernels, local(): pl.pallas_call(lambda *refs: layer_kernel(False, 0, sb, *refs), grid=(ns...  3.22 us
    ppermute x1, starting transfers between devices, local(): lax.ppermute(theta[ns:, :8, :], 'gz', [((i + 1) % ngz, i) for i in range(...  3.07 us
    unnamed x19, local copies, waits for them, and re-layouts  2.89 us
  transfers between devices with their start and end apart: 5, of which 1 were waited for; matrix products, arithmetic and copies ran while one was open for 10% of the time, Pallas kernels for 29%

profile of v7, /device:TPU:0, one launch (start us, length us, event | category | flops | bytes accessed | tf_op | source)
XLA Modules:
  0.0 57.9 jit_solution(13331309613442105718)
XLA Ops:
  0.6 4.8 %shard_map.104 = (f32[15,8,128]{2,1,0:T(8,128)}, f32[15,8,128]{2,1,0:T(8,128)}, f32[15,8,128]{2,1,0:T(8,128)}, f32[15,8,128]{2,1,0:T(8,128)}) custom-call(f32[152,32,128]{2,1,0:T(8,128)} %refs_5_.3, bf16[152,32,128]{2,1,0:T(8,128)(2,1)} %refs_7_.2), custom_call_target="tpu_custom_call" | custom-call | tf_op jit(solution)/shard_map/pallas_call | solution.py:205
  5.5 4.8 %collective-permute-start.2 = (f32[15,8,128]{2,1,0:T(8,128)}, f32[15,8,128]{2,1,0:T(8,128)S(1)}, u32[]{:S(2)}, u32[]{:S(2)}) collective-permute-start(f32[15,8,128]{2,1,0:T(8,128)} %get-tuple-element.35.refs_8_.refs_14_), channel_id=1, source_target_pairs={{0,8},{8,16},{16,24},{1,9},{9,17},{17,25},{2,10},{10,18},{18,26},{... | collective-permute-start | bytes 184328 | tf_op jit(solution)/shard_map/ppermute | solution.py:213
  10.3 0.1 fusion.21
  10.4 1.1 %copy.22.refs_7_ = f32[32,31,31]{2,1,0:T(8,128)} copy(f32[32,31,31]{2,0,1:T(8,128)S(1)} %copy-done) | data formatting | bytes 246016 | tf_op args[8]
  11.5 0.1 pad_maximum_fusion.3
  11.6 0.1 pad_maximum_fusion.1
  11.7 0.6 %pad_maximum_fusion.refs_0_ = f32[3,153]{1,0:T(4,128)} fusion(f32[1,153]{1,0:T(1,128)S(1)} %bitcast.36, f32[1,153]{1,0:T(1,128)S(1)} %bitcast.37, f32[1,153]{1,0:T(1,128)S(1)} %bitcast.35), kind=kLoop, calls=%fused_computation.29 | loop fusion | flops 918 | bytes 3672 | tf_op jit(solution)/shard_map/stack | solution.py:189
  12.3 3.2 %shard_map.105 = (f32[152,32,128]{2,1,0:T(8,128)}, f32[32,32,128]{2,1,0:T(8,128)}, f32[8,3,32,128]{3,2,1,0:T(8,128)}) custom-call(f32[3,153]{1,0:T(4,128)} %pad_maximum_fusion.refs_0_, s32[32]{0:T(128)} %refs_1_.3, s32[128]{0:T(128)} %refs_2_.3, f32[152,32,128]{2,1,0:T(8,128)} %refs_5_.3, f32[152,32,128]{2,1,0:T(8,128)} %refs_5_.3, f32[152,32,128]{2,1,0:T(8,128)} %refs_5_.3, ...), custom_call_target="tpu_custom_call" | custom-call | tf_op jit(solution)/shard_map/pallas_call | solution.py:218
  15.5 5.0 %all-to-all-start = ((f32[8,3,32,128]{3,2,1,0:T(8,128)}), f32[8,3,32,128]{3,2,1,0:T(8,128)S(1)}, u32[]{:S(2)}, u32[]{:S(2)}) async-start(f32[8,3,32,128]{3,2,1,0:T(8,128)} %get-tuple-element.41), calls=%async_computation | async-start | bytes 786432 | tf_op jit(solution)/shard_map/all_to_all | solution.py:237
  20.5 1.3 %collective-permute-start.3 = (f32[15,8,128]{2,1,0:T(8,128)S(1)}, f32[15,8,128]{2,1,0:T(8,128)}, u32[]{:S(2)}, u32[]{:S(2)}) collective-permute-start(f32[15,8,128]{2,1,0:T(8,128)S(1)} %copy-done.4), channel_id=1, source_target_pairs={{8,0},{16,8},{24,16},{9,1},{17,9},{25,17},{10,2},{18,10},{26,18},{... | collective-permute-start | bytes 184328 | tf_op jit(solution)/shard_map/ppermute | solution.py:214
  21.8 2.0 %fusion.19 = (f32[120,8,128]{2,1,0:T(8,128)S(1)}, f32[120,8,128]{2,1,0:T(8,128)}) fusion(f32[152,32,128]{2,1,0:T(8,128)} %refs_5_.3), kind=kLoop, calls=%fused_computation.60 | loop fusion | bytes 1966080 | tf_op jit(solution)/shard_map/slice | solution.py:203
  23.8 0.5 collective-permute-start
  24.3 3.1 %collective-permute-start.1 = (f32[120,8,128]{2,1,0:T(8,128)S(1)}, f32[120,8,128]{2,1,0:T(8,128)S(1)}, u32[]{:S(2)}, u32[]{:S(2)}) collective-permute-start(f32[120,8,128]{2,1,0:T(8,128)S(1)} %get-tuple-element.50), channel_id=1, source_target_pairs={{1,0},{2,1},{3,2},{4,3},{5,4},{6,5},{7,6},{0,7},{9,8},{10,9},{11,1... | collective-permute-start | bytes 1474568 | tf_op jit(solution)/shard_map/ppermute | solution.py:203
  27.4 0.2 add_reduce_fusion
  27.6 0.2 fusion.20
  28.1 0.4 copy.29
  28.5 0.4 copy.30
  29.0 0.1 divide_reduce_fusion.1
  29.2 12.8 %collective-permute-done.refs_9_ = f32[120,8,128]{2,1,0:T(8,128)S(1)} collective-permute-done((f32[120,8,128]{2,1,0:T(8,128)}, f32[120,8,128]{2,1,0:T(8,128)S(1)}, u32[]{:S(2)}, u32[]{:S(2)}) %collective-permute-start) | collective-permute-done | bytes 491552 | tf_op jit(solution)/shard_map/ppermute | solution.py:202
  42.0 0.8 %copy-done.2 = f32[120,8,128]{2,1,0:T(8,128)} copy-done((f32[120,8,128]{2,1,0:T(8,128)}, f32[120,8,128]{2,1,0:T(8,128)S(1)}, u32[]{:S(2)}) %copy-start.2) | copy-done | bytes 491544
  42.8 0.2 copy-done.3
  42.9 13.6 %shard_map.106 = (f32[152,32,128]{2,1,0:T(8,128)}, f32[152,32,128]{2,1,0:T(8,128)}) custom-call(f32[3,153]{1,0:T(4,128)} %pad_maximum_fusion.refs_0_, s32[32]{0:T(128)} %refs_1_.3, s32[128]{0:T(128)} %refs_2_.3, f32[152,32,128]{2,1,0:T(8,128)} %refs_5_.3, f32[152,32,128]{2,1,0:T(8,128)} %refs_5_.3, ...), custom_call_target="tpu_custom_call", output_to_operand_aliasing={{0}: (17, {})} | custom-call | tf_op jit(solution)/shard_map/pallas_call | solution.py:257
  56.6 0.1 multiply_reduce_fusion.1
  56.7 1.2 %select_dynamic-update-slice_fusion = f32[152,32,128]{2,1,0:T(8,128)} fusion(f32[152,32,128]{2,1,0:T(8,128)} %get-tuple-element.40, f32[32,32,128]{2,1,0:T(8,128)S(1)} %copy-done.1, f32[32,128]{1,0:T(8,128)S(1)} %get-tuple-element.47, f32[32,32]{1,0:T(8,128)S(1)} %scatter.9, f32[32,32]{1,0:T(8,128)S(1)} %scatter.6, f32[32]{0:T(128)S(1)} %copy-done.7, ...), kind=kLoop, calls=%fused_computation | loop fusion | flops 786432 | bytes 1089696 | tf_op jit(solution)/shard_map/dynamic_update_slice | solution.py:282
  (32 shorter events, 0.5 us)
Async XLA Ops:
  0.6 9.7 %copy-start.6 = (f32[2,152]{1,0:T(2,128)S(1)}, f32[2,152]{1,0:T(2,128)}, u32[]{:S(2)}) copy-start(f32[2,152]{1,0:T(2,128)} %param.17) | copy-start | bytes 3652
  0.6 9.8 %copy-start = (f32[32,31,31]{2,0,1:T(8,128)S(1)}, f32[32,31,31]{2,0,1:T(8,128)}, u32[]{:S(2)}) copy-start(f32[32,31,31]{2,0,1:T(8,128)} %param.21) | copy-start | bytes 369028
  5.5 23.7 %collective-permute-start.2 = (f32[15,8,128]{2,1,0:T(8,128)}, f32[15,8,128]{2,1,0:T(8,128)S(1)}, u32[]{:S(2)}, u32[]{:S(2)}) collective-permute-start(f32[15,8,128]{2,1,0:T(8,128)} %get-tuple-element.35.refs_8_.refs_14_), channel_id=1, source_target_pairs={{0,8},{8,16},{16,24},{1,9},{9,17},{17,25},{2,10},{10,18},{18,26},{... | collective-permute-start | bytes 184328 | tf_op jit(solution)/shard_map/ppermute | solution.py:213
  12.3 8.2 %copy-start.4 = (f32[15,8,128]{2,1,0:T(8,128)S(1)}, f32[15,8,128]{2,1,0:T(8,128)}, u32[]{:S(2)}) copy-start(f32[15,8,128]{2,1,0:T(8,128)} %get-tuple-element.36.refs_13_) | copy-start | bytes 184324
  15.5 12.4 %copy-start.7 = (f32[32]{0:T(128)S(1)}, f32[32]{0:T(128)}, u32[]{:S(2)}) copy-start(f32[32]{0:T(128)} %param.20) | copy-start | bytes 388
  15.5 41.1 %all-to-all-start = ((f32[8,3,32,128]{3,2,1,0:T(8,128)}), f32[8,3,32,128]{3,2,1,0:T(8,128)S(1)}, u32[]{:S(2)}, u32[]{:S(2)}) async-start(f32[8,3,32,128]{3,2,1,0:T(8,128)} %get-tuple-element.41), calls=%async_computation | async-start | bytes 786432 | tf_op jit(solution)/shard_map/all_to_all | solution.py:237
  20.5 8.7 %collective-permute-start.3 = (f32[15,8,128]{2,1,0:T(8,128)S(1)}, f32[15,8,128]{2,1,0:T(8,128)}, u32[]{:S(2)}, u32[]{:S(2)}) collective-permute-start(f32[15,8,128]{2,1,0:T(8,128)S(1)} %copy-done.4), channel_id=1, source_target_pairs={{8,0},{16,8},{24,16},{9,1},{17,9},{25,17},{10,2},{18,10},{26,18},{... | collective-permute-start | bytes 184328 | tf_op jit(solution)/shard_map/ppermute | solution.py:214
  23.8 18.1 %collective-permute-start = (f32[120,8,128]{2,1,0:T(8,128)}, f32[120,8,128]{2,1,0:T(8,128)S(1)}, u32[]{:S(2)}, u32[]{:S(2)}) collective-permute-start(f32[120,8,128]{2,1,0:T(8,128)} %get-tuple-element.51), channel_id=1, source_target_pairs={{0,1},{1,2},{2,3},{3,4},{4,5},{5,6},{6,7},{7,0},{8,9},{9,10},{10,1... | collective-permute-start | bytes 1474568 | tf_op jit(solution)/shard_map/ppermute | solution.py:202
  24.3 17.7 %collective-permute-start.1 = (f32[120,8,128]{2,1,0:T(8,128)S(1)}, f32[120,8,128]{2,1,0:T(8,128)S(1)}, u32[]{:S(2)}, u32[]{:S(2)}) collective-permute-start(f32[120,8,128]{2,1,0:T(8,128)S(1)} %get-tuple-element.50), channel_id=1, source_target_pairs={{1,0},{2,1},{3,2},{4,3},{5,4},{6,5},{7,6},{0,7},{9,8},{10,9},{11,1... | collective-permute-start | bytes 1474568 | tf_op jit(solution)/shard_map/ppermute | solution.py:203
  29.2 12.8 %copy-start.5 = (f32[15,8,128]{2,1,0:T(8,128)}, f32[15,8,128]{2,1,0:T(8,128)S(1)}, u32[]{:S(2)}) copy-start(f32[15,8,128]{2,1,0:T(8,128)S(1)} %collective-permute-done.2.refs_11_) | copy-start | bytes 184324
  42.0 0.8 %copy-start.2 = (f32[120,8,128]{2,1,0:T(8,128)}, f32[120,8,128]{2,1,0:T(8,128)S(1)}, u32[]{:S(2)}) copy-start(f32[120,8,128]{2,1,0:T(8,128)S(1)} %collective-permute-done.refs_9_) | copy-start | bytes 1474564
  42.0 0.9 %copy-start.3 = (f32[120,8,128]{2,1,0:T(8,128)}, f32[120,8,128]{2,1,0:T(8,128)S(1)}, u32[]{:S(2)}) copy-start(f32[120,8,128]{2,1,0:T(8,128)S(1)} %collective-permute-done.1.refs_10_) | copy-start | bytes 1474564
  42.9 13.8 %copy-start.1 = (f32[32,32,128]{2,1,0:T(8,128)S(1)}, f32[32,32,128]{2,1,0:T(8,128)}, u32[]{:S(2)}) copy-start(f32[32,32,128]{2,1,0:T(8,128)} %get-tuple-element.42) | copy-start | bytes 1572868

commit v8 on v6

--- a/solution.py
+++ b/solution.py
@@ -61,7 +61,7 @@
 def layer_kernel(fluid, block_offset, lb, *refs):
     if fluid:
         (face_ref, wall_ref, contact_ref, th_ref, prev_ref, next_ref, st_ref,
-         u_ref, v_ref, zb_ref, za_ref, xb_ref, xa_ref, xl_ref, xr_ref, ul_ref, ur_ref,
+         u_ref, v_ref, xb_ref, xa_ref, xl_ref, xr_ref, ul_ref, ur_ref,
          _alias_ref, sn_ref, tn_ref, wallv_ref, contv_ref, ext_ref) = refs
     else:
         (face_ref, wall_ref, contact_ref, th_ref, prev_ref, next_ref, st_ref,
@@ -137,15 +137,9 @@
                 picked = jnp.where(at_l, fix_l, jnp.where(at_r, fix_r, 0.0))
                 fixes.append(pltpu.roll(picked, (w - pos) % w, 1))
             fix = jnp.concatenate(fixes, axis=0)
-            packed_b = zb_ref[s // 2]
-            packed_a = za_ref[s // 2]
-            if s % 2 == 0:
-                packed_b = pltpu.roll(packed_b, 4, 0)
-            else:
-                packed_a = pltpu.roll(packed_a, 4, 0)
-            ext_ref[0:8, :] = packed_b
+            ext_ref[0:8, :] = t[cz - 8:]
             ext_ref[8:8 + cz, :] = t
-            ext_ref[8 + cz:16 + cz, :] = packed_a
+            ext_ref[8 + cz:16 + cz, :] = t[:8]
             zm = [None] + [ext_ref[8 - j:8 - j + cz, :] for j in range(1, 5)]
             zp = [None] + [ext_ref[8 + j:8 + j + cz, :] for j in range(1, 5)]
 
@@ -181,6 +175,74 @@
                 mine_ref[n, part] = rows
 
 
+def span_fix_kernel(wall_ref, zb_ref, za_ref, zl_ref, zr_ref, v_ref, sn_in, tn_in,
+                    sn_out, tn_out, top_sn, bot_sn, top_tn, bot_tn, sems):
+    ny, cz, w = v_ref.shape
+    nf = top_sn.shape[0]
+    ns = ny - nf
+    loads = [
+        pltpu.make_async_copy(sn_in.at[pl.ds(ns, nf), pl.ds(0, 8), :], top_sn, sems.at[0]),
+        pltpu.make_async_copy(sn_in.at[pl.ds(ns, nf), pl.ds(cz - 8, 8), :], bot_sn, sems.at[1]),
+        pltpu.make_async_copy(tn_in.at[pl.ds(ns, nf), pl.ds(0, 8), :], top_tn, sems.at[2]),
+        pltpu.make_async_copy(tn_in.at[pl.ds(ns, nf), pl.ds(cz - 8, 8), :], bot_tn, sems.at[3]),
+    ]
+    for c in loads:
+        c.start()
+    sub = lax.broadcasted_iota(jnp.int32, (8, w), 0)
+    wall_top = jnp.zeros((8, w), jnp.int32)
+    wall_bot = jnp.zeros((8, w), jnp.int32)
+    for z in range(8):
+        wall_top = jnp.where(sub == z, wall_ref[z], wall_top)
+        wall_bot = jnp.where(sub == z, wall_ref[cz - 8 + z], wall_bot)
+    slope_scale = -span_courant / 60.0
+    for c in loads:
+        c.wait()
+
+    def pair(p, carry):
+        miss_top = zb_ref[p] - zl_ref[p]
+        miss_bot = za_ref[p] - zr_ref[p]
+        for h in range(2):
+            f = 2 * p + h
+            y = ns + f
+            d_top = pltpu.roll(miss_top, 4, 0) if h == 0 else miss_top
+            d_top = jnp.where(sub >= 4, d_top, 0.0)
+            d_bot = miss_bot if h == 0 else pltpu.roll(miss_bot, 4, 0)
+            d_bot = jnp.where(sub < 4, d_bot, 0.0)
+            s_top = jnp.zeros((8, w), jnp.float32)
+            m_top = jnp.zeros((8, w), jnp.float32)
+            s_bot = jnp.zeros((8, w), jnp.float32)
+            m_bot = jnp.zeros((8, w), jnp.float32)
+            for j, cs, cm in ((1, -45.0, -56.0), (2, 9.0, 28.0), (3, -1.0, -8.0), (4, 0.0, 1.0)):
+                lo = jnp.where(sub < j, pltpu.roll(d_top, j, 0), 0.0)
+                hi = jnp.where(sub >= 8 - j, pltpu.roll(d_bot, 8 - j, 0), 0.0)
+                if cs != 0.0:
+                    s_top = s_top + cs * lo
+                    s_bot = s_bot - cs * hi
+                m_top = m_top + cm * lo
+                m_bot = m_bot + cm * hi
+            v_top = v_ref[y, 0:8, :].astype(jnp.float32)
+            v_bot = v_ref[y, cz - 8:cz, :].astype(jnp.float32)
+            fix_top = jnp.where(y >= wall_top, slope_scale * v_top * s_top - damping * m_top, 0.0)
+            fix_bot = jnp.where(y >= wall_bot, slope_scale * v_bot * s_bot - damping * m_bot, 0.0)
+            top_sn[f] = top_sn[f] + fix_top
+            bot_sn[f] = bot_sn[f] + fix_bot
+            top_tn[f] = top_tn[f] + section_weight * fix_top
+            bot_tn[f] = bot_tn[f] + section_weight * fix_bot
+        return carry
+
+    lax.fori_loop(0, nf // 2, pair, 0)
+    stores = [
+        pltpu.make_async_copy(top_sn, sn_out.at[pl.ds(ns, nf), pl.ds(0, 8), :], sems.at[4]),
+        pltpu.make_async_copy(bot_sn, sn_out.at[pl.ds(ns, nf), pl.ds(cz - 8, 8), :], sems.at[5]),
+        pltpu.make_async_copy(top_tn, tn_out.at[pl.ds(ns, nf), pl.ds(0, 8), :], sems.at[6]),
+        pltpu.make_async_copy(bot_tn, tn_out.at[pl.ds(ns, nf), pl.ds(cz - 8, 8), :], sems.at[7]),
+    ]
+    for c in stores:
+        c.start()
+    for c in stores:
+        c.wait()
+
+
 def local(theta, section_store, stream_speed, span_speed, conductivity, wall_layers,
           contact, spanwise_number, block_inverse):
     f32 = jnp.float32
@@ -274,7 +336,7 @@
         lambda *refs: layer_kernel(True, nsb, LB, *refs),
         grid=(nfb,),
         in_specs=[smem, smem, smem, blk(nsb), prev_spec(nsb), next_spec(nsb), blk(nsb),
-                  blk(nsb), blk(nsb), rows_spec, rows_spec, edge_spec, edge_spec,
+                  blk(nsb), blk(nsb), edge_spec, edge_spec,
                   edge_spec, edge_spec, edge_spec, edge_spec,
                   pl.BlockSpec(memory_space=pl.ANY)],
         out_specs=[blk(nsb), blk(nsb)],
@@ -284,9 +346,21 @@
         ],
         scratch_shapes=[pltpu.VMEM((cz, w), jnp.int32), pltpu.VMEM((cz, w), f32),
                         pltpu.VMEM((cz + 16, w), f32)],
-        input_output_aliases={17: 0},
+        input_output_aliases={15: 0},
     )(faces, wall_layers, contact, theta, theta, theta, section_store,
-      stream_speed, span_speed, zb, za, xb, xa, xl, xr, ul, ur, sn_part)
+      stream_speed, span_speed, xb, xa, xl, xr, ul, ur, sn_part)
+
+    anyspec = pl.BlockSpec(memory_space=pl.ANY)
+    whole = lambda shape: pl.BlockSpec(shape, lambda i: (0,) * len(shape))
+    fluid_sn, fluid_tn = pl.pallas_call(
+        span_fix_kernel,
+        grid=(1,),
+        in_specs=[smem] + [whole((nf // 2, 8, w))] * 4 + [whole((ny, cz, w)), anyspec, anyspec],
+        out_specs=[anyspec, anyspec],
+        out_shape=[jax.ShapeDtypeStruct((ny, cz, w), f32)] * 2,
+        scratch_shapes=[pltpu.VMEM((nf, 8, w), f32)] * 4 + [pltpu.SemaphoreType.DMA((8,))],
+        input_output_aliases={6: 0, 7: 1},
+    )(wall_layers, zb, za, zl, zr, span_speed, fluid_sn, fluid_tn)
 
     row = jnp.arange(cz, dtype=jnp.int32)
     col0 = jnp.zeros((ns, cz), f32).at[:, 1:].set(block_inverse[:, :, 0])

time: 49.3 us -> 50.2 us (1.018)
  the two profiles are of different devices: /device:TPU:0 before, /device:TPU:5 now
where the time goes in v8:
time: 50.2 us; the launch traced here: 49.5 us
  Pallas kernels  27.8 us (55%)
  starting transfers between devices  14.5 us (29%)
  local copies, waits for them, and re-layouts  3.73 us (7%)
  other arithmetic  2.63 us (5%)
  between operations  0.85 us (2%)
    pallas_call x1, Pallas kernels, local(): pl.pallas_call(lambda *refs: layer_kernel(True, nsb, LB, *refs), grid=(nf...  13.5 us
    pallas_call x1, Pallas kernels, local(): pl.pallas_call(span_fix_kernel, grid=(1,), in_specs=[smem] + [whole((nf /...  6.2 us
    all_to_all x1, starting transfers between devices, local(): blocks = lax.all_to_all(spread, 'gz', 0, 0, tiled=True)  5.84 us
    pallas_call x1, Pallas kernels, local(): pl.pallas_call(pack_kernel, grid=(1,), in_specs=[pl.BlockSpec((ny, cz, w)...  4.97 us
    unnamed x19, local copies, waits for them, and re-layouts  3.29 us
    pallas_call x1, Pallas kernels, local(): pl.pallas_call(lambda *refs: layer_kernel(False, 0, sb, *refs), grid=(ns...  3.18 us
    ppermute x1, starting transfers between devices, local(): xb = lax.ppermute(xr, 'gx', [(i, i + 1) for i in range(ngx - 1)])  3.11 us
    ppermute x1, starting transfers between devices, local(): xa = lax.ppermute(xl, 'gx', [(i + 1, i) for i in range(ngx - 1)])  3.06 us
  transfers between devices with their start and end apart: 5, of which 0 were waited for; matrix products, arithmetic and copies ran while one was open for 7% of the time, Pallas kernels for 46%

profile of v8, /device:TPU:5, one launch (start us, length us, event | category | flops | bytes accessed | tf_op | source)
XLA Modules:
  0.0 49.5 jit_solution(2446055600245941867)
XLA Ops:
  0.6 5.0 %shard_map.104 = (f32[15,8,128]{2,1,0:T(8,128)}, f32[15,8,128]{2,1,0:T(8,128)}, f32[15,8,128]{2,1,0:T(8,128)}, f32[15,8,128]{2,1,0:T(8,128)}, f32[60,8,128]{2,1,0:T(8,128)}, /*index=5*/f32[60,8,128]{2,1,0:T(8,128)}) custom-call(f32[152,32,128]{2,1,0:T(8,128)} %refs_5_.3, bf16[152,32,128]{2,1,0:T(8,128)(2,1)} %refs_7_.2), custom_call_target="tpu_custom_call" | custom-call | tf_op jit(solution)/shard_map/pallas_call | solution.py:278
  5.6 3.1 %collective-permute-start.2 = (f32[15,8,128]{2,1,0:T(8,128)}, f32[15,8,128]{2,1,0:T(8,128)S(1)}, u32[]{:S(2)}, u32[]{:S(2)}) collective-permute-start(f32[15,8,128]{2,1,0:T(8,128)} %get-tuple-element.41.refs_12_), channel_id=1, source_target_pairs={{0,8},{8,16},{16,24},{1,9},{9,17},{17,25},{2,10},{10,18},{18,26},{... | collective-permute-start | bytes 184328 | tf_op jit(solution)/shard_map/ppermute | solution.py:288
  8.7 3.1 %collective-permute-start.3 = (f32[15,8,128]{2,1,0:T(8,128)}, f32[15,8,128]{2,1,0:T(8,128)S(1)}, u32[]{:S(2)}, u32[]{:S(2)}) collective-permute-start(f32[15,8,128]{2,1,0:T(8,128)} %get-tuple-element.42.refs_11_), channel_id=1, source_target_pairs={{8,0},{16,8},{24,16},{9,1},{17,9},{25,17},{10,2},{18,10},{26,18},{... | collective-permute-start | bytes 184328 | tf_op jit(solution)/shard_map/ppermute | solution.py:289
  11.8 2.5 %collective-permute-start = (f32[60,8,128]{2,1,0:T(8,128)}, f32[60,8,128]{2,1,0:T(8,128)S(1)}, u32[]{:S(2)}, u32[]{:S(2)}) collective-permute-start(f32[60,8,128]{2,1,0:T(8,128)} %get-tuple-element.39.zl_ref), channel_id=1, source_target_pairs={{0,1},{1,2},{2,3},{3,4},{4,5},{5,6},{6,7},{7,0},{8,9},{9,10},{10,1... | collective-permute-start | bytes 737288 | tf_op jit(solution)/shard_map/ppermute | solution.py:290
  14.4 1.1 %copy.24.refs_7_ = f32[32,31,31]{2,1,0:T(8,128)} copy(f32[32,31,31]{2,0,1:T(8,128)S(1)} %copy-done) | data formatting | bytes 246016 | tf_op args[8]
  15.5 0.1 pad_maximum_fusion.3
  15.5 0.1 pad_maximum_fusion.1
  15.6 0.6 %pad_maximum_fusion.refs_0_ = f32[3,153]{1,0:T(4,128)} fusion(f32[1,153]{1,0:T(1,128)S(1)} %bitcast.36, f32[1,153]{1,0:T(1,128)S(1)} %bitcast.37, f32[1,153]{1,0:T(1,128)S(1)} %bitcast.35), kind=kLoop, calls=%fused_computation.29 | loop fusion | flops 918 | bytes 3672 | tf_op jit(solution)/shard_map/stack | solution.py:265
  16.2 3.2 %shard_map.105 = (f32[152,32,128]{2,1,0:T(8,128)}, f32[32,32,128]{2,1,0:T(8,128)}, f32[8,3,32,128]{3,2,1,0:T(8,128)}) custom-call(f32[3,153]{1,0:T(4,128)} %pad_maximum_fusion.refs_0_, s32[32]{0:T(128)} %wall_ref.1, s32[128]{0:T(128)} %refs_2_.3, f32[152,32,128]{2,1,0:T(8,128)} %refs_5_.3, f32[152,32,128]{2,1,0:T(8,128)} %refs_5_.3, ...), custom_call_target="tpu_custom_call" | custom-call | tf_op jit(solution)/shard_map/pallas_call | solution.py:296
  19.4 5.8 %all-to-all-start = ((f32[8,3,32,128]{3,2,1,0:T(8,128)}), f32[8,3,32,128]{3,2,1,0:T(8,128)S(1)}, u32[]{:S(2)}, u32[]{:S(2)}) async-start(f32[8,3,32,128]{3,2,1,0:T(8,128)} %get-tuple-element.49), calls=%async_computation | async-start | bytes 786432 | tf_op jit(solution)/shard_map/all_to_all | solution.py:315
  25.2 0.2 add_reduce_fusion
  25.4 0.2 fusion.19
  25.8 0.4 copy.31
  26.2 0.4 copy.32
  26.6 0.1 scatter.6
  26.7 0.1 scatter.9
  26.9 0.1 divide_reduce_fusion.1
  27.0 0.6 %copy-done.4 = f32[15,8,128]{2,1,0:T(8,128)} copy-done((f32[15,8,128]{2,1,0:T(8,128)}, f32[15,8,128]{2,1,0:T(8,128)S(1)}, u32[]{:S(2)}) %copy-start.4) | copy-done | bytes 61464
  27.6 13.5 %shard_map.106 = (f32[152,32,128]{2,1,0:T(8,128)}, f32[152,32,128]{2,1,0:T(8,128)}) custom-call(f32[3,153]{1,0:T(4,128)} %pad_maximum_fusion.refs_0_, s32[32]{0:T(128)} %wall_ref.1, s32[128]{0:T(128)} %refs_2_.3, f32[152,32,128]{2,1,0:T(8,128)} %refs_5_.3, f32[152,32,128]{2,1,0:T(8,128)} %refs_5_.3, ...), custom_call_target="tpu_custom_call", output_to_operand_aliasing={{0}: (15, {})} | custom-call | tf_op jit(solution)/shard_map/pallas_call | solution.py:335
  41.1 0.7 %copy-done.2 = f32[60,8,128]{2,1,0:T(8,128)} copy-done((f32[60,8,128]{2,1,0:T(8,128)}, f32[60,8,128]{2,1,0:T(8,128)S(1)}, u32[]{:S(2)}) %copy-start.2) | copy-done | bytes 245784
  41.8 0.1 copy-done.3
  41.9 6.2 %shard_map.107 = (f32[152,32,128]{2,1,0:T(8,128)}, f32[152,32,128]{2,1,0:T(8,128)}) custom-call(s32[32]{0:T(128)} %wall_ref.1, f32[60,8,128]{2,1,0:T(8,128)} %copy-done.2, f32[60,8,128]{2,1,0:T(8,128)} %copy-done.3, f32[60,8,128]{2,1,0:T(8,128)} %get-tuple-element.39.zl_ref, ...), custom_call_target="tpu_custom_call", output_to_operand_aliasing={{0}: (6, {}), {1}: (7, {})} | custom-call | tf_op jit(solution)/shard_map/pallas_call | solution.py:355
  48.1 0.1 multiply_reduce_fusion.1
  48.3 1.2 %select_dynamic-update-slice_fusion = f32[152,32,128]{2,1,0:T(8,128)} fusion(f32[152,32,128]{2,1,0:T(8,128)} %get-tuple-element.48, f32[32,32,128]{2,1,0:T(8,128)S(1)} %copy-done.1, f32[32,128]{1,0:T(8,128)S(1)} %get-tuple-element.55, f32[32,32]{1,0:T(8,128)S(1)} %scatter.9, f32[32,32]{1,0:T(8,128)S(1)} %scatter.6, f32[32]{0:T(128)S(1)} %copy-done.7, ...), kind=kLoop, calls=%fused_computation | loop fusion | flops 786432 | bytes 1089696 | tf_op jit(solution)/shard_map/dynamic_update_slice | solution.py:372
  (32 shorter events, 0.4 us)
Async XLA Ops:
  0.6 13.6 %copy-start.6 = (f32[2,152]{1,0:T(2,128)S(1)}, f32[2,152]{1,0:T(2,128)}, u32[]{:S(2)}) copy-start(f32[2,152]{1,0:T(2,128)} %param.17) | copy-start | bytes 3652
  0.6 13.7 %copy-start = (f32[32,31,31]{2,0,1:T(8,128)S(1)}, f32[32,31,31]{2,0,1:T(8,128)}, u32[]{:S(2)}) copy-start(f32[32,31,31]{2,0,1:T(8,128)} %param.21) | copy-start | bytes 369028
  5.6 21.4 %collective-permute-start.2 = (f32[15,8,128]{2,1,0:T(8,128)}, f32[15,8,128]{2,1,0:T(8,128)S(1)}, u32[]{:S(2)}, u32[]{:S(2)}) collective-permute-start(f32[15,8,128]{2,1,0:T(8,128)} %get-tuple-element.41.refs_12_), channel_id=1, source_target_pairs={{0,8},{8,16},{16,24},{1,9},{9,17},{17,25},{2,10},{10,18},{18,26},{... | collective-permute-start | bytes 184328 | tf_op jit(solution)/shard_map/ppermute | solution.py:288
  8.7 18.3 %collective-permute-start.3 = (f32[15,8,128]{2,1,0:T(8,128)}, f32[15,8,128]{2,1,0:T(8,128)S(1)}, u32[]{:S(2)}, u32[]{:S(2)}) collective-permute-start(f32[15,8,128]{2,1,0:T(8,128)} %get-tuple-element.42.refs_11_), channel_id=1, source_target_pairs={{8,0},{16,8},{24,16},{9,1},{17,9},{25,17},{10,2},{18,10},{26,18},{... | collective-permute-start | bytes 184328 | tf_op jit(solution)/shard_map/ppermute | solution.py:289
  11.8 29.3 %collective-permute-start = (f32[60,8,128]{2,1,0:T(8,128)}, f32[60,8,128]{2,1,0:T(8,128)S(1)}, u32[]{:S(2)}, u32[]{:S(2)}) collective-permute-start(f32[60,8,128]{2,1,0:T(8,128)} %get-tuple-element.39.zl_ref), channel_id=1, source_target_pairs={{0,1},{1,2},{2,3},{3,4},{4,5},{5,6},{6,7},{7,0},{8,9},{9,10},{10,1... | collective-permute-start | bytes 737288 | tf_op jit(solution)/shard_map/ppermute | solution.py:290
  14.3 26.9 %collective-permute-start.1 = (f32[60,8,128]{2,1,0:T(8,128)}, f32[60,8,128]{2,1,0:T(8,128)S(1)}, u32[]{:S(2)}, u32[]{:S(2)}) collective-permute-start(f32[60,8,128]{2,1,0:T(8,128)} %get-tuple-element.40.refs_8_.zr_ref), channel_id=1, source_target_pairs={{1,0},{2,1},{3,2},{4,3},{5,4},{6,5},{7,6},{0,7},{9,8},{10,9},{11,1... | collective-permute-start | bytes 737288 | tf_op jit(solution)/shard_map/ppermute | solution.py:291
  19.4 6.4 %copy-start.7 = (f32[32]{0:T(128)S(1)}, f32[32]{0:T(128)}, u32[]{:S(2)}) copy-start(f32[32]{0:T(128)} %param.20) | copy-start | bytes 388
  19.4 28.7 %all-to-all-start = ((f32[8,3,32,128]{3,2,1,0:T(8,128)}), f32[8,3,32,128]{3,2,1,0:T(8,128)S(1)}, u32[]{:S(2)}, u32[]{:S(2)}) async-start(f32[8,3,32,128]{3,2,1,0:T(8,128)} %get-tuple-element.49), calls=%async_computation | async-start | bytes 786432 | tf_op jit(solution)/shard_map/all_to_all | solution.py:315
  27.0 0.6 %copy-start.4 = (f32[15,8,128]{2,1,0:T(8,128)}, f32[15,8,128]{2,1,0:T(8,128)S(1)}, u32[]{:S(2)}) copy-start(f32[15,8,128]{2,1,0:T(8,128)S(1)} %collective-permute-done.2.refs_9_) | copy-start | bytes 184324
  27.0 0.6 %copy-start.5 = (f32[15,8,128]{2,1,0:T(8,128)}, f32[15,8,128]{2,1,0:T(8,128)S(1)}, u32[]{:S(2)}) copy-start(f32[15,8,128]{2,1,0:T(8,128)S(1)} %collective-permute-done.3.refs_10_) | copy-start | bytes 184324
  41.1 0.7 %copy-start.2 = (f32[60,8,128]{2,1,0:T(8,128)}, f32[60,8,128]{2,1,0:T(8,128)S(1)}, u32[]{:S(2)}) copy-start(f32[60,8,128]{2,1,0:T(8,128)S(1)} %collective-permute-done.zb_ref) | copy-start | bytes 737284
  41.1 0.8 %copy-start.3 = (f32[60,8,128]{2,1,0:T(8,128)}, f32[60,8,128]{2,1,0:T(8,128)S(1)}, u32[]{:S(2)}) copy-start(f32[60,8,128]{2,1,0:T(8,128)S(1)} %collective-permute-done.1.za_ref) | copy-start | bytes 737284
  41.9 6.4 %copy-start.1 = (f32[32,32,128]{2,1,0:T(8,128)S(1)}, f32[32,32,128]{2,1,0:T(8,128)}, u32[]{:S(2)}) copy-start(f32[32,32,128]{2,1,0:T(8,128)} %get-tuple-element.50) | copy-start | bytes 1572868

commit v9 on v8

--- a/solution.py
+++ b/solution.py
@@ -230,7 +230,7 @@
             bot_tn[f] = bot_tn[f] + section_weight * fix_bot
         return carry
 
-    lax.fori_loop(0, nf // 2, pair, 0)
+    lax.fori_loop(0, nf // 2, pair, 0, unroll=10)
     stores = [
         pltpu.make_async_copy(top_sn, sn_out.at[pl.ds(ns, nf), pl.ds(0, 8), :], sems.at[4]),
         pltpu.make_async_copy(bot_sn, sn_out.at[pl.ds(ns, nf), pl.ds(cz - 8, 8), :], sems.at[5]),

time: 50.2 us -> 49.7 us (0.990)
    pallas_call x1, Pallas kernels: 6.2 us -> 5.69 us  [local(): pl.pallas_call(span_fix_kernel, grid=(1,), in_specs=[smem] + [whole((nf /...]
where the time goes in v9:
time: 49.7 us; the launch traced here: 49 us
  Pallas kernels  27.3 us (55%)
  starting transfers between devices  14.5 us (29%)
  local copies, waits for them, and re-layouts  3.73 us (8%)
  other arithmetic  2.63 us (5%)
  between operations  0.85 us (2%)
    pallas_call x1, Pallas kernels, local(): pl.pallas_call(lambda *refs: layer_kernel(True, nsb, LB, *refs), grid=(nf...  13.5 us
    all_to_all x1, starting transfers between devices, local(): blocks = lax.all_to_all(spread, 'gz', 0, 0, tiled=True)  5.84 us
    pallas_call x1, Pallas kernels, local(): pl.pallas_call(span_fix_kernel, grid=(1,), in_specs=[smem] + [whole((nf /...  5.69 us
    pallas_call x1, Pallas kernels, local(): pl.pallas_call(pack_kernel, grid=(1,), in_specs=[pl.BlockSpec((ny, cz, w)...  4.97 us
    unnamed x19, local copies, waits for them, and re-layouts  3.29 us
    pallas_call x1, Pallas kernels, local(): pl.pallas_call(lambda *refs: layer_kernel(False, 0, sb, *refs), grid=(ns...  3.18 us
    ppermute x1, starting transfers between devices, local(): xb = lax.ppermute(xr, 'gx', [(i, i + 1) for i in range(ngx - 1)])  3.11 us
    ppermute x1, starting transfers between devices, local(): xa = lax.ppermute(xl, 'gx', [(i + 1, i) for i in range(ngx - 1)])  3.06 us
  transfers between devices with their start and end apart: 5, of which 0 were waited for; matrix products, arithmetic and copies ran while one was open for 7% of the time, Pallas kernels for 46%

profile of v9, /device:TPU:5, one launch (start us, length us, event | category | flops | bytes accessed | tf_op | source)
XLA Modules:
  0.0 49.0 jit_solution(5943586524877426814)
XLA Ops:
  0.6 5.0 %shard_map.104 = (f32[15,8,128]{2,1,0:T(8,128)}, f32[15,8,128]{2,1,0:T(8,128)}, f32[15,8,128]{2,1,0:T(8,128)}, f32[15,8,128]{2,1,0:T(8,128)}, f32[60,8,128]{2,1,0:T(8,128)}, /*index=5*/f32[60,8,128]{2,1,0:T(8,128)}) custom-call(f32[152,32,128]{2,1,0:T(8,128)} %refs_5_.3, bf16[152,32,128]{2,1,0:T(8,128)(2,1)} %refs_7_.2), custom_call_target="tpu_custom_call" | custom-call | tf_op jit(solution)/shard_map/pallas_call | solution.py:278
  5.6 3.1 %collective-permute-start.2 = (f32[15,8,128]{2,1,0:T(8,128)}, f32[15,8,128]{2,1,0:T(8,128)S(1)}, u32[]{:S(2)}, u32[]{:S(2)}) collective-permute-start(f32[15,8,128]{2,1,0:T(8,128)} %get-tuple-element.41.refs_12_), channel_id=1, source_target_pairs={{0,8},{8,16},{16,24},{1,9},{9,17},{17,25},{2,10},{10,18},{18,26},{... | collective-permute-start | bytes 184328 | tf_op jit(solution)/shard_map/ppermute | solution.py:288
  8.7 3.1 %collective-permute-start.3 = (f32[15,8,128]{2,1,0:T(8,128)}, f32[15,8,128]{2,1,0:T(8,128)S(1)}, u32[]{:S(2)}, u32[]{:S(2)}) collective-permute-start(f32[15,8,128]{2,1,0:T(8,128)} %get-tuple-element.42.refs_11_), channel_id=1, source_target_pairs={{8,0},{16,8},{24,16},{9,1},{17,9},{25,17},{10,2},{18,10},{26,18},{... | collective-permute-start | bytes 184328 | tf_op jit(solution)/shard_map/ppermute | solution.py:289
  11.8 2.5 %collective-permute-start = (f32[60,8,128]{2,1,0:T(8,128)}, f32[60,8,128]{2,1,0:T(8,128)S(1)}, u32[]{:S(2)}, u32[]{:S(2)}) collective-permute-start(f32[60,8,128]{2,1,0:T(8,128)} %get-tuple-element.39.zl_ref), channel_id=1, source_target_pairs={{0,1},{1,2},{2,3},{3,4},{4,5},{5,6},{6,7},{7,0},{8,9},{9,10},{10,1... | collective-permute-start | bytes 737288 | tf_op jit(solution)/shard_map/ppermute | solution.py:290
  14.4 1.1 %copy.24.refs_7_ = f32[32,31,31]{2,1,0:T(8,128)} copy(f32[32,31,31]{2,0,1:T(8,128)S(1)} %copy-done) | data formatting | bytes 246016 | tf_op args[8]
  15.5 0.1 pad_maximum_fusion.3
  15.5 0.1 pad_maximum_fusion.1
  15.6 0.6 %pad_maximum_fusion.refs_0_ = f32[3,153]{1,0:T(4,128)} fusion(f32[1,153]{1,0:T(1,128)S(1)} %bitcast.36, f32[1,153]{1,0:T(1,128)S(1)} %bitcast.37, f32[1,153]{1,0:T(1,128)S(1)} %bitcast.35), kind=kLoop, calls=%fused_computation.29 | loop fusion | flops 918 | bytes 3672 | tf_op jit(solution)/shard_map/stack | solution.py:265
  16.2 3.2 %shard_map.105 = (f32[152,32,128]{2,1,0:T(8,128)}, f32[32,32,128]{2,1,0:T(8,128)}, f32[8,3,32,128]{3,2,1,0:T(8,128)}) custom-call(f32[3,153]{1,0:T(4,128)} %pad_maximum_fusion.refs_0_, s32[32]{0:T(128)} %wall_ref.1, s32[128]{0:T(128)} %refs_2_.3, f32[152,32,128]{2,1,0:T(8,128)} %refs_5_.3, f32[152,32,128]{2,1,0:T(8,128)} %refs_5_.3, ...), custom_call_target="tpu_custom_call" | custom-call | tf_op jit(solution)/shard_map/pallas_call | solution.py:296
  19.4 5.8 %all-to-all-start = ((f32[8,3,32,128]{3,2,1,0:T(8,128)}), f32[8,3,32,128]{3,2,1,0:T(8,128)S(1)}, u32[]{:S(2)}, u32[]{:S(2)}) async-start(f32[8,3,32,128]{3,2,1,0:T(8,128)} %get-tuple-element.49), calls=%async_computation | async-start | bytes 786432 | tf_op jit(solution)/shard_map/all_to_all | solution.py:315
  25.2 0.2 add_reduce_fusion
  25.4 0.2 fusion.19
  25.8 0.4 copy.31
  26.2 0.4 copy.32
  26.6 0.1 scatter.6
  26.7 0.1 scatter.9
  26.9 0.1 divide_reduce_fusion.1
  27.0 0.6 %copy-done.4 = f32[15,8,128]{2,1,0:T(8,128)} copy-done((f32[15,8,128]{2,1,0:T(8,128)}, f32[15,8,128]{2,1,0:T(8,128)S(1)}, u32[]{:S(2)}) %copy-start.4) | copy-done | bytes 61464
  27.6 13.5 %shard_map.106 = (f32[152,32,128]{2,1,0:T(8,128)}, f32[152,32,128]{2,1,0:T(8,128)}) custom-call(f32[3,153]{1,0:T(4,128)} %pad_maximum_fusion.refs_0_, s32[32]{0:T(128)} %wall_ref.1, s32[128]{0:T(128)} %refs_2_.3, f32[152,32,128]{2,1,0:T(8,128)} %refs_5_.3, f32[152,32,128]{2,1,0:T(8,128)} %refs_5_.3, ...), custom_call_target="tpu_custom_call", output_to_operand_aliasing={{0}: (15, {})} | custom-call | tf_op jit(solution)/shard_map/pallas_call | solution.py:335
  41.1 0.7 %copy-done.2 = f32[60,8,128]{2,1,0:T(8,128)} copy-done((f32[60,8,128]{2,1,0:T(8,128)}, f32[60,8,128]{2,1,0:T(8,128)S(1)}, u32[]{:S(2)}) %copy-start.2) | copy-done | bytes 245784
  41.8 0.1 copy-done.3
  41.9 5.7 %shard_map.107 = (f32[152,32,128]{2,1,0:T(8,128)}, f32[152,32,128]{2,1,0:T(8,128)}) custom-call(s32[32]{0:T(128)} %wall_ref.1, f32[60,8,128]{2,1,0:T(8,128)} %copy-done.2, f32[60,8,128]{2,1,0:T(8,128)} %copy-done.3, f32[60,8,128]{2,1,0:T(8,128)} %get-tuple-element.39.zl_ref, ...), custom_call_target="tpu_custom_call", output_to_operand_aliasing={{0}: (6, {}), {1}: (7, {})} | custom-call | tf_op jit(solution)/shard_map/pallas_call | solution.py:355
  47.6 0.1 multiply_reduce_fusion.1
  47.8 1.2 %select_dynamic-update-slice_fusion = f32[152,32,128]{2,1,0:T(8,128)} fusion(f32[152,32,128]{2,1,0:T(8,128)} %get-tuple-element.48, f32[32,32,128]{2,1,0:T(8,128)S(1)} %copy-done.1, f32[32,128]{1,0:T(8,128)S(1)} %get-tuple-element.55, f32[32,32]{1,0:T(8,128)S(1)} %scatter.9, f32[32,32]{1,0:T(8,128)S(1)} %scatter.6, f32[32]{0:T(128)S(1)} %copy-done.7, ...), kind=kLoop, calls=%fused_computation | loop fusion | flops 786432 | bytes 1089696 | tf_op jit(solution)/shard_map/dynamic_update_slice | solution.py:372
  (32 shorter events, 0.4 us)
Async XLA Ops:
  0.6 13.6 %copy-start.6 = (f32[2,152]{1,0:T(2,128)S(1)}, f32[2,152]{1,0:T(2,128)}, u32[]{:S(2)}) copy-start(f32[2,152]{1,0:T(2,128)} %param.17) | copy-start | bytes 3652
  0.6 13.7 %copy-start = (f32[32,31,31]{2,0,1:T(8,128)S(1)}, f32[32,31,31]{2,0,1:T(8,128)}, u32[]{:S(2)}) copy-start(f32[32,31,31]{2,0,1:T(8,128)} %param.21) | copy-start | bytes 369028
  5.6 21.4 %collective-permute-start.2 = (f32[15,8,128]{2,1,0:T(8,128)}, f32[15,8,128]{2,1,0:T(8,128)S(1)}, u32[]{:S(2)}, u32[]{:S(2)}) collective-permute-start(f32[15,8,128]{2,1,0:T(8,128)} %get-tuple-element.41.refs_12_), channel_id=1, source_target_pairs={{0,8},{8,16},{16,24},{1,9},{9,17},{17,25},{2,10},{10,18},{18,26},{... | collective-permute-start | bytes 184328 | tf_op jit(solution)/shard_map/ppermute | solution.py:288
  8.7 18.3 %collective-permute-start.3 = (f32[15,8,128]{2,1,0:T(8,128)}, f32[15,8,128]{2,1,0:T(8,128)S(1)}, u32[]{:S(2)}, u32[]{:S(2)}) collective-permute-start(f32[15,8,128]{2,1,0:T(8,128)} %get-tuple-element.42.refs_11_), channel_id=1, source_target_pairs={{8,0},{16,8},{24,16},{9,1},{17,9},{25,17},{10,2},{18,10},{26,18},{... | collective-permute-start | bytes 184328 | tf_op jit(solution)/shard_map/ppermute | solution.py:289
  11.8 29.3 %collective-permute-start = (f32[60,8,128]{2,1,0:T(8,128)}, f32[60,8,128]{2,1,0:T(8,128)S(1)}, u32[]{:S(2)}, u32[]{:S(2)}) collective-permute-start(f32[60,8,128]{2,1,0:T(8,128)} %get-tuple-element.39.zl_ref), channel_id=1, source_target_pairs={{0,1},{1,2},{2,3},{3,4},{4,5},{5,6},{6,7},{7,0},{8,9},{9,10},{10,1... | collective-permute-start | bytes 737288 | tf_op jit(solution)/shard_map/ppermute | solution.py:290
  14.3 26.9 %collective-permute-start.1 = (f32[60,8,128]{2,1,0:T(8,128)}, f32[60,8,128]{2,1,0:T(8,128)S(1)}, u32[]{:S(2)}, u32[]{:S(2)}) collective-permute-start(f32[60,8,128]{2,1,0:T(8,128)} %get-tuple-element.40.refs_8_.zr_ref), channel_id=1, source_target_pairs={{1,0},{2,1},{3,2},{4,3},{5,4},{6,5},{7,6},{0,7},{9,8},{10,9},{11,1... | collective-permute-start | bytes 737288 | tf_op jit(solution)/shard_map/ppermute | solution.py:291
  19.4 6.4 %copy-start.7 = (f32[32]{0:T(128)S(1)}, f32[32]{0:T(128)}, u32[]{:S(2)}) copy-start(f32[32]{0:T(128)} %param.20) | copy-start | bytes 388
  19.4 28.2 %all-to-all-start = ((f32[8,3,32,128]{3,2,1,0:T(8,128)}), f32[8,3,32,128]{3,2,1,0:T(8,128)S(1)}, u32[]{:S(2)}, u32[]{:S(2)}) async-start(f32[8,3,32,128]{3,2,1,0:T(8,128)} %get-tuple-element.49), calls=%async_computation | async-start | bytes 786432 | tf_op jit(solution)/shard_map/all_to_all | solution.py:315
  27.0 0.6 %copy-start.4 = (f32[15,8,128]{2,1,0:T(8,128)}, f32[15,8,128]{2,1,0:T(8,128)S(1)}, u32[]{:S(2)}) copy-start(f32[15,8,128]{2,1,0:T(8,128)S(1)} %collective-permute-done.2.refs_9_) | copy-start | bytes 184324
  27.0 0.6 %copy-start.5 = (f32[15,8,128]{2,1,0:T(8,128)}, f32[15,8,128]{2,1,0:T(8,128)S(1)}, u32[]{:S(2)}) copy-start(f32[15,8,128]{2,1,0:T(8,128)S(1)} %collective-permute-done.3.refs_10_) | copy-start | bytes 184324
  41.1 0.7 %copy-start.2 = (f32[60,8,128]{2,1,0:T(8,128)}, f32[60,8,128]{2,1,0:T(8,128)S(1)}, u32[]{:S(2)}) copy-start(f32[60,8,128]{2,1,0:T(8,128)S(1)} %collective-permute-done.zb_ref) | copy-start | bytes 737284
  41.1 0.8 %copy-start.3 = (f32[60,8,128]{2,1,0:T(8,128)}, f32[60,8,128]{2,1,0:T(8,128)S(1)}, u32[]{:S(2)}) copy-start(f32[60,8,128]{2,1,0:T(8,128)S(1)} %collective-permute-done.1.za_ref) | copy-start | bytes 737284
  41.9 5.9 %copy-start.1 = (f32[32,32,128]{2,1,0:T(8,128)S(1)}, f32[32,32,128]{2,1,0:T(8,128)}, u32[]{:S(2)}) copy-start(f32[32,32,128]{2,1,0:T(8,128)} %get-tuple-element.50) | copy-start | bytes 1572868

commit v10 on v9

--- a/solution.py
+++ b/solution.py
@@ -195,50 +195,60 @@
         wall_top = jnp.where(sub == z, wall_ref[z], wall_top)
         wall_bot = jnp.where(sub == z, wall_ref[cz - 8 + z], wall_bot)
     slope_scale = -span_courant / 60.0
-    for c in loads:
-        c.wait()
-
-    def pair(p, carry):
-        miss_top = zb_ref[p] - zl_ref[p]
-        miss_bot = za_ref[p] - zr_ref[p]
-        for h in range(2):
-            f = 2 * p + h
-            y = ns + f
-            d_top = pltpu.roll(miss_top, 4, 0) if h == 0 else miss_top
-            d_top = jnp.where(sub >= 4, d_top, 0.0)
-            d_bot = miss_bot if h == 0 else pltpu.roll(miss_bot, 4, 0)
-            d_bot = jnp.where(sub < 4, d_bot, 0.0)
-            s_top = jnp.zeros((8, w), jnp.float32)
-            m_top = jnp.zeros((8, w), jnp.float32)
-            s_bot = jnp.zeros((8, w), jnp.float32)
-            m_bot = jnp.zeros((8, w), jnp.float32)
-            for j, cs, cm in ((1, -45.0, -56.0), (2, 9.0, 28.0), (3, -1.0, -8.0), (4, 0.0, 1.0)):
-                lo = jnp.where(sub < j, pltpu.roll(d_top, j, 0), 0.0)
-                hi = jnp.where(sub >= 8 - j, pltpu.roll(d_bot, 8 - j, 0), 0.0)
-                if cs != 0.0:
-                    s_top = s_top + cs * lo
-                    s_bot = s_bot - cs * hi
-                m_top = m_top + cm * lo
-                m_bot = m_bot + cm * hi
-            v_top = v_ref[y, 0:8, :].astype(jnp.float32)
-            v_bot = v_ref[y, cz - 8:cz, :].astype(jnp.float32)
-            fix_top = jnp.where(y >= wall_top, slope_scale * v_top * s_top - damping * m_top, 0.0)
-            fix_bot = jnp.where(y >= wall_bot, slope_scale * v_bot * s_bot - damping * m_bot, 0.0)
-            top_sn[f] = top_sn[f] + fix_top
-            bot_sn[f] = bot_sn[f] + fix_bot
-            top_tn[f] = top_tn[f] + section_weight * fix_top
-            bot_tn[f] = bot_tn[f] + section_weight * fix_bot
-        return carry
-
-    lax.fori_loop(0, nf // 2, pair, 0, unroll=10)
-    stores = [
-        pltpu.make_async_copy(top_sn, sn_out.at[pl.ds(ns, nf), pl.ds(0, 8), :], sems.at[4]),
-        pltpu.make_async_copy(bot_sn, sn_out.at[pl.ds(ns, nf), pl.ds(cz - 8, 8), :], sems.at[5]),
-        pltpu.make_async_copy(top_tn, tn_out.at[pl.ds(ns, nf), pl.ds(0, 8), :], sems.at[6]),
-        pltpu.make_async_copy(bot_tn, tn_out.at[pl.ds(ns, nf), pl.ds(cz - 8, 8), :], sems.at[7]),
+
+    def side(top, sn_buf, tn_buf):
+        def pair(p, carry):
+            if top:
+                miss = zb_ref[p] - zl_ref[p]
+            else:
+                miss = za_ref[p] - zr_ref[p]
+            for h in range(2):
+                f = 2 * p + h
+                y = ns + f
+                if top:
+                    d = pltpu.roll(miss, 4, 0) if h == 0 else miss
+                    d = jnp.where(sub >= 4, d, 0.0)
+                else:
+                    d = miss if h == 0 else pltpu.roll(miss, 4, 0)
+                    d = jnp.where(sub < 4, d, 0.0)
+                s_acc = jnp.zeros((8, w), jnp.float32)
+                m_acc = jnp.zeros((8, w), jnp.float32)
+                for j, cs, cm in ((1, -45.0, -56.0), (2, 9.0, 28.0), (3, -1.0, -8.0), (4, 0.0, 1.0)):
+                    if top:
+                        term = jnp.where(sub < j, pltpu.roll(d, j, 0), 0.0)
+                    else:
+                        term = jnp.where(sub >= 8 - j, pltpu.roll(d, 8 - j, 0), 0.0)
+                        cs = -cs
+                    if cs != 0.0:
+                        s_acc = s_acc + cs * term
+                    m_acc = m_acc + cm * term
+                rows = slice(0, 8) if top else slice(cz - 8, cz)
+                speed = v_ref[y, rows, :].astype(jnp.float32)
+                wall = wall_top if top else wall_bot
+                fix = jnp.where(y >= wall, slope_scale * speed * s_acc - damping * m_acc, 0.0)
+                sn_buf[f] = sn_buf[f] + fix
+                tn_buf[f] = tn_buf[f] + section_weight * fix
+            return carry
+
+        lax.fori_loop(0, nf // 2, pair, 0, unroll=10)
+
+    targets = [
+        (top_sn, sn_out.at[pl.ds(ns, nf), pl.ds(0, 8), :], sems.at[4]),
+        (top_tn, tn_out.at[pl.ds(ns, nf), pl.ds(0, 8), :], sems.at[5]),
+        (bot_sn, sn_out.at[pl.ds(ns, nf), pl.ds(cz - 8, 8), :], sems.at[6]),
+        (bot_tn, tn_out.at[pl.ds(ns, nf), pl.ds(cz - 8, 8), :], sems.at[7]),
     ]
-    for c in stores:
-        c.start()
+    stores = [pltpu.make_async_copy(*t) for t in targets]
+    loads[0].wait()
+    loads[2].wait()
+    side(True, top_sn, top_tn)
+    stores[0].start()
+    stores[1].start()
+    loads[1].wait()
+    loads[3].wait()
+    side(False, bot_sn, bot_tn)
+    stores[2].start()
+    stores[3].start()
     for c in stores:
         c.wait()
 

time: 49.7 us -> 49.3 us (level)
  Pallas kernels: 27.3 us -> 26.8 us
  transfers between devices with their start and end apart: 5 -> 5, of which waited for: 0 -> 0; matrix products, arithmetic and copies ran while one was open for 7% -> 7% of each run, Pallas kernels for 46% -> 45%
where the time goes in v10:
time: 49.3 us; the launch traced here: 48.5 us
  Pallas kernels  26.8 us (54%)
  starting transfers between devices  14.5 us (29%)
  local copies, waits for them, and re-layouts  3.73 us (8%)
  other arithmetic  2.63 us (5%)
  between operations  0.85 us (2%)
    pallas_call x1, Pallas kernels, local(): pl.pallas_call(lambda *refs: layer_kernel(True, nsb, LB, *refs), grid=(nf...  13.5 us
    all_to_all x1, starting transfers between devices, local(): blocks = lax.all_to_all(spread, 'gz', 0, 0, tiled=True)  5.84 us
    pallas_call x1, Pallas kernels, local(): pl.pallas_call(span_fix_kernel, grid=(1,), in_specs=[smem] + [whole((nf /...  5.24 us
    pallas_call x1, Pallas kernels, local(): pl.pallas_call(pack_kernel, grid=(1,), in_specs=[pl.BlockSpec((ny, cz, w)...  4.97 us
    unnamed x19, local copies, waits for them, and re-layouts  3.29 us
    pallas_call x1, Pallas kernels, local(): pl.pallas_call(lambda *refs: layer_kernel(False, 0, sb, *refs), grid=(ns...  3.18 us
    ppermute x1, starting transfers between devices, local(): xb = lax.ppermute(xr, 'gx', [(i, i + 1) for i in range(ngx - 1)])  3.11 us
    ppermute x1, starting transfers between devices, local(): xa = lax.ppermute(xl, 'gx', [(i + 1, i) for i in range(ngx - 1)])  3.06 us
  transfers between devices with their start and end apart: 5, of which 0 were waited for; matrix products, arithmetic and copies ran while one was open for 7% of the time, Pallas kernels for 45%

profile of v10, /device:TPU:5, one launch (start us, length us, event | category | flops | bytes accessed | tf_op | source)
XLA Modules:
  0.0 48.5 jit_solution(10004992494479778993)
XLA Ops:
  0.6 5.0 %shard_map.104 = (f32[15,8,128]{2,1,0:T(8,128)}, f32[15,8,128]{2,1,0:T(8,128)}, f32[15,8,128]{2,1,0:T(8,128)}, f32[15,8,128]{2,1,0:T(8,128)}, f32[60,8,128]{2,1,0:T(8,128)}, /*index=5*/f32[60,8,128]{2,1,0:T(8,128)}) custom-call(f32[152,32,128]{2,1,0:T(8,128)} %refs_5_.3, bf16[152,32,128]{2,1,0:T(8,128)(2,1)} %refs_7_.2), custom_call_target="tpu_custom_call" | custom-call | tf_op jit(solution)/shard_map/pallas_call | solution.py:288
  5.6 3.1 %collective-permute-start.2 = (f32[15,8,128]{2,1,0:T(8,128)}, f32[15,8,128]{2,1,0:T(8,128)S(1)}, u32[]{:S(2)}, u32[]{:S(2)}) collective-permute-start(f32[15,8,128]{2,1,0:T(8,128)} %get-tuple-element.41.refs_12_), channel_id=1, source_target_pairs={{0,8},{8,16},{16,24},{1,9},{9,17},{17,25},{2,10},{10,18},{18,26},{... | collective-permute-start | bytes 184328 | tf_op jit(solution)/shard_map/ppermute | solution.py:298
  8.7 3.1 %collective-permute-start.3 = (f32[15,8,128]{2,1,0:T(8,128)}, f32[15,8,128]{2,1,0:T(8,128)S(1)}, u32[]{:S(2)}, u32[]{:S(2)}) collective-permute-start(f32[15,8,128]{2,1,0:T(8,128)} %get-tuple-element.42.refs_11_), channel_id=1, source_target_pairs={{8,0},{16,8},{24,16},{9,1},{17,9},{25,17},{10,2},{18,10},{26,18},{... | collective-permute-start | bytes 184328 | tf_op jit(solution)/shard_map/ppermute | solution.py:299
  11.8 2.5 %collective-permute-start = (f32[60,8,128]{2,1,0:T(8,128)}, f32[60,8,128]{2,1,0:T(8,128)S(1)}, u32[]{:S(2)}, u32[]{:S(2)}) collective-permute-start(f32[60,8,128]{2,1,0:T(8,128)} %get-tuple-element.39.zl_ref), channel_id=1, source_target_pairs={{0,1},{1,2},{2,3},{3,4},{4,5},{5,6},{6,7},{7,0},{8,9},{9,10},{10,1... | collective-permute-start | bytes 737288 | tf_op jit(solution)/shard_map/ppermute | solution.py:300
  14.4 1.1 %copy.24.refs_7_ = f32[32,31,31]{2,1,0:T(8,128)} copy(f32[32,31,31]{2,0,1:T(8,128)S(1)} %copy-done) | data formatting | bytes 246016 | tf_op args[8]
  15.5 0.1 pad_maximum_fusion.3
  15.5 0.1 pad_maximum_fusion.1
  15.6 0.6 %pad_maximum_fusion.refs_0_ = f32[3,153]{1,0:T(4,128)} fusion(f32[1,153]{1,0:T(1,128)S(1)} %bitcast.36, f32[1,153]{1,0:T(1,128)S(1)} %bitcast.37, f32[1,153]{1,0:T(1,128)S(1)} %bitcast.35), kind=kLoop, calls=%fused_computation.29 | loop fusion | flops 918 | bytes 3672 | tf_op jit(solution)/shard_map/stack | solution.py:275
  16.2 3.2 %shard_map.105 = (f32[152,32,128]{2,1,0:T(8,128)}, f32[32,32,128]{2,1,0:T(8,128)}, f32[8,3,32,128]{3,2,1,0:T(8,128)}) custom-call(f32[3,153]{1,0:T(4,128)} %pad_maximum_fusion.refs_0_, s32[32]{0:T(128)} %wall_ref.1, s32[128]{0:T(128)} %refs_2_.3, f32[152,32,128]{2,1,0:T(8,128)} %refs_5_.3, f32[152,32,128]{2,1,0:T(8,128)} %refs_5_.3, ...), custom_call_target="tpu_custom_call" | custom-call | tf_op jit(solution)/shard_map/pallas_call | solution.py:306
  19.4 5.8 %all-to-all-start = ((f32[8,3,32,128]{3,2,1,0:T(8,128)}), f32[8,3,32,128]{3,2,1,0:T(8,128)S(1)}, u32[]{:S(2)}, u32[]{:S(2)}) async-start(f32[8,3,32,128]{3,2,1,0:T(8,128)} %get-tuple-element.49), calls=%async_computation | async-start | bytes 786432 | tf_op jit(solution)/shard_map/all_to_all | solution.py:325
  25.2 0.2 add_reduce_fusion
  25.4 0.2 fusion.19
  25.8 0.4 copy.31
  26.2 0.4 copy.32
  26.6 0.1 scatter.6
  26.7 0.1 scatter.9
  26.9 0.1 divide_reduce_fusion.1
  27.0 0.6 %copy-done.4 = f32[15,8,128]{2,1,0:T(8,128)} copy-done((f32[15,8,128]{2,1,0:T(8,128)}, f32[15,8,128]{2,1,0:T(8,128)S(1)}, u32[]{:S(2)}) %copy-start.4) | copy-done | bytes 61464
  27.6 13.5 %shard_map.106 = (f32[152,32,128]{2,1,0:T(8,128)}, f32[152,32,128]{2,1,0:T(8,128)}) custom-call(f32[3,153]{1,0:T(4,128)} %pad_maximum_fusion.refs_0_, s32[32]{0:T(128)} %wall_ref.1, s32[128]{0:T(128)} %refs_2_.3, f32[152,32,128]{2,1,0:T(8,128)} %refs_5_.3, f32[152,32,128]{2,1,0:T(8,128)} %refs_5_.3, ...), custom_call_target="tpu_custom_call", output_to_operand_aliasing={{0}: (15, {})} | custom-call | tf_op jit(solution)/shard_map/pallas_call | solution.py:345
  41.1 0.7 %copy-done.2 = f32[60,8,128]{2,1,0:T(8,128)} copy-done((f32[60,8,128]{2,1,0:T(8,128)}, f32[60,8,128]{2,1,0:T(8,128)S(1)}, u32[]{:S(2)}) %copy-start.2) | copy-done | bytes 245784
  41.8 0.1 copy-done.3
  41.9 5.2 %shard_map.107 = (f32[152,32,128]{2,1,0:T(8,128)}, f32[152,32,128]{2,1,0:T(8,128)}) custom-call(s32[32]{0:T(128)} %wall_ref.1, f32[60,8,128]{2,1,0:T(8,128)} %copy-done.2, f32[60,8,128]{2,1,0:T(8,128)} %copy-done.3, f32[60,8,128]{2,1,0:T(8,128)} %get-tuple-element.39.zl_ref, ...), custom_call_target="tpu_custom_call", output_to_operand_aliasing={{0}: (6, {}), {1}: (7, {})} | custom-call | tf_op jit(solution)/shard_map/pallas_call | solution.py:365
  47.2 0.1 multiply_reduce_fusion.1
  47.4 1.2 %select_dynamic-update-slice_fusion = f32[152,32,128]{2,1,0:T(8,128)} fusion(f32[152,32,128]{2,1,0:T(8,128)} %get-tuple-element.48, f32[32,32,128]{2,1,0:T(8,128)S(1)} %copy-done.1, f32[32,128]{1,0:T(8,128)S(1)} %get-tuple-element.55, f32[32,32]{1,0:T(8,128)S(1)} %scatter.9, f32[32,32]{1,0:T(8,128)S(1)} %scatter.6, f32[32]{0:T(128)S(1)} %copy-done.7, ...), kind=kLoop, calls=%fused_computation | loop fusion | flops 786432 | bytes 1089696 | tf_op jit(solution)/shard_map/dynamic_update_slice | solution.py:382
  (32 shorter events, 0.4 us)
Async XLA Ops:
  0.6 13.6 %copy-start.6 = (f32[2,152]{1,0:T(2,128)S(1)}, f32[2,152]{1,0:T(2,128)}, u32[]{:S(2)}) copy-start(f32[2,152]{1,0:T(2,128)} %param.17) | copy-start | bytes 3652
  0.6 13.7 %copy-start = (f32[32,31,31]{2,0,1:T(8,128)S(1)}, f32[32,31,31]{2,0,1:T(8,128)}, u32[]{:S(2)}) copy-start(f32[32,31,31]{2,0,1:T(8,128)} %param.21) | copy-start | bytes 369028
  5.6 21.4 %collective-permute-start.2 = (f32[15,8,128]{2,1,0:T(8,128)}, f32[15,8,128]{2,1,0:T(8,128)S(1)}, u32[]{:S(2)}, u32[]{:S(2)}) collective-permute-start(f32[15,8,128]{2,1,0:T(8,128)} %get-tuple-element.41.refs_12_), channel_id=1, source_target_pairs={{0,8},{8,16},{16,24},{1,9},{9,17},{17,25},{2,10},{10,18},{18,26},{... | collective-permute-start | bytes 184328 | tf_op jit(solution)/shard_map/ppermute | solution.py:298
  8.7 18.3 %collective-permute-start.3 = (f32[15,8,128]{2,1,0:T(8,128)}, f32[15,8,128]{2,1,0:T(8,128)S(1)}, u32[]{:S(2)}, u32[]{:S(2)}) collective-permute-start(f32[15,8,128]{2,1,0:T(8,128)} %get-tuple-element.42.refs_11_), channel_id=1, source_target_pairs={{8,0},{16,8},{24,16},{9,1},{17,9},{25,17},{10,2},{18,10},{26,18},{... | collective-permute-start | bytes 184328 | tf_op jit(solution)/shard_map/ppermute | solution.py:299
  11.8 29.3 %collective-permute-start = (f32[60,8,128]{2,1,0:T(8,128)}, f32[60,8,128]{2,1,0:T(8,128)S(1)}, u32[]{:S(2)}, u32[]{:S(2)}) collective-permute-start(f32[60,8,128]{2,1,0:T(8,128)} %get-tuple-element.39.zl_ref), channel_id=1, source_target_pairs={{0,1},{1,2},{2,3},{3,4},{4,5},{5,6},{6,7},{7,0},{8,9},{9,10},{10,1... | collective-permute-start | bytes 737288 | tf_op jit(solution)/shard_map/ppermute | solution.py:300
  14.3 26.9 %collective-permute-start.1 = (f32[60,8,128]{2,1,0:T(8,128)}, f32[60,8,128]{2,1,0:T(8,128)S(1)}, u32[]{:S(2)}, u32[]{:S(2)}) collective-permute-start(f32[60,8,128]{2,1,0:T(8,128)} %get-tuple-element.40.refs_8_.zr_ref), channel_id=1, source_target_pairs={{1,0},{2,1},{3,2},{4,3},{5,4},{6,5},{7,6},{0,7},{9,8},{10,9},{11,1... | collective-permute-start | bytes 737288 | tf_op jit(solution)/shard_map/ppermute | solution.py:301
  19.4 6.4 %copy-start.7 = (f32[32]{0:T(128)S(1)}, f32[32]{0:T(128)}, u32[]{:S(2)}) copy-start(f32[32]{0:T(128)} %param.20) | copy-start | bytes 388
  19.4 27.8 %all-to-all-start = ((f32[8,3,32,128]{3,2,1,0:T(8,128)}), f32[8,3,32,128]{3,2,1,0:T(8,128)S(1)}, u32[]{:S(2)}, u32[]{:S(2)}) async-start(f32[8,3,32,128]{3,2,1,0:T(8,128)} %get-tuple-element.49), calls=%async_computation | async-start | bytes 786432 | tf_op jit(solution)/shard_map/all_to_all | solution.py:325
  27.0 0.6 %copy-start.4 = (f32[15,8,128]{2,1,0:T(8,128)}, f32[15,8,128]{2,1,0:T(8,128)S(1)}, u32[]{:S(2)}) copy-start(f32[15,8,128]{2,1,0:T(8,128)S(1)} %collective-permute-done.2.refs_9_) | copy-start | bytes 184324
  27.0 0.6 %copy-start.5 = (f32[15,8,128]{2,1,0:T(8,128)}, f32[15,8,128]{2,1,0:T(8,128)S(1)}, u32[]{:S(2)}) copy-start(f32[15,8,128]{2,1,0:T(8,128)S(1)} %collective-permute-done.3.refs_10_) | copy-start | bytes 184324
  41.1 0.7 %copy-start.2 = (f32[60,8,128]{2,1,0:T(8,128)}, f32[60,8,128]{2,1,0:T(8,128)S(1)}, u32[]{:S(2)}) copy-start(f32[60,8,128]{2,1,0:T(8,128)S(1)} %collective-permute-done.zb_ref) | copy-start | bytes 737284
  41.1 0.8 %copy-start.3 = (f32[60,8,128]{2,1,0:T(8,128)}, f32[60,8,128]{2,1,0:T(8,128)S(1)}, u32[]{:S(2)}) copy-start(f32[60,8,128]{2,1,0:T(8,128)S(1)} %collective-permute-done.1.za_ref) | copy-start | bytes 737284
  41.9 5.4 %copy-start.1 = (f32[32,32,128]{2,1,0:T(8,128)S(1)}, f32[32,32,128]{2,1,0:T(8,128)}, u32[]{:S(2)}) copy-start(f32[32,32,128]{2,1,0:T(8,128)} %get-tuple-element.50) | copy-start | bytes 1572868

commit v11 on v10

--- a/solution.py
+++ b/solution.py
@@ -62,7 +62,8 @@
     if fluid:
         (face_ref, wall_ref, contact_ref, th_ref, prev_ref, next_ref, st_ref,
          u_ref, v_ref, xb_ref, xa_ref, xl_ref, xr_ref, ul_ref, ur_ref,
-         _alias_ref, sn_ref, tn_ref, wallv_ref, contv_ref, ext_ref) = refs
+         _alias_ref, sn_ref, tn_ref, tsn_ref, bsn_ref, ttn_ref, btn_ref,
+         wallv_ref, contv_ref, ext_ref) = refs
     else:
         (face_ref, wall_ref, contact_ref, th_ref, prev_ref, next_ref, st_ref,
          bs_ref, _order_ref, sn_ref, int_ref, mine_ref, wallv_ref, contv_ref) = refs
@@ -162,6 +163,10 @@
         sn_ref[s] = sn
         if fluid:
             tn_ref[s] = adv
+            tsn_ref[s] = sn[0:8]
+            bsn_ref[s] = sn[cz - 8:]
+            ttn_ref[s] = adv[0:8]
+            btn_ref[s] = adv[cz - 8:]
         else:
             inner = jnp.dot(bs_ref[s], adv[1:], precision=lax.Precision.HIGHEST,
                             preferred_element_type=jnp.float32)
@@ -175,19 +180,16 @@
                 mine_ref[n, part] = rows
 
 
-def span_fix_kernel(wall_ref, zb_ref, za_ref, zl_ref, zr_ref, v_ref, sn_in, tn_in,
-                    sn_out, tn_out, top_sn, bot_sn, top_tn, bot_tn, sems):
+def span_fix_kernel(wall_ref, zb_ref, za_ref, zl_ref, zr_ref, v_ref, ta_ref, tb_ref, tc_ref,
+                    td_ref, sn_in, tn_in, sn_out, tn_out, top_sn, bot_sn, top_tn, bot_tn, sems):
     ny, cz, w = v_ref.shape
     nf = top_sn.shape[0]
     ns = ny - nf
-    loads = [
-        pltpu.make_async_copy(sn_in.at[pl.ds(ns, nf), pl.ds(0, 8), :], top_sn, sems.at[0]),
-        pltpu.make_async_copy(sn_in.at[pl.ds(ns, nf), pl.ds(cz - 8, 8), :], bot_sn, sems.at[1]),
-        pltpu.make_async_copy(tn_in.at[pl.ds(ns, nf), pl.ds(0, 8), :], top_tn, sems.at[2]),
-        pltpu.make_async_copy(tn_in.at[pl.ds(ns, nf), pl.ds(cz - 8, 8), :], bot_tn, sems.at[3]),
-    ]
-    for c in loads:
-        c.start()
+    del sn_in, tn_in
+    top_sn[...] = ta_ref[...]
+    bot_sn[...] = tb_ref[...]
+    top_tn[...] = tc_ref[...]
+    bot_tn[...] = td_ref[...]
     sub = lax.broadcasted_iota(jnp.int32, (8, w), 0)
     wall_top = jnp.zeros((8, w), jnp.int32)
     wall_bot = jnp.zeros((8, w), jnp.int32)
@@ -239,13 +241,9 @@
         (bot_tn, tn_out.at[pl.ds(ns, nf), pl.ds(cz - 8, 8), :], sems.at[7]),
     ]
     stores = [pltpu.make_async_copy(*t) for t in targets]
-    loads[0].wait()
-    loads[2].wait()
     side(True, top_sn, top_tn)
     stores[0].start()
     stores[1].start()
-    loads[1].wait()
-    loads[3].wait()
     side(False, bot_sn, bot_tn)
     stores[2].start()
     stores[3].start()
@@ -342,18 +340,18 @@
     head_values = jnp.sum(weights(k).T[:, :, None] * targets, axis=0)
     following = jnp.sum(weights(k + 1).T[:, :, None] * targets, axis=0)
 
-    fluid_sn, fluid_tn = pl.pallas_call(
+    fluid_sn, fluid_tn, tiles_a, tiles_b, tiles_c, tiles_d = pl.pallas_call(
         lambda *refs: layer_kernel(True, nsb, LB, *refs),
         grid=(nfb,),
         in_specs=[smem, smem, smem, blk(nsb), prev_spec(nsb), next_spec(nsb), blk(nsb),
                   blk(nsb), blk(nsb), edge_spec, edge_spec,
                   edge_spec, edge_spec, edge_spec, edge_spec,
                   pl.BlockSpec(memory_space=pl.ANY)],
-        out_specs=[blk(nsb), blk(nsb)],
+        out_specs=[blk(nsb), blk(nsb)] + [pl.BlockSpec((LB, 8, w), lambda i: (i, 0, 0))] * 4,
         out_shape=[
             jax.ShapeDtypeStruct((ny, cz, w), f32),
             jax.ShapeDtypeStruct((ny, cz, w), f32),
-        ],
+        ] + [jax.ShapeDtypeStruct((nf, 8, w), f32)] * 4,
         scratch_shapes=[pltpu.VMEM((cz, w), jnp.int32), pltpu.VMEM((cz, w), f32),
                         pltpu.VMEM((cz + 16, w), f32)],
         input_output_aliases={15: 0},
@@ -365,12 +363,14 @@
     fluid_sn, fluid_tn = pl.pallas_call(
         span_fix_kernel,
         grid=(1,),
-        in_specs=[smem] + [whole((nf // 2, 8, w))] * 4 + [whole((ny, cz, w)), anyspec, anyspec],
+        in_specs=[smem] + [whole((nf // 2, 8, w))] * 4 + [whole((ny, cz, w))]
+        + [whole((nf, 8, w))] * 4 + [anyspec, anyspec],
         out_specs=[anyspec, anyspec],
         out_shape=[jax.ShapeDtypeStruct((ny, cz, w), f32)] * 2,
         scratch_shapes=[pltpu.VMEM((nf, 8, w), f32)] * 4 + [pltpu.SemaphoreType.DMA((8,))],
-        input_output_aliases={6: 0, 7: 1},
-    )(wall_layers, zb, za, zl, zr, span_speed, fluid_sn, fluid_tn)
+        input_output_aliases={10: 0, 11: 1},
+    )(wall_layers, zb, za, zl, zr, span_speed, tiles_a, tiles_b, tiles_c, tiles_d,
+      fluid_sn, fluid_tn)
 
     row = jnp.arange(cz, dtype=jnp.int32)
     col0 = jnp.zeros((ns, cz), f32).at[:, 1:].set(block_inverse[:, :, 0])

time: 49.3 us -> 48.8 us (0.990)
    pallas_call x1, Pallas kernels: 5.24 us -> 4.53 us  [local(): pl.pallas_call(span_fix_kernel, grid=(1,), in_specs=[smem] + [whole((nf /...]
where the time goes in v11:
time: 48.8 us; the launch traced here: 48.2 us
  Pallas kernels  26.5 us (54%)
  starting transfers between devices  14.5 us (30%)
  local copies, waits for them, and re-layouts  3.7 us (8%)
  other arithmetic  2.62 us (5%)
  between operations  0.85 us (2%)
    pallas_call x1, Pallas kernels, local(): pl.pallas_call(lambda *refs: layer_kernel(True, nsb, LB, *refs), grid=(nf...  13.8 us
    all_to_all x1, starting transfers between devices, local(): blocks = lax.all_to_all(spread, 'gz', 0, 0, tiled=True)  5.85 us
    pallas_call x1, Pallas kernels, local(): pl.pallas_call(pack_kernel, grid=(1,), in_specs=[pl.BlockSpec((ny, cz, w)...  4.95 us
    pallas_call x1, Pallas kernels, local(): pl.pallas_call(span_fix_kernel, grid=(1,), in_specs=[smem] + [whole((nf /...  4.53 us
    unnamed x19, local copies, waits for them, and re-layouts  3.26 us
    pallas_call x1, Pallas kernels, local(): pl.pallas_call(lambda *refs: layer_kernel(False, 0, sb, *refs), grid=(ns...  3.21 us
    ppermute x1, starting transfers between devices, local(): xb = lax.ppermute(xr, 'gx', [(i, i + 1) for i in range(ngx - 1)])  3.11 us
    ppermute x1, starting transfers between devices, local(): xa = lax.ppermute(xl, 'gx', [(i + 1, i) for i in range(ngx - 1)])  3.06 us
  transfers between devices with their start and end apart: 5, of which 0 were waited for; matrix products, arithmetic and copies ran while one was open for 7% of the time, Pallas kernels for 45%

profile of v11, /device:TPU:5, one launch (start us, length us, event | category | flops | bytes accessed | tf_op | source)
XLA Modules:
  0.0 48.2 jit_solution(13484767380764826617)
XLA Ops:
  0.6 4.9 %shard_map.104 = (f32[15,8,128]{2,1,0:T(8,128)}, f32[15,8,128]{2,1,0:T(8,128)}, f32[15,8,128]{2,1,0:T(8,128)}, f32[15,8,128]{2,1,0:T(8,128)}, f32[60,8,128]{2,1,0:T(8,128)}, /*index=5*/f32[60,8,128]{2,1,0:T(8,128)}) custom-call(f32[152,32,128]{2,1,0:T(8,128)} %refs_5_.3, bf16[152,32,128]{2,1,0:T(8,128)(2,1)} %refs_7_.2), custom_call_target="tpu_custom_call" | custom-call | tf_op jit(solution)/shard_map/pallas_call | solution.py:286
  5.6 3.1 %collective-permute-start.2 = (f32[15,8,128]{2,1,0:T(8,128)}, f32[15,8,128]{2,1,0:T(8,128)S(1)}, u32[]{:S(2)}, u32[]{:S(2)}) collective-permute-start(f32[15,8,128]{2,1,0:T(8,128)} %get-tuple-element.45.refs_12_), channel_id=1, source_target_pairs={{0,8},{8,16},{16,24},{1,9},{9,17},{17,25},{2,10},{10,18},{18,26},{... | collective-permute-start | bytes 184328 | tf_op jit(solution)/shard_map/ppermute | solution.py:296
  8.7 3.1 %collective-permute-start.3 = (f32[15,8,128]{2,1,0:T(8,128)}, f32[15,8,128]{2,1,0:T(8,128)S(1)}, u32[]{:S(2)}, u32[]{:S(2)}) collective-permute-start(f32[15,8,128]{2,1,0:T(8,128)} %get-tuple-element.46.refs_11_), channel_id=1, source_target_pairs={{8,0},{16,8},{24,16},{9,1},{17,9},{25,17},{10,2},{18,10},{26,18},{... | collective-permute-start | bytes 184328 | tf_op jit(solution)/shard_map/ppermute | solution.py:297
  11.8 2.5 %collective-permute-start = (f32[60,8,128]{2,1,0:T(8,128)}, f32[60,8,128]{2,1,0:T(8,128)S(1)}, u32[]{:S(2)}, u32[]{:S(2)}) collective-permute-start(f32[60,8,128]{2,1,0:T(8,128)} %get-tuple-element.43.zl_ref), channel_id=1, source_target_pairs={{0,1},{1,2},{2,3},{3,4},{4,5},{5,6},{6,7},{7,0},{8,9},{9,10},{10,1... | collective-permute-start | bytes 737288 | tf_op jit(solution)/shard_map/ppermute | solution.py:298
  14.3 1.1 %copy.24.refs_7_ = f32[32,31,31]{2,1,0:T(8,128)} copy(f32[32,31,31]{2,0,1:T(8,128)S(1)} %copy-done) | data formatting | bytes 246016 | tf_op args[8]
  15.4 0.1 pad_maximum_fusion.3
  15.5 0.1 pad_maximum_fusion.1
  15.6 0.6 %pad_maximum_fusion.refs_0_ = f32[3,153]{1,0:T(4,128)} fusion(f32[1,153]{1,0:T(1,128)S(1)} %bitcast.36, f32[1,153]{1,0:T(1,128)S(1)} %bitcast.37, f32[1,153]{1,0:T(1,128)S(1)} %bitcast.35), kind=kLoop, calls=%fused_computation.29 | loop fusion | flops 918 | bytes 3672 | tf_op jit(solution)/shard_map/stack | solution.py:273
  16.2 3.2 %shard_map.105 = (f32[152,32,128]{2,1,0:T(8,128)}, f32[32,32,128]{2,1,0:T(8,128)}, f32[8,3,32,128]{3,2,1,0:T(8,128)}) custom-call(f32[3,153]{1,0:T(4,128)} %pad_maximum_fusion.refs_0_, s32[32]{0:T(128)} %wall_ref.1, s32[128]{0:T(128)} %refs_2_.3, f32[152,32,128]{2,1,0:T(8,128)} %refs_5_.3, f32[152,32,128]{2,1,0:T(8,128)} %refs_5_.3, ...), custom_call_target="tpu_custom_call" | custom-call | tf_op jit(solution)/shard_map/pallas_call | solution.py:304
  19.4 5.9 %all-to-all-start = ((f32[8,3,32,128]{3,2,1,0:T(8,128)}), f32[8,3,32,128]{3,2,1,0:T(8,128)S(1)}, u32[]{:S(2)}, u32[]{:S(2)}) async-start(f32[8,3,32,128]{3,2,1,0:T(8,128)} %get-tuple-element.57), calls=%async_computation | async-start | bytes 786432 | tf_op jit(solution)/shard_map/all_to_all | solution.py:323
  25.3 0.2 add_reduce_fusion
  25.4 0.2 fusion.19
  25.9 0.4 copy.31
  26.2 0.4 copy.32
  26.7 0.1 scatter.6
  26.7 0.1 scatter.9
  26.9 0.1 divide_reduce_fusion.1
  27.0 0.6 %copy-done.4 = f32[15,8,128]{2,1,0:T(8,128)} copy-done((f32[15,8,128]{2,1,0:T(8,128)}, f32[15,8,128]{2,1,0:T(8,128)S(1)}, u32[]{:S(2)}) %copy-start.4) | copy-done | bytes 61464
  27.6 13.8 %shard_map.106 = (f32[152,32,128]{2,1,0:T(8,128)}, f32[152,32,128]{2,1,0:T(8,128)}, f32[120,8,128]{2,1,0:T(8,128)}, f32[120,8,128]{2,1,0:T(8,128)}, f32[120,8,128]{2,1,0:T(8,128)}, /*index=5*/f32[120,8,128]{2,1,0:T(8,128)}) custom-call(f32[3,153]{1,0:T(4,128)} %pad_maximum_fusion.refs_0_, s32[32]{0:T(128)} %wall_ref.1, ...), custom_call_target="tpu_custom_call", output_to_operand_aliasing={{0}: (15, {})} | custom-call | tf_op jit(solution)/shard_map/pallas_call | solution.py:343
  41.5 0.7 %copy-done.2 = f32[60,8,128]{2,1,0:T(8,128)} copy-done((f32[60,8,128]{2,1,0:T(8,128)}, f32[60,8,128]{2,1,0:T(8,128)S(1)}, u32[]{:S(2)}) %copy-start.2) | copy-done | bytes 245784
  42.1 0.1 copy-done.3
  42.2 4.5 %shard_map.107 = (f32[152,32,128]{2,1,0:T(8,128)}, f32[152,32,128]{2,1,0:T(8,128)}) custom-call(s32[32]{0:T(128)} %wall_ref.1, f32[60,8,128]{2,1,0:T(8,128)} %copy-done.2, f32[60,8,128]{2,1,0:T(8,128)} %copy-done.3, f32[60,8,128]{2,1,0:T(8,128)} %get-tuple-element.43.zl_ref, ...), custom_call_target="tpu_custom_call", output_to_operand_aliasing={{0}: (10, {}), {1}: (11, {})} | custom-call | tf_op jit(solution)/shard_map/pallas_call | solution.py:363
  46.8 0.1 multiply_reduce_fusion.1
  47.0 1.2 %select_dynamic-update-slice_fusion = f32[152,32,128]{2,1,0:T(8,128)} fusion(f32[152,32,128]{2,1,0:T(8,128)} %get-tuple-element.56, f32[32,32,128]{2,1,0:T(8,128)S(1)} %copy-done.1, f32[32,128]{1,0:T(8,128)S(1)} %get-tuple-element.63, f32[32,32]{1,0:T(8,128)S(1)} %scatter.9, f32[32,32]{1,0:T(8,128)S(1)} %scatter.6, f32[32]{0:T(128)S(1)} %copy-done.7, ...), kind=kLoop, calls=%fused_computation | loop fusion | flops 786432 | bytes 1089696 | tf_op jit(solution)/shard_map/dynamic_update_slice | solution.py:382
  (32 shorter events, 0.4 us)
Async XLA Ops:
  0.6 13.6 %copy-start.6 = (f32[2,152]{1,0:T(2,128)S(1)}, f32[2,152]{1,0:T(2,128)}, u32[]{:S(2)}) copy-start(f32[2,152]{1,0:T(2,128)} %param.17) | copy-start | bytes 3652
  0.6 13.7 %copy-start = (f32[32,31,31]{2,0,1:T(8,128)S(1)}, f32[32,31,31]{2,0,1:T(8,128)}, u32[]{:S(2)}) copy-start(f32[32,31,31]{2,0,1:T(8,128)} %param.21) | copy-start | bytes 369028
  5.6 21.4 %collective-permute-start.2 = (f32[15,8,128]{2,1,0:T(8,128)}, f32[15,8,128]{2,1,0:T(8,128)S(1)}, u32[]{:S(2)}, u32[]{:S(2)}) collective-permute-start(f32[15,8,128]{2,1,0:T(8,128)} %get-tuple-element.45.refs_12_), channel_id=1, source_target_pairs={{0,8},{8,16},{16,24},{1,9},{9,17},{17,25},{2,10},{10,18},{18,26},{... | collective-permute-start | bytes 184328 | tf_op jit(solution)/shard_map/ppermute | solution.py:296
  8.7 18.3 %collective-permute-start.3 = (f32[15,8,128]{2,1,0:T(8,128)}, f32[15,8,128]{2,1,0:T(8,128)S(1)}, u32[]{:S(2)}, u32[]{:S(2)}) collective-permute-start(f32[15,8,128]{2,1,0:T(8,128)} %get-tuple-element.46.refs_11_), channel_id=1, source_target_pairs={{8,0},{16,8},{24,16},{9,1},{17,9},{25,17},{10,2},{18,10},{26,18},{... | collective-permute-start | bytes 184328 | tf_op jit(solution)/shard_map/ppermute | solution.py:297
  11.8 29.7 %collective-permute-start = (f32[60,8,128]{2,1,0:T(8,128)}, f32[60,8,128]{2,1,0:T(8,128)S(1)}, u32[]{:S(2)}, u32[]{:S(2)}) collective-permute-start(f32[60,8,128]{2,1,0:T(8,128)} %get-tuple-element.43.zl_ref), channel_id=1, source_target_pairs={{0,1},{1,2},{2,3},{3,4},{4,5},{5,6},{6,7},{7,0},{8,9},{9,10},{10,1... | collective-permute-start | bytes 737288 | tf_op jit(solution)/shard_map/ppermute | solution.py:298
  14.2 27.2 %collective-permute-start.1 = (f32[60,8,128]{2,1,0:T(8,128)}, f32[60,8,128]{2,1,0:T(8,128)S(1)}, u32[]{:S(2)}, u32[]{:S(2)}) collective-permute-start(f32[60,8,128]{2,1,0:T(8,128)} %get-tuple-element.44.refs_8_.zr_ref), channel_id=1, source_target_pairs={{1,0},{2,1},{3,2},{4,3},{5,4},{6,5},{7,6},{0,7},{9,8},{10,9},{11,1... | collective-permute-start | bytes 737288 | tf_op jit(solution)/shard_map/ppermute | solution.py:299
  19.4 6.4 %copy-start.7 = (f32[32]{0:T(128)S(1)}, f32[32]{0:T(128)}, u32[]{:S(2)}) copy-start(f32[32]{0:T(128)} %param.20) | copy-start | bytes 388
  19.4 27.4 %all-to-all-start = ((f32[8,3,32,128]{3,2,1,0:T(8,128)}), f32[8,3,32,128]{3,2,1,0:T(8,128)S(1)}, u32[]{:S(2)}, u32[]{:S(2)}) async-start(f32[8,3,32,128]{3,2,1,0:T(8,128)} %get-tuple-element.57), calls=%async_computation | async-start | bytes 786432 | tf_op jit(solution)/shard_map/all_to_all | solution.py:323
  27.0 0.6 %copy-start.4 = (f32[15,8,128]{2,1,0:T(8,128)}, f32[15,8,128]{2,1,0:T(8,128)S(1)}, u32[]{:S(2)}) copy-start(f32[15,8,128]{2,1,0:T(8,128)S(1)} %collective-permute-done.2.refs_9_) | copy-start | bytes 184324
  27.0 0.6 %copy-start.5 = (f32[15,8,128]{2,1,0:T(8,128)}, f32[15,8,128]{2,1,0:T(8,128)S(1)}, u32[]{:S(2)}) copy-start(f32[15,8,128]{2,1,0:T(8,128)S(1)} %collective-permute-done.3.refs_10_) | copy-start | bytes 184324
  41.5 0.7 %copy-start.2 = (f32[60,8,128]{2,1,0:T(8,128)}, f32[60,8,128]{2,1,0:T(8,128)S(1)}, u32[]{:S(2)}) copy-start(f32[60,8,128]{2,1,0:T(8,128)S(1)} %collective-permute-done.zb_ref) | copy-start | bytes 737284
  41.5 0.7 %copy-start.3 = (f32[60,8,128]{2,1,0:T(8,128)}, f32[60,8,128]{2,1,0:T(8,128)S(1)}, u32[]{:S(2)}) copy-start(f32[60,8,128]{2,1,0:T(8,128)S(1)} %collective-permute-done.1.za_ref) | copy-start | bytes 737284
  42.2 4.7 %copy-start.1 = (f32[32,32,128]{2,1,0:T(8,128)S(1)}, f32[32,32,128]{2,1,0:T(8,128)}, u32[]{:S(2)}) copy-start(f32[32,32,128]{2,1,0:T(8,128)} %get-tuple-element.58) | copy-start | bytes 1572868

commit v12 on v11

--- a/solution.py
+++ b/solution.py
@@ -62,7 +62,7 @@
     if fluid:
         (face_ref, wall_ref, contact_ref, th_ref, prev_ref, next_ref, st_ref,
          u_ref, v_ref, xb_ref, xa_ref, xl_ref, xr_ref, ul_ref, ur_ref,
-         _alias_ref, sn_ref, tn_ref, tsn_ref, bsn_ref, ttn_ref, btn_ref,
+         _alias_ref, sn_ref, tn_ref, tsn_ref, bsn_ref, ttn_ref, btn_ref, tv_ref, bv_ref,
          wallv_ref, contv_ref, ext_ref) = refs
     else:
         (face_ref, wall_ref, contact_ref, th_ref, prev_ref, next_ref, st_ref,
@@ -167,6 +167,8 @@
             bsn_ref[s] = sn[cz - 8:]
             ttn_ref[s] = adv[0:8]
             btn_ref[s] = adv[cz - 8:]
+            tv_ref[s] = v[0:8]
+            bv_ref[s] = v[cz - 8:]
         else:
             inner = jnp.dot(bs_ref[s], adv[1:], precision=lax.Precision.HIGHEST,
                             preferred_element_type=jnp.float32)
@@ -180,9 +182,9 @@
                 mine_ref[n, part] = rows
 
 
-def span_fix_kernel(wall_ref, zb_ref, za_ref, zl_ref, zr_ref, v_ref, ta_ref, tb_ref, tc_ref,
+def span_fix_kernel(wall_ref, zb_ref, za_ref, zl_ref, zr_ref, tv_ref, bv_ref, ta_ref, tb_ref, tc_ref,
                     td_ref, sn_in, tn_in, sn_out, tn_out, top_sn, bot_sn, top_tn, bot_tn, sems):
-    ny, cz, w = v_ref.shape
+    ny, cz, w = sn_in.shape
     nf = top_sn.shape[0]
     ns = ny - nf
     del sn_in, tn_in
@@ -224,8 +226,7 @@
                     if cs != 0.0:
                         s_acc = s_acc + cs * term
                     m_acc = m_acc + cm * term
-                rows = slice(0, 8) if top else slice(cz - 8, cz)
-                speed = v_ref[y, rows, :].astype(jnp.float32)
+                speed = tv_ref[f] if top else bv_ref[f]
                 wall = wall_top if top else wall_bot
                 fix = jnp.where(y >= wall, slope_scale * speed * s_acc - damping * m_acc, 0.0)
                 sn_buf[f] = sn_buf[f] + fix
@@ -340,18 +341,18 @@
     head_values = jnp.sum(weights(k).T[:, :, None] * targets, axis=0)
     following = jnp.sum(weights(k + 1).T[:, :, None] * targets, axis=0)
 
-    fluid_sn, fluid_tn, tiles_a, tiles_b, tiles_c, tiles_d = pl.pallas_call(
+    fluid_sn, fluid_tn, tiles_a, tiles_b, tiles_c, tiles_d, speed_top, speed_bot = pl.pallas_call(
         lambda *refs: layer_kernel(True, nsb, LB, *refs),
         grid=(nfb,),
         in_specs=[smem, smem, smem, blk(nsb), prev_spec(nsb), next_spec(nsb), blk(nsb),
                   blk(nsb), blk(nsb), edge_spec, edge_spec,
                   edge_spec, edge_spec, edge_spec, edge_spec,
                   pl.BlockSpec(memory_space=pl.ANY)],
-        out_specs=[blk(nsb), blk(nsb)] + [pl.BlockSpec((LB, 8, w), lambda i: (i, 0, 0))] * 4,
+        out_specs=[blk(nsb), blk(nsb)] + [pl.BlockSpec((LB, 8, w), lambda i: (i, 0, 0))] * 6,
         out_shape=[
             jax.ShapeDtypeStruct((ny, cz, w), f32),
             jax.ShapeDtypeStruct((ny, cz, w), f32),
-        ] + [jax.ShapeDtypeStruct((nf, 8, w), f32)] * 4,
+        ] + [jax.ShapeDtypeStruct((nf, 8, w), f32)] * 6,
         scratch_shapes=[pltpu.VMEM((cz, w), jnp.int32), pltpu.VMEM((cz, w), f32),
                         pltpu.VMEM((cz + 16, w), f32)],
         input_output_aliases={15: 0},
@@ -363,13 +364,13 @@
     fluid_sn, fluid_tn = pl.pallas_call(
         span_fix_kernel,
         grid=(1,),
-        in_specs=[smem] + [whole((nf // 2, 8, w))] * 4 + [whole((ny, cz, w))]
-        + [whole((nf, 8, w))] * 4 + [anyspec, anyspec],
+        in_specs=[smem] + [whole((nf // 2, 8, w))] * 4
+        + [whole((nf, 8, w))] * 6 + [anyspec, anyspec],
         out_specs=[anyspec, anyspec],
         out_shape=[jax.ShapeDtypeStruct((ny, cz, w), f32)] * 2,
         scratch_shapes=[pltpu.VMEM((nf, 8, w), f32)] * 4 + [pltpu.SemaphoreType.DMA((8,))],
-        input_output_aliases={10: 0, 11: 1},
-    )(wall_layers, zb, za, zl, zr, span_speed, tiles_a, tiles_b, tiles_c, tiles_d,
+        input_output_aliases={11: 0, 12: 1},
+    )(wall_layers, zb, za, zl, zr, speed_top, speed_bot, tiles_a, tiles_b, tiles_c, tiles_d,
       fluid_sn, fluid_tn)
 
     row = jnp.arange(cz, dtype=jnp.int32)

time: 48.8 us -> 48.8 us (level)
  transfers between devices with their start and end apart: 5 -> 5, of which waited for: 0 -> 0; matrix products, arithmetic and copies ran while one was open for 7% -> 8% of each run, Pallas kernels for 45% -> 45%
where the time goes in v12:
time: 48.8 us; the launch traced here: 48.1 us
  Pallas kernels  26.4 us (54%)
  starting transfers between devices  14.5 us (30%)
  local copies, waits for them, and re-layouts  3.72 us (8%)
  other arithmetic  2.63 us (5%)
  between operations  0.85 us (2%)
    pallas_call x1, Pallas kernels, local(): pl.pallas_call(lambda *refs: layer_kernel(True, nsb, LB, *refs), grid=(nf...  13.9 us
    all_to_all x1, starting transfers between devices, local(): blocks = lax.all_to_all(spread, 'gz', 0, 0, tiled=True)  5.85 us
    pallas_call x1, Pallas kernels, local(): pl.pallas_call(pack_kernel, grid=(1,), in_specs=[pl.BlockSpec((ny, cz, w)...  4.96 us
    pallas_call x1, Pallas kernels, local(): pl.pallas_call(span_fix_kernel, grid=(1,), in_specs=[smem] + [whole((nf /...  4.42 us
    unnamed x19, local copies, waits for them, and re-layouts  3.28 us
    pallas_call x1, Pallas kernels, local(): pl.pallas_call(lambda *refs: layer_kernel(False, 0, sb, *refs), grid=(ns...  3.19 us
    ppermute x1, starting transfers between devices, local(): xb = lax.ppermute(xr, 'gx', [(i, i + 1) for i in range(ngx - 1)])  3.11 us
    ppermute x1, starting transfers between devices, local(): xa = lax.ppermute(xl, 'gx', [(i + 1, i) for i in range(ngx - 1)])  3.06 us
  transfers between devices with their start and end apart: 5, of which 0 were waited for; matrix products, arithmetic and copies ran while one was open for 8% of the time, Pallas kernels for 45%

profile of v12, /device:TPU:5, one launch (start us, length us, event | category | flops | bytes accessed | tf_op | source)
XLA Modules:
  0.0 48.1 jit_solution(10082772449999781747)
XLA Ops:
  0.6 5.0 %shard_map.104 = (f32[15,8,128]{2,1,0:T(8,128)}, f32[15,8,128]{2,1,0:T(8,128)}, f32[15,8,128]{2,1,0:T(8,128)}, f32[15,8,128]{2,1,0:T(8,128)}, f32[60,8,128]{2,1,0:T(8,128)}, /*index=5*/f32[60,8,128]{2,1,0:T(8,128)}) custom-call(f32[152,32,128]{2,1,0:T(8,128)} %refs_5_.3, bf16[152,32,128]{2,1,0:T(8,128)(2,1)} %refs_7_.2), custom_call_target="tpu_custom_call" | custom-call | tf_op jit(solution)/shard_map/pallas_call | solution.py:287
  5.6 3.1 %collective-permute-start.2 = (f32[15,8,128]{2,1,0:T(8,128)}, f32[15,8,128]{2,1,0:T(8,128)S(1)}, u32[]{:S(2)}, u32[]{:S(2)}) collective-permute-start(f32[15,8,128]{2,1,0:T(8,128)} %get-tuple-element.47.refs_12_), channel_id=1, source_target_pairs={{0,8},{8,16},{16,24},{1,9},{9,17},{17,25},{2,10},{10,18},{18,26},{... | collective-permute-start | bytes 184328 | tf_op jit(solution)/shard_map/ppermute | solution.py:297
  8.7 3.1 %collective-permute-start.3 = (f32[15,8,128]{2,1,0:T(8,128)}, f32[15,8,128]{2,1,0:T(8,128)S(1)}, u32[]{:S(2)}, u32[]{:S(2)}) collective-permute-start(f32[15,8,128]{2,1,0:T(8,128)} %get-tuple-element.48.refs_11_), channel_id=1, source_target_pairs={{8,0},{16,8},{24,16},{9,1},{17,9},{25,17},{10,2},{18,10},{26,18},{... | collective-permute-start | bytes 184328 | tf_op jit(solution)/shard_map/ppermute | solution.py:298
  11.8 2.5 %collective-permute-start = (f32[60,8,128]{2,1,0:T(8,128)}, f32[60,8,128]{2,1,0:T(8,128)S(1)}, u32[]{:S(2)}, u32[]{:S(2)}) collective-permute-start(f32[60,8,128]{2,1,0:T(8,128)} %get-tuple-element.45.zl_ref), channel_id=1, source_target_pairs={{0,1},{1,2},{2,3},{3,4},{4,5},{5,6},{6,7},{7,0},{8,9},{9,10},{10,1... | collective-permute-start | bytes 737288 | tf_op jit(solution)/shard_map/ppermute | solution.py:299
  14.3 1.1 %copy.24.refs_7_ = f32[32,31,31]{2,1,0:T(8,128)} copy(f32[32,31,31]{2,0,1:T(8,128)S(1)} %copy-done) | data formatting | bytes 246016 | tf_op args[8]
  15.4 0.1 pad_maximum_fusion.3
  15.5 0.1 pad_maximum_fusion.1
  15.6 0.6 %pad_maximum_fusion.refs_0_ = f32[3,153]{1,0:T(4,128)} fusion(f32[1,153]{1,0:T(1,128)S(1)} %bitcast.36, f32[1,153]{1,0:T(1,128)S(1)} %bitcast.37, f32[1,153]{1,0:T(1,128)S(1)} %bitcast.35), kind=kLoop, calls=%fused_computation.29 | loop fusion | flops 918 | bytes 3672 | tf_op jit(solution)/shard_map/stack | solution.py:274
  16.2 3.2 %shard_map.105 = (f32[152,32,128]{2,1,0:T(8,128)}, f32[32,32,128]{2,1,0:T(8,128)}, f32[8,3,32,128]{3,2,1,0:T(8,128)}) custom-call(f32[3,153]{1,0:T(4,128)} %pad_maximum_fusion.refs_0_, s32[32]{0:T(128)} %wall_ref.1, s32[128]{0:T(128)} %refs_2_.3, f32[152,32,128]{2,1,0:T(8,128)} %refs_5_.3, f32[152,32,128]{2,1,0:T(8,128)} %refs_5_.3, ...), custom_call_target="tpu_custom_call" | custom-call | tf_op jit(solution)/shard_map/pallas_call | solution.py:305
  19.4 5.9 %all-to-all-start = ((f32[8,3,32,128]{3,2,1,0:T(8,128)}), f32[8,3,32,128]{3,2,1,0:T(8,128)S(1)}, u32[]{:S(2)}, u32[]{:S(2)}) async-start(f32[8,3,32,128]{3,2,1,0:T(8,128)} %get-tuple-element.61), calls=%async_computation | async-start | bytes 786432 | tf_op jit(solution)/shard_map/all_to_all | solution.py:324
  25.2 0.2 add_reduce_fusion
  25.4 0.2 fusion.19
  25.8 0.4 copy.31
  26.2 0.4 copy.32
  26.6 0.1 scatter.6
  26.7 0.1 scatter.9
  26.9 0.1 divide_reduce_fusion.1
  27.0 0.6 %copy-done.4 = f32[15,8,128]{2,1,0:T(8,128)} copy-done((f32[15,8,128]{2,1,0:T(8,128)}, f32[15,8,128]{2,1,0:T(8,128)S(1)}, u32[]{:S(2)}) %copy-start.4) | copy-done | bytes 61464
  27.6 13.9 %shard_map.106 = (f32[152,32,128]{2,1,0:T(8,128)}, f32[152,32,128]{2,1,0:T(8,128)}, f32[120,8,128]{2,1,0:T(8,128)}, f32[120,8,128]{2,1,0:T(8,128)}, f32[120,8,12...) custom-call(f32[3,153]{1,0:T(4,128)} %pad_maximum_fusion.refs_0_, ...), custom_call_target="tpu_custom_call", output_to_operand_aliasing={{0}: (15, {})} | custom-call | tf_op jit(solution)/shard_map/pallas_call | solution.py:344
  41.6 0.7 %copy-done.2 = f32[60,8,128]{2,1,0:T(8,128)} copy-done((f32[60,8,128]{2,1,0:T(8,128)}, f32[60,8,128]{2,1,0:T(8,128)S(1)}, u32[]{:S(2)}) %copy-start.2) | copy-done | bytes 245784
  42.2 0.1 copy-done.3
  42.3 4.4 %shard_map.107 = (f32[152,32,128]{2,1,0:T(8,128)}, f32[152,32,128]{2,1,0:T(8,128)}) custom-call(s32[32]{0:T(128)} %wall_ref.1, f32[60,8,128]{2,1,0:T(8,128)} %copy-done.2, f32[60,8,128]{2,1,0:T(8,128)} %copy-done.3, f32[60,8,128]{2,1,0:T(8,128)} %get-tuple-element.45.zl_ref, ...), custom_call_target="tpu_custom_call", output_to_operand_aliasing={{0}: (11, {}), {1}: (12, {})} | custom-call | tf_op jit(solution)/shard_map/pallas_call | solution.py:364
  46.8 0.1 multiply_reduce_fusion.1
  46.9 1.2 %select_dynamic-update-slice_fusion = f32[152,32,128]{2,1,0:T(8,128)} fusion(f32[152,32,128]{2,1,0:T(8,128)} %get-tuple-element.60, f32[32,32,128]{2,1,0:T(8,128)S(1)} %copy-done.1, f32[32,128]{1,0:T(8,128)S(1)} %get-tuple-element.67, f32[32,32]{1,0:T(8,128)S(1)} %scatter.9, f32[32,32]{1,0:T(8,128)S(1)} %scatter.6, f32[32]{0:T(128)S(1)} %copy-done.7, ...), kind=kLoop, calls=%fused_computation | loop fusion | flops 786432 | bytes 1089696 | tf_op jit(solution)/shard_map/dynamic_update_slice | solution.py:383
  (32 shorter events, 0.4 us)
Async XLA Ops:
  0.6 13.6 %copy-start.6 = (f32[2,152]{1,0:T(2,128)S(1)}, f32[2,152]{1,0:T(2,128)}, u32[]{:S(2)}) copy-start(f32[2,152]{1,0:T(2,128)} %param.17) | copy-start | bytes 3652
  0.6 13.7 %copy-start = (f32[32,31,31]{2,0,1:T(8,128)S(1)}, f32[32,31,31]{2,0,1:T(8,128)}, u32[]{:S(2)}) copy-start(f32[32,31,31]{2,0,1:T(8,128)} %param.21) | copy-start | bytes 369028
  5.6 21.4 %collective-permute-start.2 = (f32[15,8,128]{2,1,0:T(8,128)}, f32[15,8,128]{2,1,0:T(8,128)S(1)}, u32[]{:S(2)}, u32[]{:S(2)}) collective-permute-start(f32[15,8,128]{2,1,0:T(8,128)} %get-tuple-element.47.refs_12_), channel_id=1, source_target_pairs={{0,8},{8,16},{16,24},{1,9},{9,17},{17,25},{2,10},{10,18},{18,26},{... | collective-permute-start | bytes 184328 | tf_op jit(solution)/shard_map/ppermute | solution.py:297
  8.7 18.3 %collective-permute-start.3 = (f32[15,8,128]{2,1,0:T(8,128)}, f32[15,8,128]{2,1,0:T(8,128)S(1)}, u32[]{:S(2)}, u32[]{:S(2)}) collective-permute-start(f32[15,8,128]{2,1,0:T(8,128)} %get-tuple-element.48.refs_11_), channel_id=1, source_target_pairs={{8,0},{16,8},{24,16},{9,1},{17,9},{25,17},{10,2},{18,10},{26,18},{... | collective-permute-start | bytes 184328 | tf_op jit(solution)/shard_map/ppermute | solution.py:298
  11.8 29.7 %collective-permute-start = (f32[60,8,128]{2,1,0:T(8,128)}, f32[60,8,128]{2,1,0:T(8,128)S(1)}, u32[]{:S(2)}, u32[]{:S(2)}) collective-permute-start(f32[60,8,128]{2,1,0:T(8,128)} %get-tuple-element.45.zl_ref), channel_id=1, source_target_pairs={{0,1},{1,2},{2,3},{3,4},{4,5},{5,6},{6,7},{7,0},{8,9},{9,10},{10,1... | collective-permute-start | bytes 737288 | tf_op jit(solution)/shard_map/ppermute | solution.py:299
  14.3 27.3 %collective-permute-start.1 = (f32[60,8,128]{2,1,0:T(8,128)}, f32[60,8,128]{2,1,0:T(8,128)S(1)}, u32[]{:S(2)}, u32[]{:S(2)}) collective-permute-start(f32[60,8,128]{2,1,0:T(8,128)} %get-tuple-element.46.refs_8_.zr_ref), channel_id=1, source_target_pairs={{1,0},{2,1},{3,2},{4,3},{5,4},{6,5},{7,6},{0,7},{9,8},{10,9},{11,1... | collective-permute-start | bytes 737288 | tf_op jit(solution)/shard_map/ppermute | solution.py:300
  19.4 6.4 %copy-start.7 = (f32[32]{0:T(128)S(1)}, f32[32]{0:T(128)}, u32[]{:S(2)}) copy-start(f32[32]{0:T(128)} %param.20) | copy-start | bytes 388
  19.4 27.3 %all-to-all-start = ((f32[8,3,32,128]{3,2,1,0:T(8,128)}), f32[8,3,32,128]{3,2,1,0:T(8,128)S(1)}, u32[]{:S(2)}, u32[]{:S(2)}) async-start(f32[8,3,32,128]{3,2,1,0:T(8,128)} %get-tuple-element.61), calls=%async_computation | async-start | bytes 786432 | tf_op jit(solution)/shard_map/all_to_all | solution.py:324
  27.0 0.6 %copy-start.4 = (f32[15,8,128]{2,1,0:T(8,128)}, f32[15,8,128]{2,1,0:T(8,128)S(1)}, u32[]{:S(2)}) copy-start(f32[15,8,128]{2,1,0:T(8,128)S(1)} %collective-permute-done.2.refs_9_) | copy-start | bytes 184324
  27.0 0.6 %copy-start.5 = (f32[15,8,128]{2,1,0:T(8,128)}, f32[15,8,128]{2,1,0:T(8,128)S(1)}, u32[]{:S(2)}) copy-start(f32[15,8,128]{2,1,0:T(8,128)S(1)} %collective-permute-done.3.refs_10_) | copy-start | bytes 184324
  41.5 0.7 %copy-start.2 = (f32[60,8,128]{2,1,0:T(8,128)}, f32[60,8,128]{2,1,0:T(8,128)S(1)}, u32[]{:S(2)}) copy-start(f32[60,8,128]{2,1,0:T(8,128)S(1)} %collective-permute-done.zb_ref) | copy-start | bytes 737284
  41.5 0.8 %copy-start.3 = (f32[60,8,128]{2,1,0:T(8,128)}, f32[60,8,128]{2,1,0:T(8,128)S(1)}, u32[]{:S(2)}) copy-start(f32[60,8,128]{2,1,0:T(8,128)S(1)} %collective-permute-done.1.za_ref) | copy-start | bytes 737284
  42.3 4.6 %copy-start.1 = (f32[32,32,128]{2,1,0:T(8,128)S(1)}, f32[32,32,128]{2,1,0:T(8,128)}, u32[]{:S(2)}) copy-start(f32[32,32,128]{2,1,0:T(8,128)} %get-tuple-element.62) | copy-start | bytes 1572868

commit v13 on v11

--- a/solution.py
+++ b/solution.py
@@ -232,7 +232,7 @@
                 tn_buf[f] = tn_buf[f] + section_weight * fix
             return carry
 
-        lax.fori_loop(0, nf // 2, pair, 0, unroll=10)
+        lax.fori_loop(0, nf // 2, pair, 0, unroll=20)
 
     targets = [
         (top_sn, sn_out.at[pl.ds(ns, nf), pl.ds(0, 8), :], sems.at[4]),

time: 48.8 us -> 48.8 us (level)
  no operation moved by 1% of the time
where the time goes in v13:
time: 48.8 us; the launch traced here: 48.1 us
  Pallas kernels  26.4 us (54%)
  starting transfers between devices  14.5 us (30%)
  local copies, waits for them, and re-layouts  3.7 us (8%)
  other arithmetic  2.62 us (5%)
  between operations  0.85 us (2%)
    pallas_call x1, Pallas kernels, local(): pl.pallas_call(lambda *refs: layer_kernel(True, nsb, LB, *refs), grid=(nf...  13.8 us
    all_to_all x1, starting transfers between devices, local(): blocks = lax.all_to_all(spread, 'gz', 0, 0, tiled=True)  5.85 us
    pallas_call x1, Pallas kernels, local(): pl.pallas_call(pack_kernel, grid=(1,), in_specs=[pl.BlockSpec((ny, cz, w)...  4.95 us
    pallas_call x1, Pallas kernels, local(): pl.pallas_call(span_fix_kernel, grid=(1,), in_specs=[smem] + [whole((nf /...  4.48 us
    unnamed x19, local copies, waits for them, and re-layouts  3.26 us
    pallas_call x1, Pallas kernels, local(): pl.pallas_call(lambda *refs: layer_kernel(False, 0, sb, *refs), grid=(ns...  3.21 us
    ppermute x1, starting transfers between devices, local(): xb = lax.ppermute(xr, 'gx', [(i, i + 1) for i in range(ngx - 1)])  3.11 us
    ppermute x1, starting transfers between devices, local(): xa = lax.ppermute(xl, 'gx', [(i + 1, i) for i in range(ngx - 1)])  3.06 us
  transfers between devices with their start and end apart: 5, of which 0 were waited for; matrix products, arithmetic and copies ran while one was open for 7% of the time, Pallas kernels for 45%

profile of v13, /device:TPU:5, one launch (start us, length us, event | category | flops | bytes accessed | tf_op | source)
XLA Modules:
  0.0 48.1 jit_solution(14824176924916942236)
XLA Ops:
  0.6 4.9 %shard_map.104 = (f32[15,8,128]{2,1,0:T(8,128)}, f32[15,8,128]{2,1,0:T(8,128)}, f32[15,8,128]{2,1,0:T(8,128)}, f32[15,8,128]{2,1,0:T(8,128)}, f32[60,8,128]{2,1,0:T(8,128)}, /*index=5*/f32[60,8,128]{2,1,0:T(8,128)}) custom-call(f32[152,32,128]{2,1,0:T(8,128)} %refs_5_.3, bf16[152,32,128]{2,1,0:T(8,128)(2,1)} %refs_7_.2), custom_call_target="tpu_custom_call" | custom-call | tf_op jit(solution)/shard_map/pallas_call | solution.py:286
  5.6 3.1 %collective-permute-start.2 = (f32[15,8,128]{2,1,0:T(8,128)}, f32[15,8,128]{2,1,0:T(8,128)S(1)}, u32[]{:S(2)}, u32[]{:S(2)}) collective-permute-start(f32[15,8,128]{2,1,0:T(8,128)} %get-tuple-element.45.refs_12_), channel_id=1, source_target_pairs={{0,8},{8,16},{16,24},{1,9},{9,17},{17,25},{2,10},{10,18},{18,26},{... | collective-permute-start | bytes 184328 | tf_op jit(solution)/shard_map/ppermute | solution.py:296
  8.7 3.1 %collective-permute-start.3 = (f32[15,8,128]{2,1,0:T(8,128)}, f32[15,8,128]{2,1,0:T(8,128)S(1)}, u32[]{:S(2)}, u32[]{:S(2)}) collective-permute-start(f32[15,8,128]{2,1,0:T(8,128)} %get-tuple-element.46.refs_11_), channel_id=1, source_target_pairs={{8,0},{16,8},{24,16},{9,1},{17,9},{25,17},{10,2},{18,10},{26,18},{... | collective-permute-start | bytes 184328 | tf_op jit(solution)/shard_map/ppermute | solution.py:297
  11.8 2.5 %collective-permute-start = (f32[60,8,128]{2,1,0:T(8,128)}, f32[60,8,128]{2,1,0:T(8,128)S(1)}, u32[]{:S(2)}, u32[]{:S(2)}) collective-permute-start(f32[60,8,128]{2,1,0:T(8,128)} %get-tuple-element.43.zl_ref), channel_id=1, source_target_pairs={{0,1},{1,2},{2,3},{3,4},{4,5},{5,6},{6,7},{7,0},{8,9},{9,10},{10,1... | collective-permute-start | bytes 737288 | tf_op jit(solution)/shard_map/ppermute | solution.py:298
  14.3 1.1 %copy.24.refs_7_ = f32[32,31,31]{2,1,0:T(8,128)} copy(f32[32,31,31]{2,0,1:T(8,128)S(1)} %copy-done) | data formatting | bytes 246016 | tf_op args[8]
  15.4 0.1 pad_maximum_fusion.3
  15.5 0.1 pad_maximum_fusion.1
  15.6 0.6 %pad_maximum_fusion.refs_0_ = f32[3,153]{1,0:T(4,128)} fusion(f32[1,153]{1,0:T(1,128)S(1)} %bitcast.36, f32[1,153]{1,0:T(1,128)S(1)} %bitcast.37, f32[1,153]{1,0:T(1,128)S(1)} %bitcast.35), kind=kLoop, calls=%fused_computation.29 | loop fusion | flops 918 | bytes 3672 | tf_op jit(solution)/shard_map/stack | solution.py:273
  16.2 3.2 %shard_map.105 = (f32[152,32,128]{2,1,0:T(8,128)}, f32[32,32,128]{2,1,0:T(8,128)}, f32[8,3,32,128]{3,2,1,0:T(8,128)}) custom-call(f32[3,153]{1,0:T(4,128)} %pad_maximum_fusion.refs_0_, s32[32]{0:T(128)} %wall_ref.1, s32[128]{0:T(128)} %refs_2_.3, f32[152,32,128]{2,1,0:T(8,128)} %refs_5_.3, f32[152,32,128]{2,1,0:T(8,128)} %refs_5_.3, ...), custom_call_target="tpu_custom_call" | custom-call | tf_op jit(solution)/shard_map/pallas_call | solution.py:304
  19.4 5.9 %all-to-all-start = ((f32[8,3,32,128]{3,2,1,0:T(8,128)}), f32[8,3,32,128]{3,2,1,0:T(8,128)S(1)}, u32[]{:S(2)}, u32[]{:S(2)}) async-start(f32[8,3,32,128]{3,2,1,0:T(8,128)} %get-tuple-element.57), calls=%async_computation | async-start | bytes 786432 | tf_op jit(solution)/shard_map/all_to_all | solution.py:323
  25.3 0.2 add_reduce_fusion
  25.4 0.2 fusion.19
  25.9 0.4 copy.31
  26.2 0.4 copy.32
  26.7 0.1 scatter.6
  26.7 0.1 scatter.9
  26.9 0.1 divide_reduce_fusion.1
  27.0 0.6 %copy-done.4 = f32[15,8,128]{2,1,0:T(8,128)} copy-done((f32[15,8,128]{2,1,0:T(8,128)}, f32[15,8,128]{2,1,0:T(8,128)S(1)}, u32[]{:S(2)}) %copy-start.4) | copy-done | bytes 61464
  27.6 13.8 %shard_map.106 = (f32[152,32,128]{2,1,0:T(8,128)}, f32[152,32,128]{2,1,0:T(8,128)}, f32[120,8,128]{2,1,0:T(8,128)}, f32[120,8,128]{2,1,0:T(8,128)}, f32[120,8,128]{2,1,0:T(8,128)}, /*index=5*/f32[120,8,128]{2,1,0:T(8,128)}) custom-call(f32[3,153]{1,0:T(4,128)} %pad_maximum_fusion.refs_0_, s32[32]{0:T(128)} %wall_ref.1, ...), custom_call_target="tpu_custom_call", output_to_operand_aliasing={{0}: (15, {})} | custom-call | tf_op jit(solution)/shard_map/pallas_call | solution.py:343
  41.5 0.7 %copy-done.2 = f32[60,8,128]{2,1,0:T(8,128)} copy-done((f32[60,8,128]{2,1,0:T(8,128)}, f32[60,8,128]{2,1,0:T(8,128)S(1)}, u32[]{:S(2)}) %copy-start.2) | copy-done | bytes 245784
  42.1 0.1 copy-done.3
  42.2 4.5 %shard_map.107 = (f32[152,32,128]{2,1,0:T(8,128)}, f32[152,32,128]{2,1,0:T(8,128)}) custom-call(s32[32]{0:T(128)} %wall_ref.1, f32[60,8,128]{2,1,0:T(8,128)} %copy-done.2, f32[60,8,128]{2,1,0:T(8,128)} %copy-done.3, f32[60,8,128]{2,1,0:T(8,128)} %get-tuple-element.43.zl_ref, ...), custom_call_target="tpu_custom_call", output_to_operand_aliasing={{0}: (10, {}), {1}: (11, {})} | custom-call | tf_op jit(solution)/shard_map/pallas_call | solution.py:363
  46.8 0.1 multiply_reduce_fusion.1
  46.9 1.2 %select_dynamic-update-slice_fusion = f32[152,32,128]{2,1,0:T(8,128)} fusion(f32[152,32,128]{2,1,0:T(8,128)} %get-tuple-element.56, f32[32,32,128]{2,1,0:T(8,128)S(1)} %copy-done.1, f32[32,128]{1,0:T(8,128)S(1)} %get-tuple-element.63, f32[32,32]{1,0:T(8,128)S(1)} %scatter.9, f32[32,32]{1,0:T(8,128)S(1)} %scatter.6, f32[32]{0:T(128)S(1)} %copy-done.7, ...), kind=kLoop, calls=%fused_computation | loop fusion | flops 786432 | bytes 1089696 | tf_op jit(solution)/shard_map/dynamic_update_slice | solution.py:382
  (32 shorter events, 0.4 us)
Async XLA Ops:
  0.6 13.6 %copy-start.6 = (f32[2,152]{1,0:T(2,128)S(1)}, f32[2,152]{1,0:T(2,128)}, u32[]{:S(2)}) copy-start(f32[2,152]{1,0:T(2,128)} %param.17) | copy-start | bytes 3652
  0.6 13.7 %copy-start = (f32[32,31,31]{2,0,1:T(8,128)S(1)}, f32[32,31,31]{2,0,1:T(8,128)}, u32[]{:S(2)}) copy-start(f32[32,31,31]{2,0,1:T(8,128)} %param.21) | copy-start | bytes 369028
  5.6 21.4 %collective-permute-start.2 = (f32[15,8,128]{2,1,0:T(8,128)}, f32[15,8,128]{2,1,0:T(8,128)S(1)}, u32[]{:S(2)}, u32[]{:S(2)}) collective-permute-start(f32[15,8,128]{2,1,0:T(8,128)} %get-tuple-element.45.refs_12_), channel_id=1, source_target_pairs={{0,8},{8,16},{16,24},{1,9},{9,17},{17,25},{2,10},{10,18},{18,26},{... | collective-permute-start | bytes 184328 | tf_op jit(solution)/shard_map/ppermute | solution.py:296
  8.7 18.3 %collective-permute-start.3 = (f32[15,8,128]{2,1,0:T(8,128)}, f32[15,8,128]{2,1,0:T(8,128)S(1)}, u32[]{:S(2)}, u32[]{:S(2)}) collective-permute-start(f32[15,8,128]{2,1,0:T(8,128)} %get-tuple-element.46.refs_11_), channel_id=1, source_target_pairs={{8,0},{16,8},{24,16},{9,1},{17,9},{25,17},{10,2},{18,10},{26,18},{... | collective-permute-start | bytes 184328 | tf_op jit(solution)/shard_map/ppermute | solution.py:297
  11.8 29.7 %collective-permute-start = (f32[60,8,128]{2,1,0:T(8,128)}, f32[60,8,128]{2,1,0:T(8,128)S(1)}, u32[]{:S(2)}, u32[]{:S(2)}) collective-permute-start(f32[60,8,128]{2,1,0:T(8,128)} %get-tuple-element.43.zl_ref), channel_id=1, source_target_pairs={{0,1},{1,2},{2,3},{3,4},{4,5},{5,6},{6,7},{7,0},{8,9},{9,10},{10,1... | collective-permute-start | bytes 737288 | tf_op jit(solution)/shard_map/ppermute | solution.py:298
  14.2 27.2 %collective-permute-start.1 = (f32[60,8,128]{2,1,0:T(8,128)}, f32[60,8,128]{2,1,0:T(8,128)S(1)}, u32[]{:S(2)}, u32[]{:S(2)}) collective-permute-start(f32[60,8,128]{2,1,0:T(8,128)} %get-tuple-element.44.refs_8_.zr_ref), channel_id=1, source_target_pairs={{1,0},{2,1},{3,2},{4,3},{5,4},{6,5},{7,6},{0,7},{9,8},{10,9},{11,1... | collective-permute-start | bytes 737288 | tf_op jit(solution)/shard_map/ppermute | solution.py:299
  19.4 6.4 %copy-start.7 = (f32[32]{0:T(128)S(1)}, f32[32]{0:T(128)}, u32[]{:S(2)}) copy-start(f32[32]{0:T(128)} %param.20) | copy-start | bytes 388
  19.4 27.3 %all-to-all-start = ((f32[8,3,32,128]{3,2,1,0:T(8,128)}), f32[8,3,32,128]{3,2,1,0:T(8,128)S(1)}, u32[]{:S(2)}, u32[]{:S(2)}) async-start(f32[8,3,32,128]{3,2,1,0:T(8,128)} %get-tuple-element.57), calls=%async_computation | async-start | bytes 786432 | tf_op jit(solution)/shard_map/all_to_all | solution.py:323
  27.0 0.6 %copy-start.4 = (f32[15,8,128]{2,1,0:T(8,128)}, f32[15,8,128]{2,1,0:T(8,128)S(1)}, u32[]{:S(2)}) copy-start(f32[15,8,128]{2,1,0:T(8,128)S(1)} %collective-permute-done.2.refs_9_) | copy-start | bytes 184324
  27.0 0.6 %copy-start.5 = (f32[15,8,128]{2,1,0:T(8,128)}, f32[15,8,128]{2,1,0:T(8,128)S(1)}, u32[]{:S(2)}) copy-start(f32[15,8,128]{2,1,0:T(8,128)S(1)} %collective-permute-done.3.refs_10_) | copy-start | bytes 184324
  41.5 0.7 %copy-start.2 = (f32[60,8,128]{2,1,0:T(8,128)}, f32[60,8,128]{2,1,0:T(8,128)S(1)}, u32[]{:S(2)}) copy-start(f32[60,8,128]{2,1,0:T(8,128)S(1)} %collective-permute-done.zb_ref) | copy-start | bytes 737284
  41.5 0.7 %copy-start.3 = (f32[60,8,128]{2,1,0:T(8,128)}, f32[60,8,128]{2,1,0:T(8,128)S(1)}, u32[]{:S(2)}) copy-start(f32[60,8,128]{2,1,0:T(8,128)S(1)} %collective-permute-done.1.za_ref) | copy-start | bytes 737284
  42.2 4.7 %copy-start.1 = (f32[32,32,128]{2,1,0:T(8,128)S(1)}, f32[32,32,128]{2,1,0:T(8,128)}, u32[]{:S(2)}) copy-start(f32[32,32,128]{2,1,0:T(8,128)} %get-tuple-element.58) | copy-start | bytes 1572868

commit v14 on v13

--- a/solution.py
+++ b/solution.py
@@ -232,7 +232,7 @@
                 tn_buf[f] = tn_buf[f] + section_weight * fix
             return carry
 
-        lax.fori_loop(0, nf // 2, pair, 0, unroll=20)
+        lax.fori_loop(0, nf // 2, pair, 0, unroll=30)
 
     targets = [
         (top_sn, sn_out.at[pl.ds(ns, nf), pl.ds(0, 8), :], sems.at[4]),

time: 48.8 us -> 48.8 us (level)
  no operation moved by 1% of the time
where the time goes in v14:
time: 48.8 us; the launch traced here: 48.1 us
  Pallas kernels  26.4 us (54%)
  starting transfers between devices  14.5 us (30%)
  local copies, waits for them, and re-layouts  3.7 us (8%)
  other arithmetic  2.62 us (5%)
  between operations  0.85 us (2%)
    pallas_call x1, Pallas kernels, local(): pl.pallas_call(lambda *refs: layer_kernel(True, nsb, LB, *refs), grid=(nf...  13.8 us
    all_to_all x1, starting transfers between devices, local(): blocks = lax.all_to_all(spread, 'gz', 0, 0, tiled=True)  5.85 us
    pallas_call x1, Pallas kernels, local(): pl.pallas_call(pack_kernel, grid=(1,), in_specs=[pl.BlockSpec((ny, cz, w)...  4.95 us
    pallas_call x1, Pallas kernels, local(): pl.pallas_call(span_fix_kernel, grid=(1,), in_specs=[smem] + [whole((nf /...  4.46 us
    unnamed x19, local copies, waits for them, and re-layouts  3.26 us
    pallas_call x1, Pallas kernels, local(): pl.pallas_call(lambda *refs: layer_kernel(False, 0, sb, *refs), grid=(ns...  3.21 us
    ppermute x1, starting transfers between devices, local(): xb = lax.ppermute(xr, 'gx', [(i, i + 1) for i in range(ngx - 1)])  3.11 us
    ppermute x1, starting transfers between devices, local(): xa = lax.ppermute(xl, 'gx', [(i + 1, i) for i in range(ngx - 1)])  3.06 us
  transfers between devices with their start and end apart: 5, of which 0 were waited for; matrix products, arithmetic and copies ran while one was open for 7% of the time, Pallas kernels for 45%

profile of v14, /device:TPU:5, one launch (start us, length us, event | category | flops | bytes accessed | tf_op | source)
XLA Modules:
  0.0 48.1 jit_solution(14984679642011380279)
XLA Ops:
  0.6 4.9 %shard_map.104 = (f32[15,8,128]{2,1,0:T(8,128)}, f32[15,8,128]{2,1,0:T(8,128)}, f32[15,8,128]{2,1,0:T(8,128)}, f32[15,8,128]{2,1,0:T(8,128)}, f32[60,8,128]{2,1,0:T(8,128)}, /*index=5*/f32[60,8,128]{2,1,0:T(8,128)}) custom-call(f32[152,32,128]{2,1,0:T(8,128)} %refs_5_.3, bf16[152,32,128]{2,1,0:T(8,128)(2,1)} %refs_7_.2), custom_call_target="tpu_custom_call" | custom-call | tf_op jit(solution)/shard_map/pallas_call | solution.py:286
  5.6 3.1 %collective-permute-start.2 = (f32[15,8,128]{2,1,0:T(8,128)}, f32[15,8,128]{2,1,0:T(8,128)S(1)}, u32[]{:S(2)}, u32[]{:S(2)}) collective-permute-start(f32[15,8,128]{2,1,0:T(8,128)} %get-tuple-element.45.refs_12_), channel_id=1, source_target_pairs={{0,8},{8,16},{16,24},{1,9},{9,17},{17,25},{2,10},{10,18},{18,26},{... | collective-permute-start | bytes 184328 | tf_op jit(solution)/shard_map/ppermute | solution.py:296
  8.7 3.1 %collective-permute-start.3 = (f32[15,8,128]{2,1,0:T(8,128)}, f32[15,8,128]{2,1,0:T(8,128)S(1)}, u32[]{:S(2)}, u32[]{:S(2)}) collective-permute-start(f32[15,8,128]{2,1,0:T(8,128)} %get-tuple-element.46.refs_11_), channel_id=1, source_target_pairs={{8,0},{16,8},{24,16},{9,1},{17,9},{25,17},{10,2},{18,10},{26,18},{... | collective-permute-start | bytes 184328 | tf_op jit(solution)/shard_map/ppermute | solution.py:297
  11.8 2.5 %collective-permute-start = (f32[60,8,128]{2,1,0:T(8,128)}, f32[60,8,128]{2,1,0:T(8,128)S(1)}, u32[]{:S(2)}, u32[]{:S(2)}) collective-permute-start(f32[60,8,128]{2,1,0:T(8,128)} %get-tuple-element.43.zl_ref), channel_id=1, source_target_pairs={{0,1},{1,2},{2,3},{3,4},{4,5},{5,6},{6,7},{7,0},{8,9},{9,10},{10,1... | collective-permute-start | bytes 737288 | tf_op jit(solution)/shard_map/ppermute | solution.py:298
  14.3 1.1 %copy.24.refs_7_ = f32[32,31,31]{2,1,0:T(8,128)} copy(f32[32,31,31]{2,0,1:T(8,128)S(1)} %copy-done) | data formatting | bytes 246016 | tf_op args[8]
  15.4 0.1 pad_maximum_fusion.3
  15.5 0.1 pad_maximum_fusion.1
  15.6 0.6 %pad_maximum_fusion.refs_0_ = f32[3,153]{1,0:T(4,128)} fusion(f32[1,153]{1,0:T(1,128)S(1)} %bitcast.36, f32[1,153]{1,0:T(1,128)S(1)} %bitcast.37, f32[1,153]{1,0:T(1,128)S(1)} %bitcast.35), kind=kLoop, calls=%fused_computation.29 | loop fusion | flops 918 | bytes 3672 | tf_op jit(solution)/shard_map/stack | solution.py:273
  16.2 3.2 %shard_map.105 = (f32[152,32,128]{2,1,0:T(8,128)}, f32[32,32,128]{2,1,0:T(8,128)}, f32[8,3,32,128]{3,2,1,0:T(8,128)}) custom-call(f32[3,153]{1,0:T(4,128)} %pad_maximum_fusion.refs_0_, s32[32]{0:T(128)} %wall_ref.1, s32[128]{0:T(128)} %refs_2_.3, f32[152,32,128]{2,1,0:T(8,128)} %refs_5_.3, f32[152,32,128]{2,1,0:T(8,128)} %refs_5_.3, ...), custom_call_target="tpu_custom_call" | custom-call | tf_op jit(solution)/shard_map/pallas_call | solution.py:304
  19.4 5.9 %all-to-all-start = ((f32[8,3,32,128]{3,2,1,0:T(8,128)}), f32[8,3,32,128]{3,2,1,0:T(8,128)S(1)}, u32[]{:S(2)}, u32[]{:S(2)}) async-start(f32[8,3,32,128]{3,2,1,0:T(8,128)} %get-tuple-element.57), calls=%async_computation | async-start | bytes 786432 | tf_op jit(solution)/shard_map/all_to_all | solution.py:323
  25.3 0.2 add_reduce_fusion
  25.4 0.2 fusion.19
  25.9 0.4 copy.31
  26.2 0.4 copy.32
  26.7 0.1 scatter.6
  26.7 0.1 scatter.9
  26.9 0.1 divide_reduce_fusion.1
  27.0 0.6 %copy-done.4 = f32[15,8,128]{2,1,0:T(8,128)} copy-done((f32[15,8,128]{2,1,0:T(8,128)}, f32[15,8,128]{2,1,0:T(8,128)S(1)}, u32[]{:S(2)}) %copy-start.4) | copy-done | bytes 61464
  27.6 13.8 %shard_map.106 = (f32[152,32,128]{2,1,0:T(8,128)}, f32[152,32,128]{2,1,0:T(8,128)}, f32[120,8,128]{2,1,0:T(8,128)}, f32[120,8,128]{2,1,0:T(8,128)}, f32[120,8,128]{2,1,0:T(8,128)}, /*index=5*/f32[120,8,128]{2,1,0:T(8,128)}) custom-call(f32[3,153]{1,0:T(4,128)} %pad_maximum_fusion.refs_0_, s32[32]{0:T(128)} %wall_ref.1, ...), custom_call_target="tpu_custom_call", output_to_operand_aliasing={{0}: (15, {})} | custom-call | tf_op jit(solution)/shard_map/pallas_call | solution.py:343
  41.5 0.7 %copy-done.2 = f32[60,8,128]{2,1,0:T(8,128)} copy-done((f32[60,8,128]{2,1,0:T(8,128)}, f32[60,8,128]{2,1,0:T(8,128)S(1)}, u32[]{:S(2)}) %copy-start.2) | copy-done | bytes 245784
  42.1 0.1 copy-done.3
  42.2 4.5 %shard_map.107 = (f32[152,32,128]{2,1,0:T(8,128)}, f32[152,32,128]{2,1,0:T(8,128)}) custom-call(s32[32]{0:T(128)} %wall_ref.1, f32[60,8,128]{2,1,0:T(8,128)} %copy-done.2, f32[60,8,128]{2,1,0:T(8,128)} %copy-done.3, f32[60,8,128]{2,1,0:T(8,128)} %get-tuple-element.43.zl_ref, ...), custom_call_target="tpu_custom_call", output_to_operand_aliasing={{0}: (10, {}), {1}: (11, {})} | custom-call | tf_op jit(solution)/shard_map/pallas_call | solution.py:363
  46.7 0.1 multiply_reduce_fusion.1
  46.9 1.2 %select_dynamic-update-slice_fusion = f32[152,32,128]{2,1,0:T(8,128)} fusion(f32[152,32,128]{2,1,0:T(8,128)} %get-tuple-element.56, f32[32,32,128]{2,1,0:T(8,128)S(1)} %copy-done.1, f32[32,128]{1,0:T(8,128)S(1)} %get-tuple-element.63, f32[32,32]{1,0:T(8,128)S(1)} %scatter.9, f32[32,32]{1,0:T(8,128)S(1)} %scatter.6, f32[32]{0:T(128)S(1)} %copy-done.7, ...), kind=kLoop, calls=%fused_computation | loop fusion | flops 786432 | bytes 1089696 | tf_op jit(solution)/shard_map/dynamic_update_slice | solution.py:382
  (32 shorter events, 0.4 us)
Async XLA Ops:
  0.6 13.6 %copy-start.6 = (f32[2,152]{1,0:T(2,128)S(1)}, f32[2,152]{1,0:T(2,128)}, u32[]{:S(2)}) copy-start(f32[2,152]{1,0:T(2,128)} %param.17) | copy-start | bytes 3652
  0.6 13.7 %copy-start = (f32[32,31,31]{2,0,1:T(8,128)S(1)}, f32[32,31,31]{2,0,1:T(8,128)}, u32[]{:S(2)}) copy-start(f32[32,31,31]{2,0,1:T(8,128)} %param.21) | copy-start | bytes 369028
  5.6 21.4 %collective-permute-start.2 = (f32[15,8,128]{2,1,0:T(8,128)}, f32[15,8,128]{2,1,0:T(8,128)S(1)}, u32[]{:S(2)}, u32[]{:S(2)}) collective-permute-start(f32[15,8,128]{2,1,0:T(8,128)} %get-tuple-element.45.refs_12_), channel_id=1, source_target_pairs={{0,8},{8,16},{16,24},{1,9},{9,17},{17,25},{2,10},{10,18},{18,26},{... | collective-permute-start | bytes 184328 | tf_op jit(solution)/shard_map/ppermute | solution.py:296
  8.7 18.3 %collective-permute-start.3 = (f32[15,8,128]{2,1,0:T(8,128)}, f32[15,8,128]{2,1,0:T(8,128)S(1)}, u32[]{:S(2)}, u32[]{:S(2)}) collective-permute-start(f32[15,8,128]{2,1,0:T(8,128)} %get-tuple-element.46.refs_11_), channel_id=1, source_target_pairs={{8,0},{16,8},{24,16},{9,1},{17,9},{25,17},{10,2},{18,10},{26,18},{... | collective-permute-start | bytes 184328 | tf_op jit(solution)/shard_map/ppermute | solution.py:297
  11.8 29.7 %collective-permute-start = (f32[60,8,128]{2,1,0:T(8,128)}, f32[60,8,128]{2,1,0:T(8,128)S(1)}, u32[]{:S(2)}, u32[]{:S(2)}) collective-permute-start(f32[60,8,128]{2,1,0:T(8,128)} %get-tuple-element.43.zl_ref), channel_id=1, source_target_pairs={{0,1},{1,2},{2,3},{3,4},{4,5},{5,6},{6,7},{7,0},{8,9},{9,10},{10,1... | collective-permute-start | bytes 737288 | tf_op jit(solution)/shard_map/ppermute | solution.py:298
  14.2 27.2 %collective-permute-start.1 = (f32[60,8,128]{2,1,0:T(8,128)}, f32[60,8,128]{2,1,0:T(8,128)S(1)}, u32[]{:S(2)}, u32[]{:S(2)}) collective-permute-start(f32[60,8,128]{2,1,0:T(8,128)} %get-tuple-element.44.refs_8_.zr_ref), channel_id=1, source_target_pairs={{1,0},{2,1},{3,2},{4,3},{5,4},{6,5},{7,6},{0,7},{9,8},{10,9},{11,1... | collective-permute-start | bytes 737288 | tf_op jit(solution)/shard_map/ppermute | solution.py:299
  19.4 6.4 %copy-start.7 = (f32[32]{0:T(128)S(1)}, f32[32]{0:T(128)}, u32[]{:S(2)}) copy-start(f32[32]{0:T(128)} %param.20) | copy-start | bytes 388
  19.4 27.3 %all-to-all-start = ((f32[8,3,32,128]{3,2,1,0:T(8,128)}), f32[8,3,32,128]{3,2,1,0:T(8,128)S(1)}, u32[]{:S(2)}, u32[]{:S(2)}) async-start(f32[8,3,32,128]{3,2,1,0:T(8,128)} %get-tuple-element.57), calls=%async_computation | async-start | bytes 786432 | tf_op jit(solution)/shard_map/all_to_all | solution.py:323
  27.0 0.6 %copy-start.4 = (f32[15,8,128]{2,1,0:T(8,128)}, f32[15,8,128]{2,1,0:T(8,128)S(1)}, u32[]{:S(2)}) copy-start(f32[15,8,128]{2,1,0:T(8,128)S(1)} %collective-permute-done.2.refs_9_) | copy-start | bytes 184324
  27.0 0.6 %copy-start.5 = (f32[15,8,128]{2,1,0:T(8,128)}, f32[15,8,128]{2,1,0:T(8,128)S(1)}, u32[]{:S(2)}) copy-start(f32[15,8,128]{2,1,0:T(8,128)S(1)} %collective-permute-done.3.refs_10_) | copy-start | bytes 184324
  41.5 0.7 %copy-start.2 = (f32[60,8,128]{2,1,0:T(8,128)}, f32[60,8,128]{2,1,0:T(8,128)S(1)}, u32[]{:S(2)}) copy-start(f32[60,8,128]{2,1,0:T(8,128)S(1)} %collective-permute-done.zb_ref) | copy-start | bytes 737284
  41.5 0.7 %copy-start.3 = (f32[60,8,128]{2,1,0:T(8,128)}, f32[60,8,128]{2,1,0:T(8,128)S(1)}, u32[]{:S(2)}) copy-start(f32[60,8,128]{2,1,0:T(8,128)S(1)} %collective-permute-done.1.za_ref) | copy-start | bytes 737284
  42.2 4.7 %copy-start.1 = (f32[32,32,128]{2,1,0:T(8,128)S(1)}, f32[32,32,128]{2,1,0:T(8,128)}, u32[]{:S(2)}) copy-start(f32[32,32,128]{2,1,0:T(8,128)} %get-tuple-element.58) | copy-start | bytes 1572868
